TPU v7x, 256 devices: a whole 4x4x8 slice. The times are simulated.
256 devices in a mesh: dp: 8 (over z_hi, x), seq: 32 (over y, z_lo, core).
Axes of the slice: x: 4, y: 4, z: 8 (z_hi: 2, z_lo: 4; z = z_hi * 4 + z_lo), core: 2. Of those that a mesh axis runs over, the one named last changes fastest.
Arguments:
- inputs: bfloat16 [8, 32768, 1024], P('dp', 'seq'), may hold values from -6 to 6
- cotangent: bfloat16 [8, 32768, 1024], P('dp', 'seq'), may hold values from -4 to 4
- factor_one: bfloat16 [32, 1024, 1024], P('seq'), may hold values from -0.1875 to 0.1875
- factor_two: bfloat16 [32, 1024, 1024], P('seq'), may hold values from -0.1875 to 0.1875
Outputs:
- mixed: bfloat16 [8, 32768, 1024], P('dp', 'seq')
- grad_input: bfloat16 [8, 32768, 1024], P('dp', 'seq')
- grad_one: float32 [32, 1024, 1024], P('seq', 'dp')
- grad_two: float32 [32, 1024, 1024], P('seq', 'dp')
All inputs are finite; a program needn't handle non-finite values.
Results may differ from a plain program's by a relative error of at most 0.014.
Values may be sent and summed in bfloat16 or wider, within the bound.
No kernel may reach another device: no remote copies, remote signals or barrier semaphores. Data moves between devices by JAX's collectives and lax.ppermute only.
A program may use at most 128 MiB of HBM per device.

v0:
```python
import jax
import jax.numpy as jnp
from jax import lax
from jax.sharding import PartitionSpec as P


def local(inputs, cotangent, factor_one, factor_two):
    seqs, block, width = inputs.shape
    count = lax.axis_size("seq")
    rows = block // count
    fone = factor_one[0]
    ftwo = factor_two[0]
    xfull = inputs.astype(jnp.float32)
    dyfull = cotangent.astype(jnp.float32)
    first = jnp.einsum("kj,sjc->skc", fone, inputs, preferred_element_type=jnp.float32).astype(
        jnp.bfloat16
    )
    gated = (dyfull * xfull).astype(jnp.bfloat16)
    moved = lax.all_to_all(
        first.reshape(seqs, count, rows, 1, width), "seq", split_axis=1, concat_axis=3, tiled=True
    )
    moved = moved.reshape(seqs, block, width)
    second = jnp.einsum("pq,sqc->spc", ftwo, moved, preferred_element_type=jnp.float32).astype(
        jnp.bfloat16
    )
    monarch = lax.all_to_all(
        second.reshape(seqs, 1, rows, count, width), "seq", split_axis=3, concat_axis=1, tiled=True
    )
    monarch = monarch.reshape(seqs, block, width)
    gated_moved = lax.all_to_all(
        gated.reshape(seqs, count, rows, 1, width), "seq", split_axis=1, concat_axis=3, tiled=True
    )
    gated_moved = gated_moved.reshape(seqs, block, width)
    back_two = jnp.einsum(
        "pq,spc->sqc", ftwo, gated_moved, preferred_element_type=jnp.float32
    ).astype(jnp.bfloat16)
    back_moved = lax.all_to_all(
        back_two.reshape(seqs, 1, rows, count, width),
        "seq",
        split_axis=3,
        concat_axis=1,
        tiled=True,
    )
    back_moved = back_moved.reshape(seqs, block, width)
    mfull = monarch.astype(jnp.float32)
    mixed = (xfull * mfull).astype(jnp.bfloat16)
    part_two = jnp.einsum("spc,sqc->pq", gated_moved, moved, preferred_element_type=jnp.float32)
    part_one = jnp.einsum("skc,sjc->kj", back_moved, inputs, preferred_element_type=jnp.float32)
    grad_one, grad_two = (
        lax.psum_scatter(
            part_one.astype(jnp.bfloat16), "dp", scatter_dimension=0, tiled=True
        ).astype(jnp.float32),
        lax.psum_scatter(
            part_two.astype(jnp.bfloat16), "dp", scatter_dimension=0, tiled=True
        ).astype(jnp.float32),
    )
    spread = jnp.einsum("kj,skc->sjc", fone, back_moved, preferred_element_type=jnp.float32)
    grad_input = (dyfull * mfull + spread).astype(jnp.bfloat16)
    return (mixed, grad_input, grad_one[None], grad_two[None])


def solution(mesh):
    in_specs = (
        P("dp", "seq", None),
        P("dp", "seq", None),
        P("seq", None, None),
        P("seq", None, None),
    )
    out_specs = (
        P("dp", "seq", None),
        P("dp", "seq", None),
        P("seq", "dp", None),
        P("seq", "dp", None),
    )
    return jax.shard_map(local, mesh=mesh, in_specs=in_specs, out_specs=out_specs, check_vma=False)
```

profile of v0, /device:TPU:8, one launch (start us, length us, event | category | flops | bytes accessed | tf_op | source)
XLA Modules:
  0.0 429.8 jit_solution(16111633440075535005)
XLA Ops:
  7.2 0.0 copy-start
  7.2 4.7 %fusion.17 = bf16[1024,1024]{0,1:T(8,128)(2,1)S(1)} fusion(bf16[1,1024,1024]{2,1,0:T(8,128)(2,1)} %param.4, bf16[1,1024,1024]{2,1,0:T(8,128)(2,1)} %param.6), kind=kOutput, calls=%fused_computation.19 | convolution fusion | flops 2148532224 | bytes 6291456 | tf_op jit(solution)/shard_map/kj,sjc->skc/dot_general | solution.py:15
  11.9 56.7 %all_to_all.54 = bf16[1,32,32,1,1024]{4,2,3,0,1:T(8,128)(2,1)S(1)} all-to-all(bf16[1,32,32,1,1024]{4,2,3,0,1:T(8,128)(2,1)S(1)} %bitcast.90), channel_id=1, replica_groups=mesh['dp'=8,'seq'=32] {'seq'}, dimensions={1} | all-to-all | bytes 4194304 | tf_op jit(solution)/shard_map/all_to_all | solution.py:19
  68.6 1.2 copy.26
  69.8 0.0 copy-start.1
  69.8 0.0 copy-done
  69.8 2.4 fusion.22
  72.1 0.0 copy-done.1
  72.2 2.5 copy.27
  74.6 7.2 %all-to-all-start.1 = ((bf16[1,1,32,32,1024]{4,2,1,0,3:T(8,128)(2,1)}), bf16[1,1,32,32,1024]{4,2,1,0,3:T(8,128)(2,1)}, u32[]{:S(2)}, u32[]{:S(2)}) async-start(bf16[1,1,32,32,1024]{4,2,1,0,3:T(8,128)(2,1)} %copy.27), calls=%async_computation.1 | async-start | bytes 4194304 | tf_op jit(solution)/shard_map/all_to_all | solution.py:26
  81.8 3.9 copy.24
  85.7 3.9 copy.30
  89.7 40.1 %all-to-all-done.1 = bf16[1,1,32,32,1024]{4,2,1,0,3:T(8,128)(2,1)} async-done(((bf16[1,1,32,32,1024]{4,2,1,0,3:T(8,128)(2,1)}), bf16[1,1,32,32,1024]{4,2,1,0,3:T(8,128)(2,1)}, u32[]{:S(2)}, u32[]{:S(2)}) %all-to-all-start.1) | async-done | bytes 2097184 | tf_op jit(solution)/shard_map/all_to_all | solution.py:26
  129.7 4.1 bitcast_convert_fusion
  133.8 5.3 %copy.29 = f32[1,1024,1024]{1,2,0:T(8,128)} copy(f32[1,1024,1024]{2,1,0:T(8,128)} %bitcast.84) | data formatting | bytes 8388608 | tf_op jit(solution)/shard_map/convert_element_type | solution.py:45
  139.1 6.9 %fusion.3 = (bf16[1,1024,1024]{1,2,0:T(8,128)(2,1)}, bf16[1,1024,1024]{1,2,0:T(8,128)(2,1)}) fusion(bf16[1,1024,1024]{1,2,0:T(8,128)(2,1)} %copy.24, bf16[1,1024,1024]{1,2,0:T(8,128)(2,1)} %copy.30, f32[1,1024,1024]{1,2,0:T(8,128)} %copy.29), kind=kLoop, calls=%fused_computation.6 | loop fusion | flops 6291456 | bytes 12582912 | tf_op jit(solution)/shard_map/convert_element_type | solution.py:18
  146.0 3.9 copy.32
  149.9 54.3 %all_to_all.55 = bf16[1,32,32,1,1024]{4,2,3,0,1:T(8,128)(2,1)S(1)} all-to-all(bf16[1,32,32,1,1024]{4,2,3,0,1:T(8,128)(2,1)} %bitcast.85), channel_id=1, replica_groups=mesh['dp'=8,'seq'=32] {'seq'}, dimensions={1} | all-to-all | bytes 4194304 | tf_op jit(solution)/shard_map/all_to_all | solution.py:30
  204.2 1.2 copy.34
  205.4 0.0 copy-start.2
  205.4 2.4 fusion.25
  207.8 0.0 copy-done.2
  207.9 2.5 copy.35
  210.3 7.2 %all-to-all-start.3 = ((bf16[1,1,32,32,1024]{4,2,1,0,3:T(8,128)(2,1)}), bf16[1,1,32,32,1024]{4,2,1,0,3:T(8,128)(2,1)}, u32[]{:S(2)}, u32[]{:S(2)}) async-start(bf16[1,1,32,32,1024]{4,2,1,0,3:T(8,128)(2,1)} %copy.35), calls=%async_computation.3 | async-start | bytes 4194304 | tf_op jit(solution)/shard_map/all_to_all | solution.py:37
  217.6 0.0 reduce-scatter.5.cloned.1.call-start
  217.6 5.9 %convolution_convert_fusion = bf16[1024,1024]{1,0:T(8,128)(2,1)} fusion(bf16[1024,1024]{1,0:T(8,128)(2,1)} %bitcast.89, bf16[1024,1024]{1,0:T(8,128)(2,1)} %bitcast.87), kind=kOutput, calls=%fused_computation.22 | convolution fusion | flops 2148532224 | bytes 6291456 | tf_op jit(solution)/shard_map/spc,sqc->pq/dot_general | solution.py:47
  223.5 0.0 reduce-scatter.5.cloned.1.call-update
  223.6 0.3 reduce-scatter.3.cloned.1.call-start
  223.8 59.9 %all-to-all-done.3 = bf16[1,1,32,32,1024]{4,2,1,0,3:T(8,128)(2,1)} async-done(((bf16[1,1,32,32,1024]{4,2,1,0,3:T(8,128)(2,1)}), bf16[1,1,32,32,1024]{4,2,1,0,3:T(8,128)(2,1)}, u32[]{:S(2)}, u32[]{:S(2)}) %all-to-all-start.3) | async-done | bytes 2097184 | tf_op jit(solution)/shard_map/all_to_all | solution.py:37
  283.8 5.9 %fusion.14 = bf16[1024,1024]{1,0:T(8,128)(2,1)} fusion(bf16[1024,1024]{1,0:T(8,128)(2,1)} %bitcast.29, bf16[1,1024,1024]{2,1,0:T(8,128)(2,1)} %param.4), kind=kOutput, calls=%fused_computation.18 | convolution fusion | flops 2148532224 | bytes 6291456 | tf_op jit(solution)/shard_map/skc,sjc->kj/dot_general | solution.py:48
  289.7 0.0 reduce-scatter.3.cloned.1.call-update
  289.7 3.9 copy.36
  293.7 7.9 %fusion.2 = bf16[1,1024,1024]{1,2,0:T(8,128)(2,1)} fusion(f32[1,1024,1024]{1,2,0:T(8,128)} %copy.29, bf16[1,1024,1024]{1,2,0:T(8,128)(2,1)} %copy.30, bf16[1024,1024]{1,0:T(8,128)(2,1)} %bitcast.29, bf16[1,1024,1024]{2,1,0:T(8,128)(2,1)} %param.6), kind=kOutput, calls=%fused_computation.5 | convolution fusion | flops 2151677952 | bytes 12582912 | tf_op jit(solution)/shard_map/kj,skc->sjc/dot_general | solution.py:57
  301.6 3.9 copy.37
  305.5 20.0 %reduce-scatter.5.cloned.1.call-done = bf16[128,1024]{1,0:T(8,128)(2,1)} async-done(((bf16[1024,1024]{1,0:T(8,128)(2,1)}), bf16[128,1024]{1,0:T(8,128)(2,1)}) %reduce-scatter.5.cloned.1.call-update) | async-done | bytes 262160 | tf_op jit(solution)/shard_map/reduce_scatter | solution.py:53
  325.5 1.8 bitcast_convert_fusion.1
  327.3 93.9 %reduce-scatter.3.cloned.1.call-done = bf16[128,1024]{1,0:T(8,128)(2,1)} async-done(((bf16[1024,1024]{1,0:T(8,128)(2,1)}), bf16[128,1024]{1,0:T(8,128)(2,1)}) %reduce-scatter.3.cloned.1.call-update) | async-done | bytes 262160 | tf_op jit(solution)/shard_map/reduce_scatter | solution.py:50
  421.2 1.8 bitcast_convert_fusion.2
Async XLA Ops:
  7.2 62.6 %copy-start = (bf16[1,1024,1024]{2,1,0:T(8,128)(2,1)S(1)}, bf16[1,1024,1024]{2,1,0:T(8,128)(2,1)}, u32[]{:S(2)}) copy-start(bf16[1,1024,1024]{2,1,0:T(8,128)(2,1)} %param.7) | copy-start | bytes 6291460
  69.8 2.4 copy-start.1
  74.6 55.1 %all-to-all-start.1 = ((bf16[1,1,32,32,1024]{4,2,1,0,3:T(8,128)(2,1)}), bf16[1,1,32,32,1024]{4,2,1,0,3:T(8,128)(2,1)}, u32[]{:S(2)}, u32[]{:S(2)}) async-start(bf16[1,1,32,32,1024]{4,2,1,0,3:T(8,128)(2,1)} %copy.27), calls=%async_computation.1 | async-start | bytes 4194304 | tf_op jit(solution)/shard_map/all_to_all | solution.py:26
  205.4 2.5 copy-start.2
  210.3 73.4 %all-to-all-start.3 = ((bf16[1,1,32,32,1024]{4,2,1,0,3:T(8,128)(2,1)}), bf16[1,1,32,32,1024]{4,2,1,0,3:T(8,128)(2,1)}, u32[]{:S(2)}, u32[]{:S(2)}) async-start(bf16[1,1,32,32,1024]{4,2,1,0,3:T(8,128)(2,1)} %copy.35), calls=%async_computation.3 | async-start | bytes 4194304 | tf_op jit(solution)/shard_map/all_to_all | solution.py:37
  217.6 108.0 %reduce-scatter.5.cloned.1.call-start = ((), (), s32[]{:S(2)}) async-start(), calls=%async_computation.7 | async-start | bytes 2359296 | tf_op jit(solution)/shard_map/reduce_scatter | solution.py:53
  223.6 197.6 %reduce-scatter.3.cloned.1.call-start = ((), (), s32[]{:S(2)}) async-start(), calls=%async_computation.6 | async-start | bytes 2359296 | tf_op jit(solution)/shard_map/reduce_scatter | solution.py:50
Sparse Core Ops, SparseCore 0:
  223.7 101.8 reduce-scatter.4
  329.6 91.5 reduce-scatter.2
where the time goes:
time: 431 us; the launch traced here: 430 us
  waiting for transfers between devices  214 us (50%)
  blocking collectives  111 us (26%)
  local copies, waits for them, and re-layouts  32.3 us (7%)
  matrix products  29.2 us (7%)
  starting transfers between devices  14.7 us (3%)
  other arithmetic  14.5 us (3%)
  between operations  14.1 us (3%)
    reduce_scatter x1, waiting for transfers between devices, local(): lax.psum_scatter(part_one.astype(jnp.bfloat16), 'dp', scatter_dimension=0...  93.9 us
    all_to_all x1, waiting for transfers between devices, local(): lax.all_to_all(back_two.reshape(seqs, 1, rows, count, width), 'seq', spli...  59.9 us
    all_to_all x1, blocking collectives, local(): lax.all_to_all(first.reshape(seqs, count, rows, 1, width), 'seq', split_a...  56.7 us
    all_to_all x1, blocking collectives, local(): lax.all_to_all(gated.reshape(seqs, count, rows, 1, width), 'seq', split_a...  54.3 us
    all_to_all x1, waiting for transfers between devices, local(): lax.all_to_all(second.reshape(seqs, 1, rows, count, width), 'seq', split_...  40.1 us
    reduce_scatter x1, waiting for transfers between devices, local(): lax.psum_scatter(part_two.astype(jnp.bfloat16), 'dp', scatter_dimension=0...  20 us
    unnamed x10, local copies, waits for them, and re-layouts  15.8 us
  transfers between devices with their start and end apart: 4, of which 4 were waited for; matrix products, arithmetic and copies ran while one was open for 9% of the time, Pallas kernels for 0%

commit v1 on v0

v1 whole, which is shorter than its diff:
```python
import numpy as np
import jax
import jax.numpy as jnp
from jax import lax
from jax.sharding import PartitionSpec as P


def _dp_rings(mesh):
    devs = np.asarray(mesh.devices)
    names = list(mesh.axis_names)
    col = devs.reshape(devs.shape[names.index("dp")], -1) if names.index("dp") == 0 else devs.T
    ndp = col.shape[0]
    try:
        zs = [tuple(col[d, 0].coords)[2] for d in range(ndp)]
        ring = sum(1 for z in zs if z == zs[0])
        if ndp % ring or any(zs[d] != zs[(d // ring) * ring] for d in range(ndp)):
            ring = ndp
    except Exception:
        ring = ndp
    return ring


def _dp_reduce(part, ring):
    ndp = lax.axis_size("dp")
    groups = ndp // ring
    rows = part.shape[0] // ndp
    width = part.shape[1]
    d = lax.axis_index("dp")
    hi = d // ring
    lo = d % ring
    chunks = part.reshape(groups, ring, rows, width)
    acc = lax.dynamic_index_in_dim(chunks, lo, axis=1, keepdims=False).astype(jnp.float32)
    for s in range(1, ring):
        piece = lax.dynamic_index_in_dim(chunks, (lo + s) % ring, axis=1, keepdims=False)
        perm = [(g * ring + t, g * ring + (t + s) % ring) for g in range(groups) for t in range(ring)]
        acc = acc + lax.ppermute(piece, "dp", perm).astype(jnp.float32)
    own = lax.dynamic_index_in_dim(acc, hi, axis=0, keepdims=False)
    for s in range(1, groups):
        piece = lax.dynamic_index_in_dim(acc, (hi + s) % groups, axis=0, keepdims=False)
        perm = [(g * ring + t, ((g + s) % groups) * ring + t) for g in range(groups) for t in range(ring)]
        own = own + lax.ppermute(piece, "dp", perm)
    return own


def local(inputs, cotangent, factor_one, factor_two, ring):
    seqs, block, width = inputs.shape
    count = lax.axis_size("seq")
    rows = block // count
    fone = factor_one[0]
    ftwo = factor_two[0]
    xfull = inputs.astype(jnp.float32)
    dyfull = cotangent.astype(jnp.float32)
    first = jnp.einsum("kj,sjc->skc", fone, inputs, preferred_element_type=jnp.float32).astype(
        jnp.bfloat16
    )
    gated = (dyfull * xfull).astype(jnp.bfloat16)
    out1 = jnp.stack([first, gated]).reshape(2 * seqs, count, rows, 1, width)
    in1 = lax.all_to_all(out1, "seq", split_axis=1, concat_axis=3, tiled=True)
    in1 = in1.reshape(2, seqs, block, width)
    moved = in1[0]
    gated_moved = in1[1]
    second = jnp.einsum("pq,sqc->spc", ftwo, moved, preferred_element_type=jnp.float32).astype(
        jnp.bfloat16
    )
    back_two = jnp.einsum(
        "pq,spc->sqc", ftwo, gated_moved, preferred_element_type=jnp.float32
    ).astype(jnp.bfloat16)
    part_two = jnp.einsum("spc,sqc->pq", gated_moved, moved, preferred_element_type=jnp.float32)
    grad_two = _dp_reduce(part_two.astype(jnp.bfloat16), ring)
    out2 = jnp.stack([second, back_two]).reshape(2 * seqs, 1, rows, count, width)
    in2 = lax.all_to_all(out2, "seq", split_axis=3, concat_axis=1, tiled=True)
    in2 = in2.reshape(2, seqs, block, width)
    monarch = in2[0]
    back_moved = in2[1]
    mfull = monarch.astype(jnp.float32)
    mixed = (xfull * mfull).astype(jnp.bfloat16)
    part_one = jnp.einsum("skc,sjc->kj", back_moved, inputs, preferred_element_type=jnp.float32)
    grad_one = _dp_reduce(part_one.astype(jnp.bfloat16), ring)
    spread = jnp.einsum("kj,skc->sjc", fone, back_moved, preferred_element_type=jnp.float32)
    grad_input = (dyfull * mfull + spread).astype(jnp.bfloat16)
    return (mixed, grad_input, grad_one[None], grad_two[None])


def solution(mesh):
    ring = _dp_rings(mesh)
    in_specs = (
        P("dp", "seq", None),
        P("dp", "seq", None),
        P("seq", None, None),
        P("seq", None, None),
    )
    out_specs = (
        P("dp", "seq", None),
        P("dp", "seq", None),
        P("seq", "dp", None),
        P("seq", "dp", None),
    )
    body = lambda a, b, c, d: local(a, b, c, d, ring)
    return jax.shard_map(body, mesh=mesh, in_specs=in_specs, out_specs=out_specs, check_vma=False)
```

time: 431 us -> 331 us (0.77)
  waiting for transfers between devices: 214 us -> 119 us
  between operations: 14.1 us -> 0.93 us
  starting transfers between devices: 14.7 us -> 26.4 us
  blocking collectives: 111 us -> 102 us
  local copies, waits for them, and re-layouts: 32.3 us -> 38.7 us
  other arithmetic: 14.5 us -> 20.6 us
  matrix products: 29.2 us -> 23.3 us
    reduce_scatter x2 -> x0, waiting for transfers between devices: 114 us -> none  [the longest x1 93.9 us: local(): lax.psum_scatter(part_one.astype(jnp.bfloat16), 'dp', scatter_dimension=0...]
    ppermute x0 -> x8, waiting for transfers between devices: none -> 99.8 us  [the longest x2 70.3 us: _dp_reduce(): own = own + lax.ppermute(piece, 'dp', perm)]
    all_to_all x2 -> x1, waiting for transfers between devices: 100 us -> 19 us  [local(): in2 = lax.all_to_all(out2, 'seq', split_axis=3, concat_axis=1, tiled=True)]
    ppermute x0 -> x8, starting transfers between devices: none -> 19.2 us  [the longest x6 10.2 us: _dp_reduce(): acc = acc + lax.ppermute(piece, 'dp', perm).astype(jnp.float32)]
    all_to_all x2 -> x1, blocking collectives: 111 us -> 102 us  [local(): in1 = lax.all_to_all(out1, 'seq', split_axis=1, concat_axis=3, tiled=True)]
    all_to_all x2 -> x1, starting transfers between devices: 14.4 us -> 7.24 us  [local(): in2 = lax.all_to_all(out2, 'seq', split_axis=3, concat_axis=1, tiled=True)]
    reshape x2 -> x0, local copies, waits for them, and re-layouts: 4.94 us -> none  [the longest x1 2.47 us: local(): second.reshape(seqs, 1, rows, count, width)]
    unnamed x10 -> x26, local copies, waits for them, and re-layouts: 15.8 us -> 16.9 us
  transfers between devices with their start and end apart: 4 -> 9, of which waited for: 4 -> 7; matrix products, arithmetic and copies ran while one was open for 9% -> 11% of each run, Pallas kernels for 0% -> 0%
where the time goes in v1:
time: 331 us; the launch traced here: 330 us
  waiting for transfers between devices  119 us (36%)
  blocking collectives  102 us (31%)
  local copies, waits for them, and re-layouts  38.7 us (12%)
  starting transfers between devices  26.4 us (8%)
  matrix products  23.3 us (7%)
  other arithmetic  20.6 us (6%)
    all_to_all x1, blocking collectives, local(): in1 = lax.all_to_all(out1, 'seq', split_axis=1, concat_axis=3, tiled=True)  102 us
    ppermute x2, waiting for transfers between devices, _dp_reduce(): own = own + lax.ppermute(piece, 'dp', perm)  70.3 us
    ppermute x6, waiting for transfers between devices, _dp_reduce(): acc = acc + lax.ppermute(piece, 'dp', perm).astype(jnp.float32)  29.4 us
    all_to_all x1, waiting for transfers between devices, local(): in2 = lax.all_to_all(out2, 'seq', split_axis=3, concat_axis=1, tiled=True)  19 us
    unnamed x26, local copies, waits for them, and re-layouts  16.9 us
    ppermute x6, starting transfers between devices, _dp_reduce(): acc = acc + lax.ppermute(piece, 'dp', perm).astype(jnp.float32)  10.2 us
    ppermute x2, starting transfers between devices, _dp_reduce(): own = own + lax.ppermute(piece, 'dp', perm)  9.03 us
    all_to_all x1, starting transfers between devices, local(): in2 = lax.all_to_all(out2, 'seq', split_axis=3, concat_axis=1, tiled=True)  7.24 us
  transfers between devices with their start and end apart: 9, of which 7 were waited for; matrix products, arithmetic and copies ran while one was open for 11% of the time, Pallas kernels for 0%

profile of v1, /device:TPU:8, one launch (start us, length us, event | category | flops | bytes accessed | tf_op | source)
XLA Modules:
  0.0 330.3 jit_solution(8153390242816870938)
XLA Ops:
  0.6 4.1 %copy.26 = bf16[1,1024,1024]{1,2,0:T(8,128)(2,1)} copy(bf16[1,1024,1024]{2,1,0:T(8,128)(2,1)} %param.5) | data formatting | bytes 4194304 | tf_op args[1]
  4.8 3.9 %copy.25 = bf16[1,1024,1024]{1,2,0:T(8,128)(2,1)} copy(bf16[1,1024,1024]{2,1,0:T(8,128)(2,1)} %param.4) | data formatting | bytes 4194304 | tf_op args[0]
  8.7 4.5 %fusion.1 = bf16[1,1024,1024]{1,2,0:T(8,128)(2,1)} fusion(bf16[1,1024,1024]{1,2,0:T(8,128)(2,1)} %copy.25, bf16[1,1024,1024]{1,2,0:T(8,128)(2,1)} %copy.26), kind=kLoop, calls=%fused_computation.4 | loop fusion | flops 4194304 | bytes 6291456 | tf_op jit(solution)/shard_map/convert_element_type | solution.py:56
  13.2 3.9 %copy.27 = bf16[1,1024,1024]{2,1,0:T(8,128)(2,1)} copy(bf16[1,1024,1024]{1,2,0:T(8,128)(2,1)} %fusion.1) | data formatting | bytes 4194304 | tf_op jit(solution)/shard_map/convert_element_type | solution.py:56
  17.1 4.7 %fusion.17 = bf16[1024,1024]{0,1:T(8,128)(2,1)S(1)} fusion(bf16[1,1024,1024]{2,1,0:T(8,128)(2,1)} %param.4, bf16[1,1024,1024]{2,1,0:T(8,128)(2,1)} %param.6), kind=kOutput, calls=%fused_computation.23 | convolution fusion | flops 2148532224 | bytes 6291456 | tf_op jit(solution)/shard_map/kj,sjc->skc/dot_general | solution.py:53
  22.3 0.8 copy.28
  23.1 101.7 %all_to_all.30 = bf16[2,32,32,1,1024]{4,2,3,0,1:T(8,128)(2,1)S(1)} all-to-all(bf16[2,32,32,1,1024]{4,2,3,0,1:T(8,128)(2,1)S(1)} %copy.28), channel_id=1, replica_groups=mesh['dp'=8,'seq'=32] {'seq'}, dimensions={1} | all-to-all | bytes 8388608 | tf_op jit(solution)/shard_map/all_to_all | solution.py:58
  124.7 2.3 copy.40
  127.1 0.6 fusion.35
  127.7 2.4 fusion.22
  130.1 1.2 copy.30
  131.2 2.4 fusion.25
  133.7 1.2 copy.31
  134.8 2.4 pad_maximum_fusion.1
  137.2 7.2 %all-to-all-start.1 = ((bf16[2,1,32,32,1024]{4,2,0,1,3:T(8,128)(2,1)}), bf16[2,1,32,32,1024]{4,2,0,1,3:T(8,128)(2,1)}, u32[]{:S(2)}, u32[]{:S(2)}) async-start(bf16[2,1,32,32,1024]{4,2,0,1,3:T(8,128)(2,1)} %pad_maximum_fusion.1), calls=%async_computation.1 | async-start | bytes 8388608 | tf_op jit(solution)/shard_map/all_to_all | solution.py:71
  144.5 4.6 %convolution_convert_fusion = bf16[1024,1024]{1,0:T(8,128)(2,1)S(1)} fusion(bf16[1024,1024]{1,0:T(8,128)(2,1)} %bitcast.115, bf16[1024,1024]{1,0:T(8,128)(2,1)} %bitcast.113), kind=kOutput, calls=%fused_computation.26 | convolution fusion | flops 2148532224 | bytes 6291456 | tf_op jit(solution)/shard_map/spc,sqc->pq/dot_general | solution.py:68
  149.2 1.1 dynamic-slice_bitcast_fusion.3
  150.2 1.5 collective-permute-start.4
  151.7 1.7 collective-permute-start.6
  153.5 1.8 collective-permute-start.5
  155.3 10.4 %collective-permute-done.4 = bf16[2,128,1024]{2,1,0:T(8,128)(2,1)} collective-permute-done((bf16[2,128,1024]{2,1,0:T(8,128)(2,1)}, bf16[2,128,1024]{2,1,0:T(8,128)(2,1)}, u32[]{:S(2)}, u32[]{:S(2)}) %collective-permute-start.4) | collective-permute-done | bytes 524320 | tf_op jit(solution)/shard_map/ppermute | solution.py:36
  165.7 0.9 collective-permute-done.6
  166.6 11.3 %collective-permute-done.5 = bf16[2,128,1024]{2,1,0:T(8,128)(2,1)} collective-permute-done((bf16[2,128,1024]{2,1,0:T(8,128)(2,1)S(1)}, bf16[2,128,1024]{2,1,0:T(8,128)(2,1)}, u32[]{:S(2)}, u32[]{:S(2)}) %collective-permute-start.5) | collective-permute-done | bytes 524320 | tf_op jit(solution)/shard_map/ppermute | solution.py:36
  177.9 1.9 fusion.29
  179.8 4.6 %collective-permute-start.7 = (f32[128,1024]{1,0:T(8,128)S(1)}, f32[128,1024]{1,0:T(8,128)S(1)}, u32[]{:S(2)}, u32[]{:S(2)}) collective-permute-start(f32[128,1024]{1,0:T(8,128)S(1)} %dynamic-slice_bitcast_fusion), channel_id=1, source_target_pairs={{0,128},{32,160},{64,192},{96,224},{128,0},{160,32},{192,64},{224,... | collective-permute-start | bytes 1572872 | tf_op jit(solution)/shard_map/ppermute | solution.py:41
  184.4 56.0 %collective-permute-done.7 = f32[128,1024]{1,0:T(8,128)S(1)} collective-permute-done((f32[128,1024]{1,0:T(8,128)S(1)}, f32[128,1024]{1,0:T(8,128)S(1)}, u32[]{:S(2)}, u32[]{:S(2)}) %collective-permute-start.7) | collective-permute-done | bytes 524320 | tf_op jit(solution)/shard_map/ppermute | solution.py:41
  240.4 0.9 fusion.32
  241.2 19.0 %all-to-all-done.1 = bf16[2,1,32,32,1024]{4,2,0,1,3:T(8,128)(2,1)} async-done(((bf16[2,1,32,32,1024]{4,2,0,1,3:T(8,128)(2,1)}), bf16[2,1,32,32,1024]{4,2,0,1,3:T(8,128)(2,1)}, u32[]{:S(2)}, u32[]{:S(2)}) %all-to-all-start.1) | async-done | bytes 4194336 | tf_op jit(solution)/shard_map/all_to_all | solution.py:71
  260.2 2.6 copy.39
  262.8 0.6 fusion.34
  263.5 1.0 copy-done.5
  264.4 2.4 fusion.14
  266.8 1.1 dynamic-slice_bitcast_fusion.7
  267.9 1.5 collective-permute-start
  269.5 1.7 collective-permute-start.2
  271.2 1.9 collective-permute-start.1
  273.0 2.6 bitcast_convert_fusion
  275.6 5.5 %copy.33 = f32[1,1024,1024]{1,2,0:T(8,128)} copy(f32[1,1024,1024]{2,1,0:T(8,128)} %bitcast_convert_fusion) | data formatting | bytes 8388608 | tf_op jit(solution)/shard_map/convert_element_type | solution.py:75
  281.1 4.3 %fusion = bf16[1,1024,1024]{1,2,0:T(8,128)(2,1)} fusion(f32[1,1024,1024]{1,2,0:T(8,128)} %copy.33, bf16[1,1024,1024]{1,2,0:T(8,128)(2,1)S(1)} %copy-done.2), kind=kLoop, calls=%fused_computation.3 | loop fusion | flops 3145728 | bytes 8388608 | tf_op jit(solution)/shard_map/convert_element_type | solution.py:76
  285.4 3.9 %copy.35 = bf16[1,1024,1024]{2,1,0:T(8,128)(2,1)} copy(bf16[1,1024,1024]{1,2,0:T(8,128)(2,1)} %fusion) | data formatting | bytes 4194304
  289.4 6.8 %collective-permute-done.1 = bf16[2,128,1024]{2,1,0:T(8,128)(2,1)} collective-permute-done((bf16[2,128,1024]{2,1,0:T(8,128)(2,1)S(1)}, bf16[2,128,1024]{2,1,0:T(8,128)(2,1)}, u32[]{:S(2)}, u32[]{:S(2)}) %collective-permute-start.1) | collective-permute-done | bytes 524320 | tf_op jit(solution)/shard_map/ppermute | solution.py:36
  296.2 1.8 fusion.31
  298.0 0.8 dynamic-slice_bitcast_fusion.4
  298.8 4.4 %collective-permute-start.3 = (f32[128,1024]{1,0:T(8,128)}, f32[128,1024]{1,0:T(8,128)}, u32[]{:S(2)}, u32[]{:S(2)}) collective-permute-start(f32[128,1024]{1,0:T(8,128)} %dynamic-slice_bitcast_fusion.4), channel_id=1, source_target_pairs={{0,128},{32,160},{64,192},{96,224},{128,0},{160,32},{192,64},{224,... | collective-permute-start | bytes 1572872 | tf_op jit(solution)/shard_map/ppermute | solution.py:41
  303.3 6.9 %fusion.3 = bf16[1,1024,1024]{1,2,0:T(8,128)(2,1)} fusion(f32[1,1024,1024]{1,2,0:T(8,128)S(1)} %copy-done.3, bf16[1,1024,1024]{1,2,0:T(8,128)(2,1)} %copy.26, bf16[1024,1024]{1,0:T(8,128)(2,1)} %bitcast.117, bf16[1,1024,1024]{2,1,0:T(8,128)(2,1)} %param.6), kind=kOutput, calls=%fused_computation.6 | convolution fusion | flops 2151677952 | bytes 12582912 | tf_op jit(solution)/shard_map/kj,skc->sjc/dot_general | solution.py:79
  310.2 3.9 %copy.36 = bf16[1,1024,1024]{2,1,0:T(8,128)(2,1)} copy(bf16[1,1024,1024]{1,2,0:T(8,128)(2,1)} %fusion.3) | data formatting | bytes 4194304
  314.1 14.4 %collective-permute-done.3 = f32[128,1024]{1,0:T(8,128)} collective-permute-done((f32[128,1024]{1,0:T(8,128)}, f32[128,1024]{1,0:T(8,128)}, u32[]{:S(2)}, u32[]{:S(2)}) %collective-permute-start.3) | collective-permute-done | bytes 524320 | tf_op jit(solution)/shard_map/ppermute | solution.py:41
  328.4 1.9 fusion.33
  (25 shorter events, 0.5 us)
Async XLA Ops:
  0.6 127.1 %copy-start = (bf16[1,1024,1024]{2,1,0:T(8,128)(2,1)S(1)}, bf16[1,1024,1024]{2,1,0:T(8,128)(2,1)}, u32[]{:S(2)}) copy-start(bf16[1,1024,1024]{2,1,0:T(8,128)(2,1)} %param.7) | copy-start | bytes 6291460
  17.1 4.7 %copy-start.4 = (bf16[1,1024,1024]{2,1,0:T(8,128)(2,1)S(1)}, bf16[1,1024,1024]{2,1,0:T(8,128)(2,1)}, u32[]{:S(2)}) copy-start(bf16[1,1024,1024]{2,1,0:T(8,128)(2,1)} %copy.27) | copy-start | bytes 6291460
  127.7 2.4 copy-start.8
  127.7 3.6 %copy-start.9 = (bf16[1,1,32,32,1,1024]{5,3,2,4,1,0:T(8,128)(2,1)}, bf16[1,1,32,32,1,1024]{5,3,2,4,1,0:T(8,128)(2,1)S(1)}, u32[]{:S(2)}) copy-start(bf16[1,1,32,32,1,1024]{5,3,2,4,1,0:T(8,128)(2,1)S(1)} %get-tuple-element.19) | copy-start | bytes 6291460
  137.2 123.0 %all-to-all-start.1 = ((bf16[2,1,32,32,1024]{4,2,0,1,3:T(8,128)(2,1)}), bf16[2,1,32,32,1024]{4,2,0,1,3:T(8,128)(2,1)}, u32[]{:S(2)}, u32[]{:S(2)}) async-start(bf16[2,1,32,32,1024]{4,2,0,1,3:T(8,128)(2,1)} %pad_maximum_fusion.1), calls=%async_computation.1 | async-start | bytes 8388608 | tf_op jit(solution)/shard_map/all_to_all | solution.py:71
  149.1 17.5 %copy-start.6 = (bf16[1024,1024]{1,0:T(8,128)(2,1)}, bf16[1024,1024]{1,0:T(8,128)(2,1)S(1)}, u32[]{:S(2)}) copy-start(bf16[1024,1024]{1,0:T(8,128)(2,1)S(1)} %convolution_convert_fusion) | copy-start | bytes 6291460
  150.2 15.5 %collective-permute-start.4 = (bf16[2,128,1024]{2,1,0:T(8,128)(2,1)}, bf16[2,128,1024]{2,1,0:T(8,128)(2,1)}, u32[]{:S(2)}, u32[]{:S(2)}) collective-permute-start(bf16[2,128,1024]{2,1,0:T(8,128)(2,1)} %get-tuple-element.20), channel_id=1, source_target_pairs={{0,32},{32,64},{64,96},{96,0},{128,160},{160,192},{192,224},{224,1... | collective-permute-start | bytes 1572872 | tf_op jit(solution)/shard_map/ppermute | solution.py:36
  151.7 14.9 %collective-permute-start.6 = (bf16[2,128,1024]{2,1,0:T(8,128)(2,1)S(1)}, bf16[2,128,1024]{2,1,0:T(8,128)(2,1)}, u32[]{:S(2)}, u32[]{:S(2)}) collective-permute-start(bf16[2,128,1024]{2,1,0:T(8,128)(2,1)S(1)} %get-tuple-element.21), channel_id=1, source_target_pairs={{0,96},{32,0},{64,32},{96,64},{128,224},{160,128},{192,160},{224,1... | collective-permute-start | bytes 1572872 | tf_op jit(solution)/shard_map/ppermute | solution.py:36
  153.5 24.4 %collective-permute-start.5 = (bf16[2,128,1024]{2,1,0:T(8,128)(2,1)S(1)}, bf16[2,128,1024]{2,1,0:T(8,128)(2,1)}, u32[]{:S(2)}, u32[]{:S(2)}) collective-permute-start(bf16[2,128,1024]{2,1,0:T(8,128)(2,1)S(1)} %get-tuple-element.22), channel_id=1, source_target_pairs={{0,64},{32,96},{64,0},{96,32},{128,192},{160,224},{192,128},{224,1... | collective-permute-start | bytes 1572872 | tf_op jit(solution)/shard_map/ppermute | solution.py:36
  179.8 60.5 %collective-permute-start.7 = (f32[128,1024]{1,0:T(8,128)S(1)}, f32[128,1024]{1,0:T(8,128)S(1)}, u32[]{:S(2)}, u32[]{:S(2)}) collective-permute-start(f32[128,1024]{1,0:T(8,128)S(1)} %dynamic-slice_bitcast_fusion), channel_id=1, source_target_pairs={{0,128},{32,160},{64,192},{96,224},{128,0},{160,32},{192,64},{224,... | collective-permute-start | bytes 1572872 | tf_op jit(solution)/shard_map/ppermute | solution.py:41
  262.8 1.6 copy-start.5
  263.4 3.4 %copy-start.10 = (bf16[1,32,1,32,1,1024]{5,3,1,4,2,0:T(8,128)(2,1)}, bf16[1,32,1,32,1,1024]{5,3,1,4,2,0:T(8,128)(2,1)S(1)}, u32[]{:S(2)}) copy-start(bf16[1,32,1,32,1,1024]{5,3,1,4,2,0:T(8,128)(2,1)S(1)} %get-tuple-element.16) | copy-start | bytes 6291460
  266.8 6.2 %copy-start.7 = (bf16[1024,1024]{1,0:T(8,128)(2,1)}, bf16[1024,1024]{1,0:T(8,128)(2,1)S(1)}, u32[]{:S(2)}) copy-start(bf16[1024,1024]{1,0:T(8,128)(2,1)S(1)} %fusion.14) | copy-start | bytes 6291460
  267.9 21.4 %collective-permute-start = (bf16[2,128,1024]{2,1,0:T(8,128)(2,1)}, bf16[2,128,1024]{2,1,0:T(8,128)(2,1)}, u32[]{:S(2)}, u32[]{:S(2)}) collective-permute-start(bf16[2,128,1024]{2,1,0:T(8,128)(2,1)} %get-tuple-element.23), channel_id=1, source_target_pairs={{0,32},{32,64},{64,96},{96,0},{128,160},{160,192},{192,224},{224,1... | collective-permute-start | bytes 1572872 | tf_op jit(solution)/shard_map/ppermute | solution.py:36
  269.5 19.9 %collective-permute-start.2 = (bf16[2,128,1024]{2,1,0:T(8,128)(2,1)S(1)}, bf16[2,128,1024]{2,1,0:T(8,128)(2,1)}, u32[]{:S(2)}, u32[]{:S(2)}) collective-permute-start(bf16[2,128,1024]{2,1,0:T(8,128)(2,1)S(1)} %get-tuple-element.24), channel_id=1, source_target_pairs={{0,96},{32,0},{64,32},{96,64},{128,224},{160,128},{192,160},{224,1... | collective-permute-start | bytes 1572872 | tf_op jit(solution)/shard_map/ppermute | solution.py:36
  271.2 25.0 %collective-permute-start.1 = (bf16[2,128,1024]{2,1,0:T(8,128)(2,1)S(1)}, bf16[2,128,1024]{2,1,0:T(8,128)(2,1)}, u32[]{:S(2)}, u32[]{:S(2)}) collective-permute-start(bf16[2,128,1024]{2,1,0:T(8,128)(2,1)S(1)} %get-tuple-element.25), channel_id=1, source_target_pairs={{0,64},{32,96},{64,0},{96,32},{128,192},{160,224},{192,128},{224,1... | collective-permute-start | bytes 1572872 | tf_op jit(solution)/shard_map/ppermute | solution.py:36
  275.6 5.5 %copy-start.2 = (bf16[1,1024,1024]{1,2,0:T(8,128)(2,1)S(1)}, bf16[1,1024,1024]{1,2,0:T(8,128)(2,1)}, u32[]{:S(2)}) copy-start(bf16[1,1024,1024]{1,2,0:T(8,128)(2,1)} %copy.25) | copy-start | bytes 6291460
  289.3 13.9 %copy-start.3 = (f32[1,1024,1024]{1,2,0:T(8,128)S(1)}, f32[1,1024,1024]{1,2,0:T(8,128)}, u32[]{:S(2)}) copy-start(f32[1,1024,1024]{1,2,0:T(8,128)} %copy.33) | copy-start | bytes 12582916
  298.8 29.6 %collective-permute-start.3 = (f32[128,1024]{1,0:T(8,128)}, f32[128,1024]{1,0:T(8,128)}, u32[]{:S(2)}, u32[]{:S(2)}) collective-permute-start(f32[128,1024]{1,0:T(8,128)} %dynamic-slice_bitcast_fusion.4), channel_id=1, source_target_pairs={{0,128},{32,160},{64,192},{96,224},{128,0},{160,32},{192,64},{224,... | collective-permute-start | bytes 1572872 | tf_op jit(solution)/shard_map/ppermute | solution.py:41
  303.3 27.1 %copy-start.1 = (bf16[1,1024,1024]{2,1,0:T(8,128)(2,1)S(1)}, bf16[1,1024,1024]{2,1,0:T(8,128)(2,1)}, u32[]{:S(2)}) copy-start(bf16[1,1024,1024]{2,1,0:T(8,128)(2,1)} %param.7) | copy-start | bytes 6291460

commit v2 on v1

--- a/solution.py
+++ b/solution.py
@@ -38,8 +38,24 @@
     for s in range(1, groups):
         piece = lax.dynamic_index_in_dim(acc, (hi + s) % groups, axis=0, keepdims=False)
         perm = [(g * ring + t, ((g + s) % groups) * ring + t) for g in range(groups) for t in range(ring)]
-        own = own + lax.ppermute(piece, "dp", perm)
+        own = own + lax.ppermute(piece.astype(jnp.bfloat16), "dp", perm).astype(jnp.float32)
     return own
+
+
+def _to_moved(data, count, rows):
+    seqs, block, width = data.shape
+    out = lax.all_to_all(
+        data.reshape(seqs, count, rows, 1, width), "seq", split_axis=1, concat_axis=3, tiled=True
+    )
+    return out.reshape(seqs, block, width)
+
+
+def _from_moved(data, count, rows):
+    seqs, block, width = data.shape
+    out = lax.all_to_all(
+        data.reshape(seqs, 1, rows, count, width), "seq", split_axis=3, concat_axis=1, tiled=True
+    )
+    return out.reshape(seqs, block, width)
 
 
 def local(inputs, cotangent, factor_one, factor_two, ring):
@@ -50,33 +66,31 @@
     ftwo = factor_two[0]
     xfull = inputs.astype(jnp.float32)
     dyfull = cotangent.astype(jnp.float32)
+    gated = (dyfull * xfull).astype(jnp.bfloat16)
     first = jnp.einsum("kj,sjc->skc", fone, inputs, preferred_element_type=jnp.float32).astype(
         jnp.bfloat16
     )
-    gated = (dyfull * xfull).astype(jnp.bfloat16)
     out1 = jnp.stack([first, gated]).reshape(2 * seqs, count, rows, 1, width)
     in1 = lax.all_to_all(out1, "seq", split_axis=1, concat_axis=3, tiled=True)
     in1 = in1.reshape(2, seqs, block, width)
     moved = in1[0]
     gated_moved = in1[1]
+    back_two = jnp.einsum(
+        "pq,spc->sqc", ftwo, gated_moved, preferred_element_type=jnp.float32
+    ).astype(jnp.bfloat16)
+    back_moved = _from_moved(back_two, count, rows)
     second = jnp.einsum("pq,sqc->spc", ftwo, moved, preferred_element_type=jnp.float32).astype(
         jnp.bfloat16
     )
-    back_two = jnp.einsum(
-        "pq,spc->sqc", ftwo, gated_moved, preferred_element_type=jnp.float32
-    ).astype(jnp.bfloat16)
     part_two = jnp.einsum("spc,sqc->pq", gated_moved, moved, preferred_element_type=jnp.float32)
     grad_two = _dp_reduce(part_two.astype(jnp.bfloat16), ring)
-    out2 = jnp.stack([second, back_two]).reshape(2 * seqs, 1, rows, count, width)
-    in2 = lax.all_to_all(out2, "seq", split_axis=3, concat_axis=1, tiled=True)
-    in2 = in2.reshape(2, seqs, block, width)
-    monarch = in2[0]
-    back_moved = in2[1]
+    part_one = jnp.einsum("skc,sjc->kj", back_moved, inputs, preferred_element_type=jnp.float32)
+    part_one, second = lax.optimization_barrier((part_one.astype(jnp.bfloat16), second))
+    grad_one = _dp_reduce(part_one, ring)
+    monarch = _from_moved(second, count, rows)
+    spread = jnp.einsum("kj,skc->sjc", fone, back_moved, preferred_element_type=jnp.float32)
     mfull = monarch.astype(jnp.float32)
     mixed = (xfull * mfull).astype(jnp.bfloat16)
-    part_one = jnp.einsum("skc,sjc->kj", back_moved, inputs, preferred_element_type=jnp.float32)
-    grad_one = _dp_reduce(part_one.astype(jnp.bfloat16), ring)
-    spread = jnp.einsum("kj,skc->sjc", fone, back_moved, preferred_element_type=jnp.float32)
     grad_input = (dyfull * mfull + spread).astype(jnp.bfloat16)
     return (mixed, grad_input, grad_one[None], grad_two[None])
 

time: 331 us -> 311 us (0.940); the launches traced: 330 us -> 305 us
  waiting for transfers between devices: 119 us -> 69.4 us
  starting transfers between devices: 26.4 us -> 43.6 us
  matrix products: 23.3 us -> 31 us
  other arithmetic: 20.6 us -> 16.1 us
  local copies, waits for them, and re-layouts: 38.7 us -> 42.6 us
    ppermute x2, waiting for transfers between devices: 70.3 us -> 6.51 us  [_dp_reduce(): lax.ppermute(piece.astype(jnp.bfloat16), 'dp', perm).astype(jnp.float32)]
    all_to_all x1 -> x2, waiting for transfers between devices: 19 us -> 42.6 us  [_from_moved(): lax.all_to_all(data.reshape(seqs, 1, rows, count, width), 'seq', split_ax...]
    ppermute x6, starting transfers between devices: 10.2 us -> 20.7 us  [_dp_reduce(): acc = acc + lax.ppermute(piece, 'dp', perm).astype(jnp.float32)]
    ppermute x6, waiting for transfers between devices: 29.4 us -> 20.3 us  [_dp_reduce(): acc = acc + lax.ppermute(piece, 'dp', perm).astype(jnp.float32)]
    all_to_all x1 -> x2, starting transfers between devices: 7.24 us -> 13.9 us  [_from_moved(): lax.all_to_all(data.reshape(seqs, 1, rows, count, width), 'seq', split_ax...]
    reshape x0 -> x2, local copies, waits for them, and re-layouts: none -> 4.95 us  [_from_moved(): data.reshape(seqs, 1, rows, count, width)]
    dot_general x1, matrix products: 2.37 us -> 5.9 us  [local(): jnp.einsum('skc,sjc->kj', back_moved, inputs, preferred_element_type=jnp....]
    unnamed x26 -> x24, local copies, waits for them, and re-layouts: 16.9 us -> 17.9 us
  transfers between devices with their start and end apart: 9 -> 10, of which waited for: 7 -> 6; matrix products, arithmetic and copies ran while one was open for 11% -> 6% of each run, Pallas kernels for 0% -> 0%
where the time goes in v2:
time: 311 us; the launch traced here: 305 us
  blocking collectives  102 us (33%)
  waiting for transfers between devices  69.4 us (22%)
  starting transfers between devices  43.6 us (14%)
  local copies, waits for them, and re-layouts  42.6 us (14%)
  matrix products  31 us (10%)
  other arithmetic  16.1 us (5%)
    all_to_all x1, blocking collectives, local(): in1 = lax.all_to_all(out1, 'seq', split_axis=1, concat_axis=3, tiled=True)  102 us
    all_to_all x2, waiting for transfers between devices, _from_moved(): lax.all_to_all(data.reshape(seqs, 1, rows, count, width), 'seq', split_ax...  42.6 us
    ppermute x6, starting transfers between devices, _dp_reduce(): acc = acc + lax.ppermute(piece, 'dp', perm).astype(jnp.float32)  20.7 us
    ppermute x6, waiting for transfers between devices, _dp_reduce(): acc = acc + lax.ppermute(piece, 'dp', perm).astype(jnp.float32)  20.3 us
    unnamed x24, local copies, waits for them, and re-layouts  17.9 us
    all_to_all x2, starting transfers between devices, _from_moved(): lax.all_to_all(data.reshape(seqs, 1, rows, count, width), 'seq', split_ax...  13.9 us
    ppermute x2, starting transfers between devices, _dp_reduce(): lax.ppermute(piece.astype(jnp.bfloat16), 'dp', perm).astype(jnp.float32)  8.98 us
    dot_general x1, matrix products, local(): jnp.einsum('kj,skc->sjc', fone, back_moved, preferred_element_type=jnp.fl...  8 us
  transfers between devices with their start and end apart: 10, of which 6 were waited for; matrix products, arithmetic and copies ran while one was open for 6% of the time, Pallas kernels for 0%

profile of v2, /device:TPU:8, one launch (start us, length us, event | category | flops | bytes accessed | tf_op | source)
XLA Modules:
  0.0 305.2 jit_solution(11577243763415519562)
XLA Ops:
  0.6 4.1 %copy.31 = bf16[1,1024,1024]{1,2,0:T(8,128)(2,1)} copy(bf16[1,1024,1024]{2,1,0:T(8,128)(2,1)} %param.5) | data formatting | bytes 4194304 | tf_op args[1]
  4.7 3.9 %copy.30 = bf16[1,1024,1024]{1,2,0:T(8,128)(2,1)} copy(bf16[1,1024,1024]{2,1,0:T(8,128)(2,1)} %param.4) | data formatting | bytes 4194304 | tf_op args[0]
  8.7 4.5 %fusion.1 = bf16[1,1024,1024]{1,2,0:T(8,128)(2,1)} fusion(bf16[1,1024,1024]{1,2,0:T(8,128)(2,1)} %copy.30, bf16[1,1024,1024]{1,2,0:T(8,128)(2,1)} %copy.31), kind=kLoop, calls=%fused_computation.4 | loop fusion | flops 4194304 | bytes 6291456 | tf_op jit(solution)/shard_map/convert_element_type | solution.py:69
  13.2 3.9 %copy.32 = bf16[1,1024,1024]{2,1,0:T(8,128)(2,1)} copy(bf16[1,1024,1024]{1,2,0:T(8,128)(2,1)} %fusion.1) | data formatting | bytes 4194304 | tf_op jit(solution)/shard_map/convert_element_type | solution.py:69
  17.1 4.7 %fusion.17 = bf16[1024,1024]{0,1:T(8,128)(2,1)S(1)} fusion(bf16[1,1024,1024]{2,1,0:T(8,128)(2,1)} %param.4, bf16[1,1024,1024]{2,1,0:T(8,128)(2,1)} %param.6), kind=kOutput, calls=%fused_computation.22 | convolution fusion | flops 2148532224 | bytes 6291456 | tf_op jit(solution)/shard_map/kj,sjc->skc/dot_general | solution.py:70
  21.8 0.4 pad_maximum_fusion
  22.2 0.8 copy.33
  23.0 101.7 %all_to_all.39 = bf16[2,32,32,1,1024]{4,2,3,0,1:T(8,128)(2,1)S(1)} all-to-all(bf16[2,32,32,1,1024]{4,2,3,0,1:T(8,128)(2,1)S(1)} %copy.33), channel_id=1, replica_groups=mesh['dp'=8,'seq'=32] {'seq'}, dimensions={1} | all-to-all | bytes 8388608 | tf_op jit(solution)/shard_map/all_to_all | solution.py:74
  124.7 2.3 copy.48
  127.0 1.8 fusion.35
  128.8 2.5 fusion.22
  131.3 2.5 copy.35
  133.8 7.3 %all-to-all-start.1 = ((bf16[1,1,32,32,1024]{4,2,1,0,3:T(8,128)(2,1)}), bf16[1,1,32,32,1024]{4,2,1,0,3:T(8,128)(2,1)}, u32[]{:S(2)}, u32[]{:S(2)}) async-start(bf16[1,1,32,32,1024]{4,2,1,0,3:T(8,128)(2,1)} %copy.35), calls=%async_computation.1 | async-start | bytes 4194304 | tf_op jit(solution)/shard_map/all_to_all | solution.py:55
  141.1 5.3 %convert_bitcast_fusion = bf16[1,1024,1024]{1,2,0:T(8,128)(2,1)} fusion(bf16[1024,1024]{1,0:T(8,128)(2,1)} %bitcast.120, bf16[1,1024,1024]{2,1,0:T(8,128)(2,1)S(1)} %copy-done), kind=kOutput, calls=%fused_computation.20 | convolution fusion | flops 2148532224 | bytes 6291456 | tf_op jit(solution)/shard_map/pq,sqc->spc/dot_general | solution.py:82
  146.4 42.6 %all-to-all-done.1 = bf16[1,1,32,32,1024]{4,2,1,0,3:T(8,128)(2,1)} async-done(((bf16[1,1,32,32,1024]{4,2,1,0,3:T(8,128)(2,1)}), bf16[1,1,32,32,1024]{4,2,1,0,3:T(8,128)(2,1)}, u32[]{:S(2)}, u32[]{:S(2)}) %all-to-all-start.1) | async-done | bytes 2097184 | tf_op jit(solution)/shard_map/all_to_all | solution.py:55
  189.0 5.9 %fusion.14 = bf16[1024,1024]{1,0:T(8,128)(2,1)} fusion(bf16[1024,1024]{1,0:T(8,128)(2,1)} %bitcast.15, bf16[1,1024,1024]{2,1,0:T(8,128)(2,1)} %param.4), kind=kOutput, calls=%fused_computation.21 | convolution fusion | flops 2148532224 | bytes 6291456 | tf_op jit(solution)/shard_map/skc,sjc->kj/dot_general | solution.py:87
  194.9 2.9 copy.36
  197.8 2.5 copy.37
  200.3 6.5 %all-to-all-start.2 = ((bf16[1,1,32,32,1024]{4,2,1,0,3:T(8,128)(2,1)}), bf16[1,1,32,32,1024]{4,2,1,0,3:T(8,128)(2,1)S(1)}, u32[]{:S(2)}, u32[]{:S(2)}) async-start(bf16[1,1,32,32,1024]{4,2,1,0,3:T(8,128)(2,1)} %copy.37), calls=%async_computation.2 | async-start | bytes 4194304 | tf_op jit(solution)/shard_map/all_to_all | solution.py:55
  206.9 4.6 %convolution_convert_fusion = bf16[1024,1024]{1,0:T(8,128)(2,1)S(1)} fusion(bf16[1024,1024]{1,0:T(8,128)(2,1)} %bitcast.123, bf16[1024,1024]{1,0:T(8,128)(2,1)} %bitcast.121), kind=kOutput, calls=%fused_computation.24 | convolution fusion | flops 2148532224 | bytes 6291456 | tf_op jit(solution)/shard_map/spc,sqc->pq/dot_general | solution.py:85
  211.7 1.6 collective-permute-start.4
  213.2 1.7 collective-permute-start.6
  215.0 1.8 collective-permute-start.5
  216.8 1.2 dynamic-slice_bitcast_fusion.5
  218.0 0.6 collective-permute-start
  218.6 2.6 collective-permute-start.2
  221.2 7.2 %collective-permute-done.4 = bf16[2,128,1024]{2,1,0:T(8,128)(2,1)S(1)} collective-permute-done((bf16[2,128,1024]{2,1,0:T(8,128)(2,1)S(1)}, bf16[2,128,1024]{2,1,0:T(8,128)(2,1)S(1)}, u32[]{:S(2)}, u32[]{:S(2)}) %collective-permute-start.4) | collective-permute-done | bytes 524320 | tf_op jit(solution)/shard_map/ppermute | solution.py:36
  228.4 0.8 copy-done.9
  229.2 12.3 %collective-permute-start.1 = (bf16[2,128,1024]{2,1,0:T(8,128)(2,1)}, bf16[2,128,1024]{2,1,0:T(8,128)(2,1)}, u32[]{:S(2)}, u32[]{:S(2)}) collective-permute-start(bf16[2,128,1024]{2,1,0:T(8,128)(2,1)} %get-tuple-element.27), channel_id=1, source_target_pairs={{0,64},{32,96},{64,0},{96,32},{128,192},{160,224},{192,128},{224,1... | collective-permute-start | bytes 1572872 | tf_op jit(solution)/shard_map/ppermute | solution.py:36
  241.6 1.8 fusion.28
  243.4 0.8 fusion.34
  244.2 4.5 %collective-permute-start.7 = (bf16[128,1024]{1,0:T(8,128)(2,1)}, bf16[128,1024]{1,0:T(8,128)(2,1)S(1)}, u32[]{:S(2)}, u32[]{:S(2)}) collective-permute-start(bf16[128,1024]{1,0:T(8,128)(2,1)} %fusion.34), channel_id=1, source_target_pairs={{0,128},{32,160},{64,192},{96,224},{128,0},{160,32},{192,64},{224,... | collective-permute-start | bytes 786440 | tf_op jit(solution)/shard_map/ppermute | solution.py:41
  248.7 0.8 collective-permute-done
  249.5 1.2 collective-permute-done.2
  250.7 11.1 %collective-permute-done.1 = bf16[2,128,1024]{2,1,0:T(8,128)(2,1)} collective-permute-done((bf16[2,128,1024]{2,1,0:T(8,128)(2,1)}, bf16[2,128,1024]{2,1,0:T(8,128)(2,1)}, u32[]{:S(2)}, u32[]{:S(2)}) %collective-permute-start.1) | collective-permute-done | bytes 524320 | tf_op jit(solution)/shard_map/ppermute | solution.py:36
  261.7 1.8 fusion.30
  263.6 1.0 copy-done.5
  264.6 0.7 fusion.33
  265.3 4.5 %collective-permute-start.3 = (bf16[128,1024]{1,0:T(8,128)(2,1)}, bf16[128,1024]{1,0:T(8,128)(2,1)}, u32[]{:S(2)}, u32[]{:S(2)}) collective-permute-start(bf16[128,1024]{1,0:T(8,128)(2,1)} %fusion.33), channel_id=1, source_target_pairs={{0,128},{32,160},{64,192},{96,224},{128,0},{160,32},{192,64},{224,... | collective-permute-start | bytes 786440 | tf_op jit(solution)/shard_map/ppermute | solution.py:41
  269.8 0.9 fusion.31
  270.7 6.5 %collective-permute-done.3 = bf16[128,1024]{1,0:T(8,128)(2,1)} collective-permute-done((bf16[128,1024]{1,0:T(8,128)(2,1)}, bf16[128,1024]{1,0:T(8,128)(2,1)}, u32[]{:S(2)}, u32[]{:S(2)}) %collective-permute-start.3) | collective-permute-done | bytes 262176 | tf_op jit(solution)/shard_map/ppermute | solution.py:41
  277.2 2.0 fusion.32
  279.2 2.5 bitcast_convert_fusion
  281.6 5.3 %copy.39 = f32[1,1024,1024]{1,2,0:T(8,128)} copy(f32[1,1024,1024]{2,1,0:T(8,128)} %bitcast.112) | data formatting | bytes 8388608 | tf_op jit(solution)/shard_map/convert_element_type | solution.py:92
  287.0 8.0 %fusion.3 = bf16[1,1024,1024]{1,2,0:T(8,128)(2,1)} fusion(f32[1,1024,1024]{1,2,0:T(8,128)} %copy.39, bf16[1,1024,1024]{1,2,0:T(8,128)(2,1)} %copy.31, bf16[1024,1024]{1,0:T(8,128)(2,1)} %bitcast.15, bf16[1,1024,1024]{2,1,0:T(8,128)(2,1)} %param.6), kind=kOutput, calls=%fused_computation.6 | convolution fusion | flops 2151677952 | bytes 12582912 | tf_op jit(solution)/shard_map/kj,skc->sjc/dot_general | solution.py:91
  295.0 2.2 fusion
  297.2 4.1 %copy.43 = bf16[1,1024,1024]{2,1,0:T(8,128)(2,1)} copy(bf16[1,1024,1024]{1,2,0:T(8,128)(2,1)} %fusion) | data formatting | bytes 4194304
  301.3 3.9 %copy.44 = bf16[1,1024,1024]{2,1,0:T(8,128)(2,1)} copy(bf16[1,1024,1024]{1,2,0:T(8,128)(2,1)} %fusion.3) | data formatting | bytes 4194304
  (23 shorter events, 0.2 us)
Async XLA Ops:
  0.6 128.2 %copy-start = (bf16[1,1024,1024]{2,1,0:T(8,128)(2,1)S(1)}, bf16[1,1024,1024]{2,1,0:T(8,128)(2,1)}, u32[]{:S(2)}) copy-start(bf16[1,1024,1024]{2,1,0:T(8,128)(2,1)} %param.7) | copy-start | bytes 6291460
  17.1 4.7 %copy-start.4 = (bf16[1,1024,1024]{2,1,0:T(8,128)(2,1)S(1)}, bf16[1,1024,1024]{2,1,0:T(8,128)(2,1)}, u32[]{:S(2)}) copy-start(bf16[1,1024,1024]{2,1,0:T(8,128)(2,1)} %copy.32) | copy-start | bytes 6291460
  128.8 2.5 copy-start.8
  133.8 55.3 %all-to-all-start.1 = ((bf16[1,1,32,32,1024]{4,2,1,0,3:T(8,128)(2,1)}), bf16[1,1,32,32,1024]{4,2,1,0,3:T(8,128)(2,1)}, u32[]{:S(2)}, u32[]{:S(2)}) async-start(bf16[1,1,32,32,1024]{4,2,1,0,3:T(8,128)(2,1)} %copy.35), calls=%async_computation.1 | async-start | bytes 4194304 | tf_op jit(solution)/shard_map/all_to_all | solution.py:55
  200.3 78.9 %all-to-all-start.2 = ((bf16[1,1,32,32,1024]{4,2,1,0,3:T(8,128)(2,1)}), bf16[1,1,32,32,1024]{4,2,1,0,3:T(8,128)(2,1)S(1)}, u32[]{:S(2)}, u32[]{:S(2)}) async-start(bf16[1,1,32,32,1024]{4,2,1,0,3:T(8,128)(2,1)} %copy.37), calls=%async_computation.2 | async-start | bytes 4194304 | tf_op jit(solution)/shard_map/all_to_all | solution.py:55
  211.5 6.5 %copy-start.7 = (bf16[1024,1024]{1,0:T(8,128)(2,1)}, bf16[1024,1024]{1,0:T(8,128)(2,1)S(1)}, u32[]{:S(2)}) copy-start(bf16[1024,1024]{1,0:T(8,128)(2,1)S(1)} %convolution_convert_fusion) | copy-start | bytes 6291460
  211.5 5.3 %copy-start.6 = (bf16[1024,1024]{1,0:T(8,128)(2,1)S(1)}, bf16[1024,1024]{1,0:T(8,128)(2,1)}, u32[]{:S(2)}) copy-start(bf16[1024,1024]{1,0:T(8,128)(2,1)} %fusion.14) | copy-start | bytes 6291460
  211.7 16.8 %collective-permute-start.4 = (bf16[2,128,1024]{2,1,0:T(8,128)(2,1)S(1)}, bf16[2,128,1024]{2,1,0:T(8,128)(2,1)S(1)}, u32[]{:S(2)}, u32[]{:S(2)}) collective-permute-start(bf16[2,128,1024]{2,1,0:T(8,128)(2,1)S(1)} %get-tuple-element.22), channel_id=1, source_target_pairs={{0,32},{32,64},{64,96},{96,0},{128,160},{160,192},{192,224},{224,1... | collective-permute-start | bytes 1572872 | tf_op jit(solution)/shard_map/ppermute | solution.py:36
  213.2 28.3 %collective-permute-start.6 = (bf16[2,128,1024]{2,1,0:T(8,128)(2,1)S(1)}, bf16[2,128,1024]{2,1,0:T(8,128)(2,1)}, u32[]{:S(2)}, u32[]{:S(2)}) collective-permute-start(bf16[2,128,1024]{2,1,0:T(8,128)(2,1)S(1)} %get-tuple-element.23), channel_id=1, source_target_pairs={{0,96},{32,0},{64,32},{96,64},{128,224},{160,128},{192,160},{224,1... | collective-permute-start | bytes 1572872 | tf_op jit(solution)/shard_map/ppermute | solution.py:36
  215.0 26.6 %collective-permute-start.5 = (bf16[2,128,1024]{2,1,0:T(8,128)(2,1)S(1)}, bf16[2,128,1024]{2,1,0:T(8,128)(2,1)}, u32[]{:S(2)}, u32[]{:S(2)}) collective-permute-start(bf16[2,128,1024]{2,1,0:T(8,128)(2,1)S(1)} %get-tuple-element.24), channel_id=1, source_target_pairs={{0,64},{32,96},{64,0},{96,32},{128,192},{160,224},{192,128},{224,1... | collective-permute-start | bytes 1572872 | tf_op jit(solution)/shard_map/ppermute | solution.py:36
  218.0 31.5 %collective-permute-start = (bf16[2,128,1024]{2,1,0:T(8,128)(2,1)}, bf16[2,128,1024]{2,1,0:T(8,128)(2,1)}, u32[]{:S(2)}, u32[]{:S(2)}) collective-permute-start(bf16[2,128,1024]{2,1,0:T(8,128)(2,1)} %get-tuple-element.25), channel_id=1, source_target_pairs={{0,32},{32,64},{64,96},{96,0},{128,160},{160,192},{192,224},{224,1... | collective-permute-start | bytes 1572872 | tf_op jit(solution)/shard_map/ppermute | solution.py:36
  218.6 32.1 %collective-permute-start.2 = (bf16[2,128,1024]{2,1,0:T(8,128)(2,1)}, bf16[2,128,1024]{2,1,0:T(8,128)(2,1)}, u32[]{:S(2)}, u32[]{:S(2)}) collective-permute-start(bf16[2,128,1024]{2,1,0:T(8,128)(2,1)} %get-tuple-element.26), channel_id=1, source_target_pairs={{0,96},{32,0},{64,32},{96,64},{128,224},{160,128},{192,160},{224,1... | collective-permute-start | bytes 1572872 | tf_op jit(solution)/shard_map/ppermute | solution.py:36
  228.4 0.8 copy-start.9
  229.2 32.5 %collective-permute-start.1 = (bf16[2,128,1024]{2,1,0:T(8,128)(2,1)}, bf16[2,128,1024]{2,1,0:T(8,128)(2,1)}, u32[]{:S(2)}, u32[]{:S(2)}) collective-permute-start(bf16[2,128,1024]{2,1,0:T(8,128)(2,1)} %get-tuple-element.27), channel_id=1, source_target_pairs={{0,64},{32,96},{64,0},{96,32},{128,192},{160,224},{192,128},{224,1... | collective-permute-start | bytes 1572872 | tf_op jit(solution)/shard_map/ppermute | solution.py:36
  244.2 25.6 %collective-permute-start.7 = (bf16[128,1024]{1,0:T(8,128)(2,1)}, bf16[128,1024]{1,0:T(8,128)(2,1)S(1)}, u32[]{:S(2)}, u32[]{:S(2)}) collective-permute-start(bf16[128,1024]{1,0:T(8,128)(2,1)} %fusion.34), channel_id=1, source_target_pairs={{0,128},{32,160},{64,192},{96,224},{128,0},{160,32},{192,64},{224,... | collective-permute-start | bytes 786440 | tf_op jit(solution)/shard_map/ppermute | solution.py:41
  263.6 1.0 copy-start.5
  265.3 11.8 %collective-permute-start.3 = (bf16[128,1024]{1,0:T(8,128)(2,1)}, bf16[128,1024]{1,0:T(8,128)(2,1)}, u32[]{:S(2)}, u32[]{:S(2)}) collective-permute-start(bf16[128,1024]{1,0:T(8,128)(2,1)} %fusion.33), channel_id=1, source_target_pairs={{0,128},{32,160},{64,192},{96,224},{128,0},{160,32},{192,64},{224,... | collective-permute-start | bytes 786440 | tf_op jit(solution)/shard_map/ppermute | solution.py:41
  287.0 8.0 %copy-start.2 = (bf16[1,1024,1024]{1,2,0:T(8,128)(2,1)S(1)}, bf16[1,1024,1024]{1,2,0:T(8,128)(2,1)}, u32[]{:S(2)}) copy-start(bf16[1,1024,1024]{1,2,0:T(8,128)(2,1)} %copy.30) | copy-start | bytes 6291460
  287.0 8.0 %copy-start.3 = (f32[1,1024,1024]{1,2,0:T(8,128)S(1)}, f32[1,1024,1024]{1,2,0:T(8,128)}, u32[]{:S(2)}) copy-start(f32[1,1024,1024]{1,2,0:T(8,128)} %copy.39) | copy-start | bytes 12582916
  297.2 8.0 %copy-start.1 = (bf16[1,1024,1024]{2,1,0:T(8,128)(2,1)S(1)}, bf16[1,1024,1024]{2,1,0:T(8,128)(2,1)}, u32[]{:S(2)}) copy-start(bf16[1,1024,1024]{2,1,0:T(8,128)(2,1)} %param.7) | copy-start | bytes 6291460

commit v3 on v2

--- a/solution.py
+++ b/solution.py
@@ -3,6 +3,11 @@
 import jax.numpy as jnp
 from jax import lax
 from jax.sharding import PartitionSpec as P
+from jax.experimental.layout import Layout, with_layout_constraint
+
+
+def _rowmajor(x):
+    return with_layout_constraint(x, Layout(tuple(range(x.ndim))))
 
 
 def _dp_rings(mesh):
@@ -66,7 +71,7 @@
     ftwo = factor_two[0]
     xfull = inputs.astype(jnp.float32)
     dyfull = cotangent.astype(jnp.float32)
-    gated = (dyfull * xfull).astype(jnp.bfloat16)
+    gated = _rowmajor((dyfull * xfull).astype(jnp.bfloat16))
     first = jnp.einsum("kj,sjc->skc", fone, inputs, preferred_element_type=jnp.float32).astype(
         jnp.bfloat16
     )
@@ -88,10 +93,11 @@
     part_one, second = lax.optimization_barrier((part_one.astype(jnp.bfloat16), second))
     grad_one = _dp_reduce(part_one, ring)
     monarch = _from_moved(second, count, rows)
-    spread = jnp.einsum("kj,skc->sjc", fone, back_moved, preferred_element_type=jnp.float32)
+    spread = _rowmajor(jnp.einsum("kj,skc->sjc", fone, back_moved, preferred_element_type=jnp.float32))
+    spread = lax.optimization_barrier(spread)
     mfull = monarch.astype(jnp.float32)
-    mixed = (xfull * mfull).astype(jnp.bfloat16)
-    grad_input = (dyfull * mfull + spread).astype(jnp.bfloat16)
+    mixed = _rowmajor((xfull * mfull).astype(jnp.bfloat16))
+    grad_input = _rowmajor((dyfull * mfull + spread).astype(jnp.bfloat16))
     return (mixed, grad_input, grad_one[None], grad_two[None])
 
 

time: 311 us -> 279 us (0.90)
  local copies, waits for them, and re-layouts: 42.6 us -> 15.6 us
  waiting for transfers between devices: 69.4 us -> 81.4 us
  starting transfers between devices: 43.6 us -> 31.9 us
  matrix products: 31 us -> 26.6 us
    unnamed x24 -> x14, local copies, waits for them, and re-layouts: 17.9 us -> 0.28 us
    ppermute x6, starting transfers between devices: 20.7 us -> 8.43 us  [_dp_reduce(): acc = acc + lax.ppermute(piece, 'dp', perm).astype(jnp.float32)]
    ppermute x6, waiting for transfers between devices: 20.3 us -> 31.9 us  [_dp_reduce(): acc = acc + lax.ppermute(piece, 'dp', perm).astype(jnp.float32)]
    convert_element_type x2 -> x0, local copies, waits for them, and re-layouts: 9.27 us -> none  [the longest x1 5.34 us: local(): mfull = monarch.astype(jnp.float32)]
    convert_element_type x3 -> x2, other arithmetic: 9.2 us -> 11.3 us  [the longest x1 7.96 us: local(): grad_input = _rowmajor((dyfull * mfull + spread).astype(jnp.bfloat16))]
  transfers between devices with their start and end apart: 10 -> 10, of which waited for: 6 -> 6; matrix products, arithmetic and copies ran while one was open for 6% -> 9% of each run, Pallas kernels for 0% -> 0%
where the time goes in v3:
time: 279 us; the launch traced here: 275 us
  blocking collectives  102 us (37%)
  waiting for transfers between devices  81.4 us (29%)
  starting transfers between devices  31.9 us (11%)
  matrix products  26.6 us (10%)
  other arithmetic  17 us (6%)
  local copies, waits for them, and re-layouts  15.6 us (6%)
    all_to_all x1, blocking collectives, local(): in1 = lax.all_to_all(out1, 'seq', split_axis=1, concat_axis=3, tiled=True)  102 us
    all_to_all x2, waiting for transfers between devices, _from_moved(): lax.all_to_all(data.reshape(seqs, 1, rows, count, width), 'seq', split_ax...  42.6 us
    ppermute x6, waiting for transfers between devices, _dp_reduce(): acc = acc + lax.ppermute(piece, 'dp', perm).astype(jnp.float32)  31.9 us
    all_to_all x2, starting transfers between devices, _from_moved(): lax.all_to_all(data.reshape(seqs, 1, rows, count, width), 'seq', split_ax...  14.4 us
    ppermute x2, starting transfers between devices, _dp_reduce(): lax.ppermute(piece.astype(jnp.bfloat16), 'dp', perm).astype(jnp.float32)  9.06 us
    ppermute x6, starting transfers between devices, _dp_reduce(): acc = acc + lax.ppermute(piece, 'dp', perm).astype(jnp.float32)  8.43 us
    convert_element_type x1, other arithmetic, local(): grad_input = _rowmajor((dyfull * mfull + spread).astype(jnp.bfloat16))  7.96 us
    ppermute x2, waiting for transfers between devices, _dp_reduce(): lax.ppermute(piece.astype(jnp.bfloat16), 'dp', perm).astype(jnp.float32)  6.9 us
  transfers between devices with their start and end apart: 10, of which 6 were waited for; matrix products, arithmetic and copies ran while one was open for 9% of the time, Pallas kernels for 0%

profile of v3, /device:TPU:8, one launch (start us, length us, event | category | flops | bytes accessed | tf_op | source)
XLA Modules:
  0.0 274.9 jit_solution(17289650747439045229)
XLA Ops:
  0.6 0.0 copy-start
  0.6 0.0 copy-start.2
  0.7 0.0 copy-start.5
  0.7 3.4 %fusion.1 = bf16[1,1024,1024]{2,1,0:T(8,128)(2,1)S(1)} fusion(bf16[1,1024,1024]{2,1,0:T(8,128)(2,1)} %param.4, bf16[1,1024,1024]{2,1,0:T(8,128)(2,1)} %param.5), kind=kLoop, calls=%fused_computation.4 | loop fusion | flops 4194304 | bytes 6291456 | tf_op jit(solution)/shard_map/convert_element_type | solution.py:74
  4.0 0.0 copy-done.2
  4.0 0.2 copy-done.5
  4.3 2.3 fusion.17
  6.6 0.4 pad_maximum_fusion
  7.0 101.7 %all_to_all.39 = bf16[2,32,32,1,1024]{4,2,0,3,1:T(8,128)(2,1)S(1)} all-to-all(bf16[2,32,32,1,1024]{4,2,0,3,1:T(8,128)(2,1)S(1)} %pad_maximum_fusion), channel_id=1, replica_groups=mesh['dp'=8,'seq'=32] {'seq'}, dimensions={1} | all-to-all | bytes 8388608 | tf_op jit(solution)/shard_map/all_to_all | solution.py:79
  108.7 2.3 copy.29
  111.0 1.8 fusion.35
  112.8 2.5 fusion.22
  115.3 2.5 copy.21
  117.7 7.2 %all-to-all-start.1 = ((bf16[1,1,32,32,1024]{4,2,1,0,3:T(8,128)(2,1)}), bf16[1,1,32,32,1024]{4,2,1,0,3:T(8,128)(2,1)}, u32[]{:S(2)}, u32[]{:S(2)}) async-start(bf16[1,1,32,32,1024]{4,2,1,0,3:T(8,128)(2,1)} %copy.21), calls=%async_computation.1 | async-start | bytes 4194304 | tf_op jit(solution)/shard_map/all_to_all | solution.py:60
  124.9 5.3 %convert_bitcast_fusion = bf16[1,1024,1024]{1,2,0:T(8,128)(2,1)} fusion(bf16[1024,1024]{1,0:T(8,128)(2,1)} %bitcast.124, bf16[1,1024,1024]{2,1,0:T(8,128)(2,1)S(1)} %copy-done), kind=kOutput, calls=%fused_computation.20 | convolution fusion | flops 2148532224 | bytes 6291456 | tf_op jit(solution)/shard_map/pq,sqc->spc/dot_general | solution.py:87
  130.3 42.6 %all-to-all-done.1 = bf16[1,1,32,32,1024]{4,2,1,0,3:T(8,128)(2,1)} async-done(((bf16[1,1,32,32,1024]{4,2,1,0,3:T(8,128)(2,1)}), bf16[1,1,32,32,1024]{4,2,1,0,3:T(8,128)(2,1)}, u32[]{:S(2)}, u32[]{:S(2)}) %all-to-all-start.1) | async-done | bytes 2097184 | tf_op jit(solution)/shard_map/all_to_all | solution.py:60
  172.8 5.9 %fusion.14 = bf16[1024,1024]{1,0:T(8,128)(2,1)} fusion(bf16[1024,1024]{1,0:T(8,128)(2,1)} %bitcast.17, bf16[1,1024,1024]{2,1,0:T(8,128)(2,1)} %param.4), kind=kOutput, calls=%fused_computation.21 | convolution fusion | flops 2148532224 | bytes 6291456 | tf_op jit(solution)/shard_map/skc,sjc->kj/dot_general | solution.py:92
  178.8 2.9 %copy.22 = bf16[1,1024,1024]{2,1,0:T(8,128)(2,1)S(1)} copy(bf16[1,1024,1024]{1,2,0:T(8,128)(2,1)} %convert_bitcast_fusion) | data formatting | bytes 4194304 | tf_op jit(solution)/shard_map/optimization_barrier | solution.py:93
  181.6 2.5 copy.23
  184.1 7.2 %all-to-all-start.2 = ((bf16[1,1,32,32,1024]{4,2,1,0,3:T(8,128)(2,1)}), bf16[1,1,32,32,1024]{4,2,1,0,3:T(8,128)(2,1)}, u32[]{:S(2)}, u32[]{:S(2)}) async-start(bf16[1,1,32,32,1024]{4,2,1,0,3:T(8,128)(2,1)} %copy.23), calls=%async_computation.2 | async-start | bytes 4194304 | tf_op jit(solution)/shard_map/all_to_all | solution.py:60
  191.4 4.6 %convolution_convert_fusion = bf16[1024,1024]{1,0:T(8,128)(2,1)S(1)} fusion(bf16[1024,1024]{1,0:T(8,128)(2,1)} %bitcast.127, bf16[1024,1024]{1,0:T(8,128)(2,1)} %bitcast.125), kind=kOutput, calls=%fused_computation.24 | convolution fusion | flops 2148532224 | bytes 6291456 | tf_op jit(solution)/shard_map/spc,sqc->pq/dot_general | solution.py:90
  196.0 0.0 copy-start.3
  196.0 1.1 dynamic-slice_bitcast_fusion.2
  197.1 1.5 collective-permute-start.4
  198.6 1.8 collective-permute-start.6
  200.3 1.8 collective-permute-start.5
  202.1 10.4 %collective-permute-done.4 = bf16[2,128,1024]{2,1,0:T(8,128)(2,1)} collective-permute-done((bf16[2,128,1024]{2,1,0:T(8,128)(2,1)}, bf16[2,128,1024]{2,1,0:T(8,128)(2,1)}, u32[]{:S(2)}, u32[]{:S(2)}) %collective-permute-start.4) | collective-permute-done | bytes 524320 | tf_op jit(solution)/shard_map/ppermute | solution.py:41
  212.6 10.2 %collective-permute-done.6 = bf16[2,128,1024]{2,1,0:T(8,128)(2,1)} collective-permute-done((bf16[2,128,1024]{2,1,0:T(8,128)(2,1)S(1)}, bf16[2,128,1024]{2,1,0:T(8,128)(2,1)}, u32[]{:S(2)}, u32[]{:S(2)}) %collective-permute-start.6) | collective-permute-done | bytes 524320 | tf_op jit(solution)/shard_map/ppermute | solution.py:41
  222.8 2.0 collective-permute-done.5
  224.8 1.9 fusion.28
  226.6 1.6 dynamic-slice_bitcast_fusion.5
  228.2 1.0 collective-permute-start
  229.2 2.3 collective-permute-start.2
  231.5 0.1 collective-permute-start.1
  231.6 0.7 fusion.34
  232.3 4.5 %collective-permute-start.7 = (bf16[128,1024]{1,0:T(8,128)(2,1)}, bf16[128,1024]{1,0:T(8,128)(2,1)S(1)}, u32[]{:S(2)}, u32[]{:S(2)}) collective-permute-start(bf16[128,1024]{1,0:T(8,128)(2,1)} %fusion.34), channel_id=1, source_target_pairs={{0,128},{32,160},{64,192},{96,224},{128,0},{160,32},{192,64},{224,... | collective-permute-start | bytes 786440 | tf_op jit(solution)/shard_map/ppermute | solution.py:46
  236.8 6.9 %collective-permute-done.7 = bf16[128,1024]{1,0:T(8,128)(2,1)S(1)} collective-permute-done((bf16[128,1024]{1,0:T(8,128)(2,1)}, bf16[128,1024]{1,0:T(8,128)(2,1)S(1)}, u32[]{:S(2)}, u32[]{:S(2)}) %collective-permute-start.7) | collective-permute-done | bytes 262176 | tf_op jit(solution)/shard_map/ppermute | solution.py:46
  243.7 0.9 fusion.31
  244.6 9.2 %collective-permute-done = bf16[2,128,1024]{2,1,0:T(8,128)(2,1)S(1)} collective-permute-done((bf16[2,128,1024]{2,1,0:T(8,128)(2,1)S(1)}, bf16[2,128,1024]{2,1,0:T(8,128)(2,1)S(1)}, u32[]{:S(2)}, u32[]{:S(2)}) %collective-permute-start) | collective-permute-done | bytes 524320 | tf_op jit(solution)/shard_map/ppermute | solution.py:41
  253.8 0.0 collective-permute-done.2
  253.8 0.0 collective-permute-done.1
  253.8 1.7 fusion.30
  255.6 4.6 %collective-permute-start.3 = (bf16[128,1024]{1,0:T(8,128)(2,1)S(1)}, bf16[128,1024]{1,0:T(8,128)(2,1)S(1)}, u32[]{:S(2)}, u32[]{:S(2)}) collective-permute-start(bf16[128,1024]{1,0:T(8,128)(2,1)S(1)} %fusion.33), channel_id=1, source_target_pairs={{0,128},{32,160},{64,192},{96,224},{128,0},{160,32},{192,64},{224,... | collective-permute-start | bytes 786440 | tf_op jit(solution)/shard_map/ppermute | solution.py:46
  260.2 6.0 %convolution_bitcast_fusion = f32[1,1024,1024]{2,1,0:T(8,128)} fusion(bf16[1024,1024]{1,0:T(8,128)(2,1)} %bitcast.17, bf16[1,1024,1024]{2,1,0:T(8,128)(2,1)S(1)} %copy-done.6), kind=kOutput, calls=%fused_computation.9 | convolution fusion | flops 2147483648 | bytes 8388608 | tf_op jit(solution)/shard_map/kj,skc->sjc/dot_general | solution.py:96
  266.1 0.0 collective-permute-done.3
  266.1 0.9 fusion.32
  267.0 0.0 all-to-all-done.2
  267.0 8.0 %fusion.3 = (bf16[1,1024,1024]{2,1,0:T(8,128)(2,1)}, bf16[1,1024,1024]{2,1,0:T(8,128)(2,1)}) fusion(f32[1,1024,1024]{2,1,0:T(8,128)} %convolution_bitcast_fusion, bf16[1,1024,1024]{2,1,0:T(8,128)(2,1)} %param.5, bf16[1,1,32,32,1024]{4,2,1,0,3:T(8,128)(2,1)} %all-to-all-done.2, bf16[1,1024,1024]{2,1,0:T(8,128)(2,1)} %param.4), kind=kLoop, calls=%fused_computation.6 | loop fusion | flops 8388608 | bytes 14680064 | tf_op jit(solution)/shard_map/convert_element_type | solution.py:100
  (9 shorter events, 0.1 us)
Async XLA Ops:
  0.6 112.2 %copy-start = (bf16[1,1024,1024]{2,1,0:T(8,128)(2,1)S(1)}, bf16[1,1024,1024]{2,1,0:T(8,128)(2,1)}, u32[]{:S(2)}) copy-start(bf16[1,1024,1024]{2,1,0:T(8,128)(2,1)} %param.7) | copy-start | bytes 6291460
  0.6 3.4 %copy-start.2 = (bf16[1,1024,1024]{2,1,0:T(8,128)(2,1)S(1)}, bf16[1,1024,1024]{2,1,0:T(8,128)(2,1)}, u32[]{:S(2)}) copy-start(bf16[1,1024,1024]{2,1,0:T(8,128)(2,1)} %param.4) | copy-start | bytes 6291460
  0.7 3.6 %copy-start.5 = (bf16[1,1024,1024]{2,1,0:T(8,128)(2,1)S(1)}, bf16[1,1024,1024]{2,1,0:T(8,128)(2,1)}, u32[]{:S(2)}) copy-start(bf16[1,1024,1024]{2,1,0:T(8,128)(2,1)} %param.6) | copy-start | bytes 6291460
  112.8 2.5 copy-start.4
  117.7 55.1 %all-to-all-start.1 = ((bf16[1,1,32,32,1024]{4,2,1,0,3:T(8,128)(2,1)}), bf16[1,1,32,32,1024]{4,2,1,0,3:T(8,128)(2,1)}, u32[]{:S(2)}, u32[]{:S(2)}) async-start(bf16[1,1,32,32,1024]{4,2,1,0,3:T(8,128)(2,1)} %copy.21), calls=%async_computation.1 | async-start | bytes 4194304 | tf_op jit(solution)/shard_map/all_to_all | solution.py:60
  184.1 82.9 %all-to-all-start.2 = ((bf16[1,1,32,32,1024]{4,2,1,0,3:T(8,128)(2,1)}), bf16[1,1,32,32,1024]{4,2,1,0,3:T(8,128)(2,1)}, u32[]{:S(2)}, u32[]{:S(2)}) async-start(bf16[1,1,32,32,1024]{4,2,1,0,3:T(8,128)(2,1)} %copy.23), calls=%async_computation.2 | async-start | bytes 4194304 | tf_op jit(solution)/shard_map/all_to_all | solution.py:60
  196.0 26.8 %copy-start.3 = (bf16[1024,1024]{1,0:T(8,128)(2,1)}, bf16[1024,1024]{1,0:T(8,128)(2,1)S(1)}, u32[]{:S(2)}) copy-start(bf16[1024,1024]{1,0:T(8,128)(2,1)S(1)} %convolution_convert_fusion) | copy-start | bytes 6291460
  197.1 15.5 %collective-permute-start.4 = (bf16[2,128,1024]{2,1,0:T(8,128)(2,1)}, bf16[2,128,1024]{2,1,0:T(8,128)(2,1)}, u32[]{:S(2)}, u32[]{:S(2)}) collective-permute-start(bf16[2,128,1024]{2,1,0:T(8,128)(2,1)} %get-tuple-element.10), channel_id=1, source_target_pairs={{0,32},{32,64},{64,96},{96,0},{128,160},{160,192},{192,224},{224,1... | collective-permute-start | bytes 1572872 | tf_op jit(solution)/shard_map/ppermute | solution.py:41
  198.6 24.2 %collective-permute-start.6 = (bf16[2,128,1024]{2,1,0:T(8,128)(2,1)S(1)}, bf16[2,128,1024]{2,1,0:T(8,128)(2,1)}, u32[]{:S(2)}, u32[]{:S(2)}) collective-permute-start(bf16[2,128,1024]{2,1,0:T(8,128)(2,1)S(1)} %get-tuple-element.11), channel_id=1, source_target_pairs={{0,96},{32,0},{64,32},{96,64},{128,224},{160,128},{192,160},{224,1... | collective-permute-start | bytes 1572872 | tf_op jit(solution)/shard_map/ppermute | solution.py:41
  200.3 24.5 %collective-permute-start.5 = (bf16[2,128,1024]{2,1,0:T(8,128)(2,1)S(1)}, bf16[2,128,1024]{2,1,0:T(8,128)(2,1)}, u32[]{:S(2)}, u32[]{:S(2)}) collective-permute-start(bf16[2,128,1024]{2,1,0:T(8,128)(2,1)S(1)} %get-tuple-element.12), channel_id=1, source_target_pairs={{0,64},{32,96},{64,0},{96,32},{128,192},{160,224},{192,128},{224,1... | collective-permute-start | bytes 1572872 | tf_op jit(solution)/shard_map/ppermute | solution.py:41
  228.2 25.6 %collective-permute-start = (bf16[2,128,1024]{2,1,0:T(8,128)(2,1)S(1)}, bf16[2,128,1024]{2,1,0:T(8,128)(2,1)S(1)}, u32[]{:S(2)}, u32[]{:S(2)}) collective-permute-start(bf16[2,128,1024]{2,1,0:T(8,128)(2,1)S(1)} %get-tuple-element.13), channel_id=1, source_target_pairs={{0,32},{32,64},{64,96},{96,0},{128,160},{160,192},{192,224},{224,1... | collective-permute-start | bytes 1572872 | tf_op jit(solution)/shard_map/ppermute | solution.py:41
  229.2 24.6 %collective-permute-start.2 = (bf16[2,128,1024]{2,1,0:T(8,128)(2,1)S(1)}, bf16[2,128,1024]{2,1,0:T(8,128)(2,1)}, u32[]{:S(2)}, u32[]{:S(2)}) collective-permute-start(bf16[2,128,1024]{2,1,0:T(8,128)(2,1)S(1)} %get-tuple-element.14), channel_id=1, source_target_pairs={{0,96},{32,0},{64,32},{96,64},{128,224},{160,128},{192,160},{224,1... | collective-permute-start | bytes 1572872 | tf_op jit(solution)/shard_map/ppermute | solution.py:41
  231.5 22.3 %collective-permute-start.1 = (bf16[2,128,1024]{2,1,0:T(8,128)(2,1)S(1)}, bf16[2,128,1024]{2,1,0:T(8,128)(2,1)}, u32[]{:S(2)}, u32[]{:S(2)}) collective-permute-start(bf16[2,128,1024]{2,1,0:T(8,128)(2,1)S(1)} %get-tuple-element.15), channel_id=1, source_target_pairs={{0,64},{32,96},{64,0},{96,32},{128,192},{160,224},{192,128},{224,1... | collective-permute-start | bytes 1572872 | tf_op jit(solution)/shard_map/ppermute | solution.py:41
  232.3 11.4 %collective-permute-start.7 = (bf16[128,1024]{1,0:T(8,128)(2,1)}, bf16[128,1024]{1,0:T(8,128)(2,1)S(1)}, u32[]{:S(2)}, u32[]{:S(2)}) collective-permute-start(bf16[128,1024]{1,0:T(8,128)(2,1)} %fusion.34), channel_id=1, source_target_pairs={{0,128},{32,160},{64,192},{96,224},{128,0},{160,32},{192,64},{224,... | collective-permute-start | bytes 786440 | tf_op jit(solution)/shard_map/ppermute | solution.py:46
  244.6 15.6 %copy-start.6 = (bf16[1,1024,1024]{2,1,0:T(8,128)(2,1)S(1)}, bf16[1,1024,1024]{2,1,0:T(8,128)(2,1)}, u32[]{:S(2)}) copy-start(bf16[1,1024,1024]{2,1,0:T(8,128)(2,1)} %param.6) | copy-start | bytes 6291460
  255.6 10.5 %collective-permute-start.3 = (bf16[128,1024]{1,0:T(8,128)(2,1)S(1)}, bf16[128,1024]{1,0:T(8,128)(2,1)S(1)}, u32[]{:S(2)}, u32[]{:S(2)}) collective-permute-start(bf16[128,1024]{1,0:T(8,128)(2,1)S(1)} %fusion.33), channel_id=1, source_target_pairs={{0,128},{32,160},{64,192},{96,224},{128,0},{160,32},{192,64},{224,... | collective-permute-start | bytes 786440 | tf_op jit(solution)/shard_map/ppermute | solution.py:46
  267.0 8.0 %copy-start.1 = (bf16[1,1024,1024]{2,1,0:T(8,128)(2,1)S(1)}, bf16[1,1024,1024]{2,1,0:T(8,128)(2,1)}, u32[]{:S(2)}) copy-start(bf16[1,1024,1024]{2,1,0:T(8,128)(2,1)} %param.7) | copy-start | bytes 6291460

commit v4 on v3

--- a/solution.py
+++ b/solution.py
@@ -90,7 +90,9 @@
     part_two = jnp.einsum("spc,sqc->pq", gated_moved, moved, preferred_element_type=jnp.float32)
     grad_two = _dp_reduce(part_two.astype(jnp.bfloat16), ring)
     part_one = jnp.einsum("skc,sjc->kj", back_moved, inputs, preferred_element_type=jnp.float32)
-    part_one, second = lax.optimization_barrier((part_one.astype(jnp.bfloat16), second))
+    part_one, second, grad_two = lax.optimization_barrier(
+        (part_one.astype(jnp.bfloat16), second, grad_two)
+    )
     grad_one = _dp_reduce(part_one, ring)
     monarch = _from_moved(second, count, rows)
     spread = _rowmajor(jnp.einsum("kj,skc->sjc", fone, back_moved, preferred_element_type=jnp.float32))

time: 279 us -> 273 us (0.978)
  waiting for transfers between devices: 81.4 us -> 76.9 us
    all_to_all x2, waiting for transfers between devices: 42.6 us -> 17.6 us  [_from_moved(): lax.all_to_all(data.reshape(seqs, 1, rows, count, width), 'seq', split_ax...]
    ppermute x6, waiting for transfers between devices: 31.9 us -> 45 us  [_dp_reduce(): acc = acc + lax.ppermute(piece, 'dp', perm).astype(jnp.float32)]
    ppermute x2, waiting for transfers between devices: 6.9 us -> 14.4 us  [_dp_reduce(): lax.ppermute(piece.astype(jnp.bfloat16), 'dp', perm).astype(jnp.float32)]
  transfers between devices with their start and end apart: 10 -> 10, of which waited for: 6 -> 10; matrix products, arithmetic and copies ran while one was open for 9% -> 8% of each run, Pallas kernels for 0% -> 0%
where the time goes in v4:
time: 273 us; the launch traced here: 270 us
  blocking collectives  102 us (37%)
  waiting for transfers between devices  76.9 us (28%)
  starting transfers between devices  34.1 us (12%)
  matrix products  25 us (9%)
  other arithmetic  16.6 us (6%)
  local copies, waits for them, and re-layouts  14.7 us (5%)
    all_to_all x1, blocking collectives, local(): in1 = lax.all_to_all(out1, 'seq', split_axis=1, concat_axis=3, tiled=True)  102 us
    ppermute x6, waiting for transfers between devices, _dp_reduce(): acc = acc + lax.ppermute(piece, 'dp', perm).astype(jnp.float32)  45 us
    all_to_all x2, waiting for transfers between devices, _from_moved(): lax.all_to_all(data.reshape(seqs, 1, rows, count, width), 'seq', split_ax...  17.6 us
    all_to_all x2, starting transfers between devices, _from_moved(): lax.all_to_all(data.reshape(seqs, 1, rows, count, width), 'seq', split_ax...  14.5 us
    ppermute x2, waiting for transfers between devices, _dp_reduce(): lax.ppermute(piece.astype(jnp.bfloat16), 'dp', perm).astype(jnp.float32)  14.4 us
    ppermute x6, starting transfers between devices, _dp_reduce(): acc = acc + lax.ppermute(piece, 'dp', perm).astype(jnp.float32)  10.4 us
    ppermute x2, starting transfers between devices, _dp_reduce(): lax.ppermute(piece.astype(jnp.bfloat16), 'dp', perm).astype(jnp.float32)  9.15 us
    convert_element_type x1, other arithmetic, local(): grad_input = _rowmajor((dyfull * mfull + spread).astype(jnp.bfloat16))  7.96 us
  transfers between devices with their start and end apart: 10, of which 10 were waited for; matrix products, arithmetic and copies ran while one was open for 8% of the time, Pallas kernels for 0%

profile of v4, /device:TPU:8, one launch (start us, length us, event | category | flops | bytes accessed | tf_op | source)
XLA Modules:
  0.0 269.8 jit_solution(1373019060020397775)
XLA Ops:
  0.6 0.0 copy-start
  0.6 0.0 copy-start.2
  0.7 0.0 copy-start.7
  0.7 3.4 %fusion.1 = bf16[1,1024,1024]{2,1,0:T(8,128)(2,1)S(1)} fusion(bf16[1,1024,1024]{2,1,0:T(8,128)(2,1)} %param.4, bf16[1,1024,1024]{2,1,0:T(8,128)(2,1)} %param.5), kind=kLoop, calls=%fused_computation.4 | loop fusion | flops 4194304 | bytes 6291456 | tf_op jit(solution)/shard_map/convert_element_type | solution.py:74
  4.0 0.0 copy-done.2
  4.0 0.2 copy-done.7
  4.3 2.3 fusion.17
  6.6 0.4 pad_maximum_fusion
  7.0 101.7 %all_to_all.39 = bf16[2,32,32,1,1024]{4,2,0,3,1:T(8,128)(2,1)S(1)} all-to-all(bf16[2,32,32,1,1024]{4,2,0,3,1:T(8,128)(2,1)S(1)} %pad_maximum_fusion), channel_id=1, replica_groups=mesh['dp'=8,'seq'=32] {'seq'}, dimensions={1} | all-to-all | bytes 8388608 | tf_op jit(solution)/shard_map/all_to_all | solution.py:79
  108.7 2.3 copy.29
  111.0 1.8 fusion.34
  112.8 2.5 fusion.22
  115.3 2.5 copy.21
  117.7 7.2 %all-to-all-start.1 = ((bf16[1,1,32,32,1024]{4,2,1,0,3:T(8,128)(2,1)}), bf16[1,1,32,32,1024]{4,2,1,0,3:T(8,128)(2,1)}, u32[]{:S(2)}, u32[]{:S(2)}) async-start(bf16[1,1,32,32,1024]{4,2,1,0,3:T(8,128)(2,1)} %copy.21), calls=%async_computation.1 | async-start | bytes 4194304 | tf_op jit(solution)/shard_map/all_to_all | solution.py:60
  125.0 4.6 %convolution_convert_fusion = bf16[1024,1024]{1,0:T(8,128)(2,1)S(1)} fusion(bf16[1024,1024]{1,0:T(8,128)(2,1)} %bitcast.124, bf16[1024,1024]{1,0:T(8,128)(2,1)} %bitcast.121), kind=kOutput, calls=%fused_computation.24 | convolution fusion | flops 2148532224 | bytes 6291456 | tf_op jit(solution)/shard_map/spc,sqc->pq/dot_general | solution.py:90
  129.6 1.3 copy-done.3
  130.9 0.9 dynamic-slice_bitcast_fusion.5
  131.9 1.5 collective-permute-start
  133.4 1.7 collective-permute-start.2
  135.1 1.8 collective-permute-start.1
  136.9 10.4 %collective-permute-done = bf16[2,128,1024]{2,1,0:T(8,128)(2,1)} collective-permute-done((bf16[2,128,1024]{2,1,0:T(8,128)(2,1)}, bf16[2,128,1024]{2,1,0:T(8,128)(2,1)}, u32[]{:S(2)}, u32[]{:S(2)}) %collective-permute-start) | collective-permute-done | bytes 524320 | tf_op jit(solution)/shard_map/ppermute | solution.py:41
  147.3 10.2 %collective-permute-done.2 = bf16[2,128,1024]{2,1,0:T(8,128)(2,1)} collective-permute-done((bf16[2,128,1024]{2,1,0:T(8,128)(2,1)S(1)}, bf16[2,128,1024]{2,1,0:T(8,128)(2,1)}, u32[]{:S(2)}, u32[]{:S(2)}) %collective-permute-start.2) | collective-permute-done | bytes 524320 | tf_op jit(solution)/shard_map/ppermute | solution.py:41
  157.6 2.0 collective-permute-done.1
  159.6 1.8 fusion.30
  161.5 4.6 %collective-permute-start.3 = (bf16[128,1024]{1,0:T(8,128)(2,1)S(1)}, bf16[128,1024]{1,0:T(8,128)(2,1)S(1)}, u32[]{:S(2)}, u32[]{:S(2)}) collective-permute-start(bf16[128,1024]{1,0:T(8,128)(2,1)S(1)} %fusion.32), channel_id=1, source_target_pairs={{0,128},{32,160},{64,192},{96,224},{128,0},{160,32},{192,64},{224,... | collective-permute-start | bytes 786440 | tf_op jit(solution)/shard_map/ppermute | solution.py:46
  166.0 3.7 %convert_bitcast_fusion = bf16[1,1024,1024]{1,2,0:T(8,128)(2,1)} fusion(bf16[1024,1024]{1,0:T(8,128)(2,1)S(1)} %bitcast.122, bf16[1,1024,1024]{2,1,0:T(8,128)(2,1)S(1)} %copy-done), kind=kOutput, calls=%fused_computation.20 | convolution fusion | flops 2148532224 | bytes 6291456 | tf_op jit(solution)/shard_map/pq,sqc->spc/dot_general | solution.py:87
  169.8 3.5 %collective-permute-done.3 = bf16[128,1024]{1,0:T(8,128)(2,1)S(1)} collective-permute-done((bf16[128,1024]{1,0:T(8,128)(2,1)S(1)}, bf16[128,1024]{1,0:T(8,128)(2,1)S(1)}, u32[]{:S(2)}, u32[]{:S(2)}) %collective-permute-start.3) | collective-permute-done | bytes 262176 | tf_op jit(solution)/shard_map/ppermute | solution.py:46
  173.3 0.9 bitcast_add_fusion.1
  174.1 9.9 %all-to-all-done.1 = bf16[1,1,32,32,1024]{4,2,1,0,3:T(8,128)(2,1)} async-done(((bf16[1,1,32,32,1024]{4,2,1,0,3:T(8,128)(2,1)}), bf16[1,1,32,32,1024]{4,2,1,0,3:T(8,128)(2,1)}, u32[]{:S(2)}, u32[]{:S(2)}) %all-to-all-start.1) | async-done | bytes 2097184 | tf_op jit(solution)/shard_map/all_to_all | solution.py:60
  184.1 5.9 %fusion.14 = bf16[1024,1024]{1,0:T(8,128)(2,1)} fusion(bf16[1024,1024]{1,0:T(8,128)(2,1)} %bitcast.17, bf16[1,1024,1024]{2,1,0:T(8,128)(2,1)} %param.4), kind=kOutput, calls=%fused_computation.21 | convolution fusion | flops 2148532224 | bytes 6291456 | tf_op jit(solution)/shard_map/skc,sjc->kj/dot_general | solution.py:92
  190.0 2.9 %copy.23 = bf16[1,1024,1024]{2,1,0:T(8,128)(2,1)S(1)} copy(bf16[1,1024,1024]{1,2,0:T(8,128)(2,1)} %convert_bitcast_fusion) | data formatting | bytes 4194304 | tf_op jit(solution)/shard_map/optimization_barrier | solution.py:93
  192.8 2.5 copy.24
  195.3 7.4 %all-to-all-start.2 = ((bf16[1,1,32,32,1024]{4,2,1,0,3:T(8,128)(2,1)}), bf16[1,1,32,32,1024]{4,2,1,0,3:T(8,128)(2,1)}, u32[]{:S(2)}, u32[]{:S(2)}) async-start(bf16[1,1,32,32,1024]{4,2,1,0,3:T(8,128)(2,1)} %copy.24), calls=%async_computation.2 | async-start | bytes 4194304 | tf_op jit(solution)/shard_map/all_to_all | solution.py:60
  202.7 0.1 dynamic-slice_bitcast_fusion.2
  202.8 0.0 copy-start.8
  202.9 1.8 collective-permute-start.4
  204.6 1.8 collective-permute-start.6
  206.4 1.8 collective-permute-start.5
  208.2 10.1 %collective-permute-done.4 = bf16[2,128,1024]{2,1,0:T(8,128)(2,1)S(1)} collective-permute-done((bf16[2,128,1024]{2,1,0:T(8,128)(2,1)S(1)}, bf16[2,128,1024]{2,1,0:T(8,128)(2,1)S(1)}, u32[]{:S(2)}, u32[]{:S(2)}) %collective-permute-start.4) | collective-permute-done | bytes 524320 | tf_op jit(solution)/shard_map/ppermute | solution.py:41
  218.3 10.5 %collective-permute-done.6 = bf16[2,128,1024]{2,1,0:T(8,128)(2,1)S(1)} collective-permute-done((bf16[2,128,1024]{2,1,0:T(8,128)(2,1)S(1)}, bf16[2,128,1024]{2,1,0:T(8,128)(2,1)S(1)}, u32[]{:S(2)}, u32[]{:S(2)}) %collective-permute-start.6) | collective-permute-done | bytes 524320 | tf_op jit(solution)/shard_map/ppermute | solution.py:41
  228.8 1.7 collective-permute-done.5
  230.5 1.4 fusion.28
  232.0 4.6 %collective-permute-start.7 = (bf16[128,1024]{1,0:T(8,128)(2,1)S(1)}, bf16[128,1024]{1,0:T(8,128)(2,1)S(1)}, u32[]{:S(2)}, u32[]{:S(2)}) collective-permute-start(bf16[128,1024]{1,0:T(8,128)(2,1)S(1)} %fusion.33), channel_id=1, source_target_pairs={{0,128},{32,160},{64,192},{96,224},{128,0},{160,32},{192,64},{224,... | collective-permute-start | bytes 786440 | tf_op jit(solution)/shard_map/ppermute | solution.py:46
  236.5 6.0 %convolution_bitcast_fusion = f32[1,1024,1024]{2,1,0:T(8,128)} fusion(bf16[1024,1024]{1,0:T(8,128)(2,1)} %bitcast.17, bf16[1,1024,1024]{2,1,0:T(8,128)(2,1)S(1)} %copy-done.8), kind=kOutput, calls=%fused_computation.9 | convolution fusion | flops 2147483648 | bytes 8388608 | tf_op jit(solution)/shard_map/kj,skc->sjc/dot_general | solution.py:98
  242.5 10.8 %collective-permute-done.7 = bf16[128,1024]{1,0:T(8,128)(2,1)S(1)} collective-permute-done((bf16[128,1024]{1,0:T(8,128)(2,1)S(1)}, bf16[128,1024]{1,0:T(8,128)(2,1)S(1)}, u32[]{:S(2)}, u32[]{:S(2)}) %collective-permute-start.7) | collective-permute-done | bytes 262176 | tf_op jit(solution)/shard_map/ppermute | solution.py:46
  253.4 0.9 fusion.31
  254.2 7.6 %all-to-all-done.2 = bf16[1,1,32,32,1024]{4,2,1,0,3:T(8,128)(2,1)} async-done(((bf16[1,1,32,32,1024]{4,2,1,0,3:T(8,128)(2,1)}), bf16[1,1,32,32,1024]{4,2,1,0,3:T(8,128)(2,1)}, u32[]{:S(2)}, u32[]{:S(2)}) %all-to-all-start.2) | async-done | bytes 2097184 | tf_op jit(solution)/shard_map/all_to_all | solution.py:60
  261.9 8.0 %fusion.3 = (bf16[1,1024,1024]{2,1,0:T(8,128)(2,1)}, bf16[1,1024,1024]{2,1,0:T(8,128)(2,1)}) fusion(f32[1,1024,1024]{2,1,0:T(8,128)} %convolution_bitcast_fusion, bf16[1,1024,1024]{2,1,0:T(8,128)(2,1)} %param.5, bf16[1,1,32,32,1024]{4,2,1,0,3:T(8,128)(2,1)} %all-to-all-done.2, bf16[1,1024,1024]{2,1,0:T(8,128)(2,1)} %param.4), kind=kLoop, calls=%fused_computation.6 | loop fusion | flops 8388608 | bytes 14680064 | tf_op jit(solution)/shard_map/convert_element_type | solution.py:102
  (13 shorter events, 0.1 us)
Async XLA Ops:
  0.6 112.2 %copy-start = (bf16[1,1024,1024]{2,1,0:T(8,128)(2,1)S(1)}, bf16[1,1024,1024]{2,1,0:T(8,128)(2,1)}, u32[]{:S(2)}) copy-start(bf16[1,1024,1024]{2,1,0:T(8,128)(2,1)} %param.7) | copy-start | bytes 6291460
  0.6 3.4 %copy-start.2 = (bf16[1,1024,1024]{2,1,0:T(8,128)(2,1)S(1)}, bf16[1,1024,1024]{2,1,0:T(8,128)(2,1)}, u32[]{:S(2)}) copy-start(bf16[1,1024,1024]{2,1,0:T(8,128)(2,1)} %param.4) | copy-start | bytes 6291460
  0.7 3.6 %copy-start.7 = (bf16[1,1024,1024]{2,1,0:T(8,128)(2,1)S(1)}, bf16[1,1024,1024]{2,1,0:T(8,128)(2,1)}, u32[]{:S(2)}) copy-start(bf16[1,1024,1024]{2,1,0:T(8,128)(2,1)} %param.6) | copy-start | bytes 6291460
  112.8 2.5 copy-start.6
  117.7 66.3 %all-to-all-start.1 = ((bf16[1,1,32,32,1024]{4,2,1,0,3:T(8,128)(2,1)}), bf16[1,1,32,32,1024]{4,2,1,0,3:T(8,128)(2,1)}, u32[]{:S(2)}, u32[]{:S(2)}) async-start(bf16[1,1,32,32,1024]{4,2,1,0,3:T(8,128)(2,1)} %copy.21), calls=%async_computation.1 | async-start | bytes 4194304 | tf_op jit(solution)/shard_map/all_to_all | solution.py:60
  129.6 1.3 copy-start.3
  131.9 15.5 %collective-permute-start = (bf16[2,128,1024]{2,1,0:T(8,128)(2,1)}, bf16[2,128,1024]{2,1,0:T(8,128)(2,1)}, u32[]{:S(2)}, u32[]{:S(2)}) collective-permute-start(bf16[2,128,1024]{2,1,0:T(8,128)(2,1)} %get-tuple-element.17), channel_id=1, source_target_pairs={{0,32},{32,64},{64,96},{96,0},{128,160},{160,192},{192,224},{224,1... | collective-permute-start | bytes 1572872 | tf_op jit(solution)/shard_map/ppermute | solution.py:41
  133.4 24.2 %collective-permute-start.2 = (bf16[2,128,1024]{2,1,0:T(8,128)(2,1)S(1)}, bf16[2,128,1024]{2,1,0:T(8,128)(2,1)}, u32[]{:S(2)}, u32[]{:S(2)}) collective-permute-start(bf16[2,128,1024]{2,1,0:T(8,128)(2,1)S(1)} %get-tuple-element.18), channel_id=1, source_target_pairs={{0,96},{32,0},{64,32},{96,64},{128,224},{160,128},{192,160},{224,1... | collective-permute-start | bytes 1572872 | tf_op jit(solution)/shard_map/ppermute | solution.py:41
  135.1 24.5 %collective-permute-start.1 = (bf16[2,128,1024]{2,1,0:T(8,128)(2,1)S(1)}, bf16[2,128,1024]{2,1,0:T(8,128)(2,1)}, u32[]{:S(2)}, u32[]{:S(2)}) collective-permute-start(bf16[2,128,1024]{2,1,0:T(8,128)(2,1)S(1)} %get-tuple-element.19), channel_id=1, source_target_pairs={{0,64},{32,96},{64,0},{96,32},{128,192},{160,224},{192,128},{224,1... | collective-permute-start | bytes 1572872 | tf_op jit(solution)/shard_map/ppermute | solution.py:41
  136.9 29.1 %copy-start.5 = (bf16[1,1,32,32,1,1024]{5,3,2,4,1,0:T(8,128)(2,1)S(1)}, bf16[1,1,32,32,1,1024]{5,3,2,4,1,0:T(8,128)(2,1)}, u32[]{:S(2)}) copy-start(bf16[1,1,32,32,1,1024]{5,3,2,4,1,0:T(8,128)(2,1)} %get-tuple-element.10) | copy-start | bytes 6291460
  161.5 11.8 %collective-permute-start.3 = (bf16[128,1024]{1,0:T(8,128)(2,1)S(1)}, bf16[128,1024]{1,0:T(8,128)(2,1)S(1)}, u32[]{:S(2)}, u32[]{:S(2)}) collective-permute-start(bf16[128,1024]{1,0:T(8,128)(2,1)S(1)} %fusion.32), channel_id=1, source_target_pairs={{0,128},{32,160},{64,192},{96,224},{128,0},{160,32},{192,64},{224,... | collective-permute-start | bytes 786440 | tf_op jit(solution)/shard_map/ppermute | solution.py:46
  195.3 7.4 %copy-start.4 = (bf16[1024,1024]{1,0:T(8,128)(2,1)S(1)}, bf16[1024,1024]{1,0:T(8,128)(2,1)}, u32[]{:S(2)}) copy-start(bf16[1024,1024]{1,0:T(8,128)(2,1)} %fusion.14) | copy-start | bytes 6291460
  195.3 66.5 %all-to-all-start.2 = ((bf16[1,1,32,32,1024]{4,2,1,0,3:T(8,128)(2,1)}), bf16[1,1,32,32,1024]{4,2,1,0,3:T(8,128)(2,1)}, u32[]{:S(2)}, u32[]{:S(2)}) async-start(bf16[1,1,32,32,1024]{4,2,1,0,3:T(8,128)(2,1)} %copy.24), calls=%async_computation.2 | async-start | bytes 4194304 | tf_op jit(solution)/shard_map/all_to_all | solution.py:60
  202.8 33.7 %copy-start.8 = (bf16[1,1024,1024]{2,1,0:T(8,128)(2,1)S(1)}, bf16[1,1024,1024]{2,1,0:T(8,128)(2,1)}, u32[]{:S(2)}) copy-start(bf16[1,1024,1024]{2,1,0:T(8,128)(2,1)} %param.6) | copy-start | bytes 6291460
  202.9 15.5 %collective-permute-start.4 = (bf16[2,128,1024]{2,1,0:T(8,128)(2,1)S(1)}, bf16[2,128,1024]{2,1,0:T(8,128)(2,1)S(1)}, u32[]{:S(2)}, u32[]{:S(2)}) collective-permute-start(bf16[2,128,1024]{2,1,0:T(8,128)(2,1)S(1)} %get-tuple-element.12), channel_id=1, source_target_pairs={{0,32},{32,64},{64,96},{96,0},{128,160},{160,192},{192,224},{224,1... | collective-permute-start | bytes 1572872 | tf_op jit(solution)/shard_map/ppermute | solution.py:41
  204.6 24.2 %collective-permute-start.6 = (bf16[2,128,1024]{2,1,0:T(8,128)(2,1)S(1)}, bf16[2,128,1024]{2,1,0:T(8,128)(2,1)S(1)}, u32[]{:S(2)}, u32[]{:S(2)}) collective-permute-start(bf16[2,128,1024]{2,1,0:T(8,128)(2,1)S(1)} %get-tuple-element.13), channel_id=1, source_target_pairs={{0,96},{32,0},{64,32},{96,64},{128,224},{160,128},{192,160},{224,1... | collective-permute-start | bytes 1572872 | tf_op jit(solution)/shard_map/ppermute | solution.py:41
  206.4 24.1 %collective-permute-start.5 = (bf16[2,128,1024]{2,1,0:T(8,128)(2,1)S(1)}, bf16[2,128,1024]{2,1,0:T(8,128)(2,1)S(1)}, u32[]{:S(2)}, u32[]{:S(2)}) collective-permute-start(bf16[2,128,1024]{2,1,0:T(8,128)(2,1)S(1)} %get-tuple-element.14), channel_id=1, source_target_pairs={{0,64},{32,96},{64,0},{96,32},{128,192},{160,224},{192,128},{224,1... | collective-permute-start | bytes 1572872 | tf_op jit(solution)/shard_map/ppermute | solution.py:41
  232.0 21.4 %collective-permute-start.7 = (bf16[128,1024]{1,0:T(8,128)(2,1)S(1)}, bf16[128,1024]{1,0:T(8,128)(2,1)S(1)}, u32[]{:S(2)}, u32[]{:S(2)}) collective-permute-start(bf16[128,1024]{1,0:T(8,128)(2,1)S(1)} %fusion.33), channel_id=1, source_target_pairs={{0,128},{32,160},{64,192},{96,224},{128,0},{160,32},{192,64},{224,... | collective-permute-start | bytes 786440 | tf_op jit(solution)/shard_map/ppermute | solution.py:46
  261.9 8.0 %copy-start.1 = (bf16[1,1024,1024]{2,1,0:T(8,128)(2,1)S(1)}, bf16[1,1024,1024]{2,1,0:T(8,128)(2,1)}, u32[]{:S(2)}) copy-start(bf16[1,1024,1024]{2,1,0:T(8,128)(2,1)} %param.7) | copy-start | bytes 6291460

commit v5 on v3

--- a/solution.py
+++ b/solution.py
@@ -89,10 +89,10 @@
     )
     part_two = jnp.einsum("spc,sqc->pq", gated_moved, moved, preferred_element_type=jnp.float32)
     grad_two = _dp_reduce(part_two.astype(jnp.bfloat16), ring)
+    second, grad_two = lax.optimization_barrier((second, grad_two))
+    monarch = _from_moved(second, count, rows)
     part_one = jnp.einsum("skc,sjc->kj", back_moved, inputs, preferred_element_type=jnp.float32)
-    part_one, second = lax.optimization_barrier((part_one.astype(jnp.bfloat16), second))
-    grad_one = _dp_reduce(part_one, ring)
-    monarch = _from_moved(second, count, rows)
+    grad_one = _dp_reduce(part_one.astype(jnp.bfloat16), ring)
     spread = _rowmajor(jnp.einsum("kj,skc->sjc", fone, back_moved, preferred_element_type=jnp.float32))
     spread = lax.optimization_barrier(spread)
     mfull = monarch.astype(jnp.float32)

time: 279 us -> 264 us (0.946)
  waiting for transfers between devices: 81.4 us -> 71.3 us
  matrix products: 26.6 us -> 23 us
    all_to_all x2, waiting for transfers between devices: 42.6 us -> 18.1 us  [_from_moved(): lax.all_to_all(data.reshape(seqs, 1, rows, count, width), 'seq', split_ax...]
    ppermute x6, waiting for transfers between devices: 31.9 us -> 45.3 us  [_dp_reduce(): acc = acc + lax.ppermute(piece, 'dp', perm).astype(jnp.float32)]
  transfers between devices with their start and end apart: 10 -> 10, of which waited for: 6 -> 10; matrix products, arithmetic and copies ran while one was open for 9% -> 11% of each run, Pallas kernels for 0% -> 0%
where the time goes in v5:
time: 264 us; the launch traced here: 261 us
  blocking collectives  102 us (39%)
  waiting for transfers between devices  71.3 us (27%)
  starting transfers between devices  33.8 us (13%)
  matrix products  23 us (9%)
  other arithmetic  15.6 us (6%)
  local copies, waits for them, and re-layouts  14.7 us (6%)
    all_to_all x1, blocking collectives, local(): in1 = lax.all_to_all(out1, 'seq', split_axis=1, concat_axis=3, tiled=True)  102 us
    ppermute x6, waiting for transfers between devices, _dp_reduce(): acc = acc + lax.ppermute(piece, 'dp', perm).astype(jnp.float32)  45.3 us
    all_to_all x2, waiting for transfers between devices, _from_moved(): lax.all_to_all(data.reshape(seqs, 1, rows, count, width), 'seq', split_ax...  18.1 us
    all_to_all x2, starting transfers between devices, _from_moved(): lax.all_to_all(data.reshape(seqs, 1, rows, count, width), 'seq', split_ax...  16.8 us
    ppermute x6, starting transfers between devices, _dp_reduce(): acc = acc + lax.ppermute(piece, 'dp', perm).astype(jnp.float32)  9.2 us
    convert_element_type x1, other arithmetic, local(): grad_input = _rowmajor((dyfull * mfull + spread).astype(jnp.bfloat16))  7.96 us
    ppermute x2, waiting for transfers between devices, _dp_reduce(): lax.ppermute(piece.astype(jnp.bfloat16), 'dp', perm).astype(jnp.float32)  7.9 us
    ppermute x2, starting transfers between devices, _dp_reduce(): lax.ppermute(piece.astype(jnp.bfloat16), 'dp', perm).astype(jnp.float32)  7.72 us
  transfers between devices with their start and end apart: 10, of which 10 were waited for; matrix products, arithmetic and copies ran while one was open for 11% of the time, Pallas kernels for 0%

profile of v5, /device:TPU:8, one launch (start us, length us, event | category | flops | bytes accessed | tf_op | source)
XLA Modules:
  0.0 260.9 jit_solution(16325528825421842184)
XLA Ops:
  0.6 0.0 copy-start
  0.6 0.0 copy-start.2
  0.7 0.0 copy-start.7
  0.7 3.4 %fusion.1 = bf16[1,1024,1024]{2,1,0:T(8,128)(2,1)S(1)} fusion(bf16[1,1024,1024]{2,1,0:T(8,128)(2,1)} %param.4, bf16[1,1024,1024]{2,1,0:T(8,128)(2,1)} %param.5), kind=kLoop, calls=%fused_computation.4 | loop fusion | flops 4194304 | bytes 6291456 | tf_op jit(solution)/shard_map/convert_element_type | solution.py:74
  4.0 0.2 copy-done.7
  4.3 2.3 fusion.17
  6.6 0.4 pad_maximum_fusion
  7.0 101.7 %all_to_all.39 = bf16[2,32,32,1,1024]{4,2,0,3,1:T(8,128)(2,1)S(1)} all-to-all(bf16[2,32,32,1,1024]{4,2,0,3,1:T(8,128)(2,1)S(1)} %pad_maximum_fusion), channel_id=1, replica_groups=mesh['dp'=8,'seq'=32] {'seq'}, dimensions={1} | all-to-all | bytes 8388608 | tf_op jit(solution)/shard_map/all_to_all | solution.py:79
  108.7 2.3 copy.29
  111.0 1.8 fusion.34
  112.8 2.5 fusion.24
  115.2 2.5 copy.24
  117.7 7.2 %all-to-all-start.2 = ((bf16[1,1,32,32,1024]{4,2,1,0,3:T(8,128)(2,1)}), bf16[1,1,32,32,1024]{4,2,1,0,3:T(8,128)(2,1)}, u32[]{:S(2)}, u32[]{:S(2)}) async-start(bf16[1,1,32,32,1024]{4,2,1,0,3:T(8,128)(2,1)} %copy.24), calls=%async_computation.2 | async-start | bytes 4194304 | tf_op jit(solution)/shard_map/all_to_all | solution.py:60
  125.0 4.6 %convolution_convert_fusion = bf16[1024,1024]{1,0:T(8,128)(2,1)S(1)} fusion(bf16[1024,1024]{1,0:T(8,128)(2,1)} %bitcast.124, bf16[1024,1024]{1,0:T(8,128)(2,1)} %bitcast.121), kind=kOutput, calls=%fused_computation.24 | convolution fusion | flops 2148532224 | bytes 6291456 | tf_op jit(solution)/shard_map/spc,sqc->pq/dot_general | solution.py:90
  129.6 1.3 copy-done.4
  130.9 0.9 dynamic-slice_bitcast_fusion.5
  131.8 1.5 collective-permute-start
  133.3 1.7 collective-permute-start.2
  135.1 1.8 collective-permute-start.1
  136.9 10.4 %collective-permute-done = bf16[2,128,1024]{2,1,0:T(8,128)(2,1)} collective-permute-done((bf16[2,128,1024]{2,1,0:T(8,128)(2,1)}, bf16[2,128,1024]{2,1,0:T(8,128)(2,1)}, u32[]{:S(2)}, u32[]{:S(2)}) %collective-permute-start) | collective-permute-done | bytes 524320 | tf_op jit(solution)/shard_map/ppermute | solution.py:41
  147.3 10.2 %collective-permute-done.2 = bf16[2,128,1024]{2,1,0:T(8,128)(2,1)} collective-permute-done((bf16[2,128,1024]{2,1,0:T(8,128)(2,1)S(1)}, bf16[2,128,1024]{2,1,0:T(8,128)(2,1)}, u32[]{:S(2)}, u32[]{:S(2)}) %collective-permute-start.2) | collective-permute-done | bytes 524320 | tf_op jit(solution)/shard_map/ppermute | solution.py:41
  157.5 2.0 collective-permute-done.1
  159.5 1.8 fusion.30
  161.4 4.6 %collective-permute-start.3 = (bf16[128,1024]{1,0:T(8,128)(2,1)S(1)}, bf16[128,1024]{1,0:T(8,128)(2,1)S(1)}, u32[]{:S(2)}, u32[]{:S(2)}) collective-permute-start(bf16[128,1024]{1,0:T(8,128)(2,1)S(1)} %fusion.32), channel_id=1, source_target_pairs={{0,128},{32,160},{64,192},{96,224},{128,0},{160,32},{192,64},{224,... | collective-permute-start | bytes 786440 | tf_op jit(solution)/shard_map/ppermute | solution.py:46
  166.0 3.7 %convert_bitcast_fusion = bf16[1,1024,1024]{1,2,0:T(8,128)(2,1)} fusion(bf16[1024,1024]{1,0:T(8,128)(2,1)S(1)} %bitcast.122, bf16[1,1024,1024]{2,1,0:T(8,128)(2,1)S(1)} %copy-done), kind=kOutput, calls=%fused_computation.20 | convolution fusion | flops 2148532224 | bytes 6291456 | tf_op jit(solution)/shard_map/pq,sqc->spc/dot_general | solution.py:87
  169.7 3.5 %collective-permute-done.3 = bf16[128,1024]{1,0:T(8,128)(2,1)S(1)} collective-permute-done((bf16[128,1024]{1,0:T(8,128)(2,1)S(1)}, bf16[128,1024]{1,0:T(8,128)(2,1)S(1)}, u32[]{:S(2)}, u32[]{:S(2)}) %collective-permute-start.3) | collective-permute-done | bytes 262176 | tf_op jit(solution)/shard_map/ppermute | solution.py:46
  173.3 0.9 bitcast_add_fusion.1
  174.1 2.9 %copy.22 = bf16[1,1024,1024]{2,1,0:T(8,128)(2,1)S(1)} copy(bf16[1,1024,1024]{1,2,0:T(8,128)(2,1)} %convert_bitcast_fusion) | data formatting | bytes 4194304 | tf_op jit(solution)/shard_map/optimization_barrier | solution.py:92
  177.0 2.5 copy.23
  179.5 4.6 %all-to-all-done.2 = bf16[1,1,32,32,1024]{4,2,1,0,3:T(8,128)(2,1)} async-done(((bf16[1,1,32,32,1024]{4,2,1,0,3:T(8,128)(2,1)}), bf16[1,1,32,32,1024]{4,2,1,0,3:T(8,128)(2,1)}, u32[]{:S(2)}, u32[]{:S(2)}) %all-to-all-start.2) | async-done | bytes 2097184 | tf_op jit(solution)/shard_map/all_to_all | solution.py:60
  184.1 9.7 %all-to-all-start.1 = ((bf16[1,1,32,32,1024]{4,2,1,0,3:T(8,128)(2,1)}), bf16[1,1,32,32,1024]{4,2,1,0,3:T(8,128)(2,1)}, u32[]{:S(2)}, u32[]{:S(2)}) async-start(bf16[1,1,32,32,1024]{4,2,1,0,3:T(8,128)(2,1)} %copy.23), calls=%async_computation.1 | async-start | bytes 4194304 | tf_op jit(solution)/shard_map/all_to_all | solution.py:60
  193.7 0.0 copy-done.3
  193.7 4.0 %fusion.14 = bf16[1024,1024]{1,0:T(8,128)(2,1)S(1)} fusion(bf16[1024,1024]{1,0:T(8,128)(2,1)} %bitcast.34, bf16[1,1024,1024]{2,1,0:T(8,128)(2,1)S(1)} %copy-done.3), kind=kOutput, calls=%fused_computation.21 | convolution fusion | flops 2148532224 | bytes 6291456 | tf_op jit(solution)/shard_map/skc,sjc->kj/dot_general | solution.py:94
  197.7 0.1 dynamic-slice_bitcast_fusion.2
  197.8 0.0 copy-start.8
  197.9 1.3 collective-permute-start.4
  199.1 2.3 collective-permute-start.6
  201.4 0.6 collective-permute-start.5
  202.0 12.0 %collective-permute-done.4 = bf16[2,128,1024]{2,1,0:T(8,128)(2,1)S(1)} collective-permute-done((bf16[2,128,1024]{2,1,0:T(8,128)(2,1)S(1)}, bf16[2,128,1024]{2,1,0:T(8,128)(2,1)S(1)}, u32[]{:S(2)}, u32[]{:S(2)}) %collective-permute-start.4) | collective-permute-done | bytes 524320 | tf_op jit(solution)/shard_map/ppermute | solution.py:41
  214.0 9.9 %collective-permute-done.6 = bf16[2,128,1024]{2,1,0:T(8,128)(2,1)S(1)} collective-permute-done((bf16[2,128,1024]{2,1,0:T(8,128)(2,1)S(1)}, bf16[2,128,1024]{2,1,0:T(8,128)(2,1)S(1)}, u32[]{:S(2)}, u32[]{:S(2)}) %collective-permute-start.6) | collective-permute-done | bytes 524320 | tf_op jit(solution)/shard_map/ppermute | solution.py:41
  223.8 0.9 collective-permute-done.5
  224.7 0.3 fusion.28
  225.1 3.1 %collective-permute-start.7 = (bf16[128,1024]{1,0:T(8,128)(2,1)S(1)}, bf16[128,1024]{1,0:T(8,128)(2,1)S(1)}, u32[]{:S(2)}, u32[]{:S(2)}) collective-permute-start(bf16[128,1024]{1,0:T(8,128)(2,1)S(1)} %fusion.33), channel_id=1, source_target_pairs={{0,128},{32,160},{64,192},{96,224},{128,0},{160,32},{192,64},{224,... | collective-permute-start | bytes 786440 | tf_op jit(solution)/shard_map/ppermute | solution.py:46
  228.2 6.0 %convolution_bitcast_fusion = f32[1,1024,1024]{2,1,0:T(8,128)} fusion(bf16[1024,1024]{1,0:T(8,128)(2,1)} %bitcast.34, bf16[1,1024,1024]{2,1,0:T(8,128)(2,1)S(1)} %copy-done.8), kind=kOutput, calls=%fused_computation.9 | convolution fusion | flops 2147483648 | bytes 8388608 | tf_op jit(solution)/shard_map/kj,skc->sjc/dot_general | solution.py:96
  234.2 4.4 %collective-permute-done.7 = bf16[128,1024]{1,0:T(8,128)(2,1)S(1)} collective-permute-done((bf16[128,1024]{1,0:T(8,128)(2,1)S(1)}, bf16[128,1024]{1,0:T(8,128)(2,1)S(1)}, u32[]{:S(2)}, u32[]{:S(2)}) %collective-permute-start.7) | collective-permute-done | bytes 262176 | tf_op jit(solution)/shard_map/ppermute | solution.py:46
  238.6 0.9 fusion.31
  239.4 13.5 %all-to-all-done.1 = bf16[1,1,32,32,1024]{4,2,1,0,3:T(8,128)(2,1)} async-done(((bf16[1,1,32,32,1024]{4,2,1,0,3:T(8,128)(2,1)}), bf16[1,1,32,32,1024]{4,2,1,0,3:T(8,128)(2,1)}, u32[]{:S(2)}, u32[]{:S(2)}) %all-to-all-start.1) | async-done | bytes 2097184 | tf_op jit(solution)/shard_map/all_to_all | solution.py:60
  252.9 8.0 %fusion.3 = (bf16[1,1024,1024]{2,1,0:T(8,128)(2,1)}, bf16[1,1024,1024]{2,1,0:T(8,128)(2,1)}) fusion(f32[1,1024,1024]{2,1,0:T(8,128)} %convolution_bitcast_fusion, bf16[1,1024,1024]{2,1,0:T(8,128)(2,1)} %param.5, bf16[1,1,32,32,1024]{4,2,1,0,3:T(8,128)(2,1)} %all-to-all-done.1, bf16[1,1024,1024]{2,1,0:T(8,128)(2,1)} %param.4), kind=kLoop, calls=%fused_computation.6 | loop fusion | flops 8388608 | bytes 14680064 | tf_op jit(solution)/shard_map/convert_element_type | solution.py:100
  (13 shorter events, 0.1 us)
Async XLA Ops:
  0.6 112.1 %copy-start = (bf16[1,1024,1024]{2,1,0:T(8,128)(2,1)S(1)}, bf16[1,1024,1024]{2,1,0:T(8,128)(2,1)}, u32[]{:S(2)}) copy-start(bf16[1,1024,1024]{2,1,0:T(8,128)(2,1)} %param.7) | copy-start | bytes 6291460
  0.6 3.4 %copy-start.2 = (bf16[1,1024,1024]{2,1,0:T(8,128)(2,1)S(1)}, bf16[1,1024,1024]{2,1,0:T(8,128)(2,1)}, u32[]{:S(2)}) copy-start(bf16[1,1024,1024]{2,1,0:T(8,128)(2,1)} %param.4) | copy-start | bytes 6291460
  0.7 3.6 %copy-start.7 = (bf16[1,1024,1024]{2,1,0:T(8,128)(2,1)S(1)}, bf16[1,1024,1024]{2,1,0:T(8,128)(2,1)}, u32[]{:S(2)}) copy-start(bf16[1,1024,1024]{2,1,0:T(8,128)(2,1)} %param.6) | copy-start | bytes 6291460
  112.8 2.5 copy-start.6
  117.7 66.3 %all-to-all-start.2 = ((bf16[1,1,32,32,1024]{4,2,1,0,3:T(8,128)(2,1)}), bf16[1,1,32,32,1024]{4,2,1,0,3:T(8,128)(2,1)}, u32[]{:S(2)}, u32[]{:S(2)}) async-start(bf16[1,1,32,32,1024]{4,2,1,0,3:T(8,128)(2,1)} %copy.24), calls=%async_computation.2 | async-start | bytes 4194304 | tf_op jit(solution)/shard_map/all_to_all | solution.py:60
  129.6 1.3 copy-start.4
  131.8 15.5 %collective-permute-start = (bf16[2,128,1024]{2,1,0:T(8,128)(2,1)}, bf16[2,128,1024]{2,1,0:T(8,128)(2,1)}, u32[]{:S(2)}, u32[]{:S(2)}) collective-permute-start(bf16[2,128,1024]{2,1,0:T(8,128)(2,1)} %get-tuple-element.15), channel_id=1, source_target_pairs={{0,32},{32,64},{64,96},{96,0},{128,160},{160,192},{192,224},{224,1... | collective-permute-start | bytes 1572872 | tf_op jit(solution)/shard_map/ppermute | solution.py:41
  133.3 24.2 %collective-permute-start.2 = (bf16[2,128,1024]{2,1,0:T(8,128)(2,1)S(1)}, bf16[2,128,1024]{2,1,0:T(8,128)(2,1)}, u32[]{:S(2)}, u32[]{:S(2)}) collective-permute-start(bf16[2,128,1024]{2,1,0:T(8,128)(2,1)S(1)} %get-tuple-element.16), channel_id=1, source_target_pairs={{0,96},{32,0},{64,32},{96,64},{128,224},{160,128},{192,160},{224,1... | collective-permute-start | bytes 1572872 | tf_op jit(solution)/shard_map/ppermute | solution.py:41
  135.1 24.5 %collective-permute-start.1 = (bf16[2,128,1024]{2,1,0:T(8,128)(2,1)S(1)}, bf16[2,128,1024]{2,1,0:T(8,128)(2,1)}, u32[]{:S(2)}, u32[]{:S(2)}) collective-permute-start(bf16[2,128,1024]{2,1,0:T(8,128)(2,1)S(1)} %get-tuple-element.17), channel_id=1, source_target_pairs={{0,64},{32,96},{64,0},{96,32},{128,192},{160,224},{192,128},{224,1... | collective-permute-start | bytes 1572872 | tf_op jit(solution)/shard_map/ppermute | solution.py:41
  136.9 29.1 %copy-start.5 = (bf16[1,1,32,32,1,1024]{5,3,2,4,1,0:T(8,128)(2,1)S(1)}, bf16[1,1,32,32,1,1024]{5,3,2,4,1,0:T(8,128)(2,1)}, u32[]{:S(2)}) copy-start(bf16[1,1,32,32,1,1024]{5,3,2,4,1,0:T(8,128)(2,1)} %get-tuple-element.9) | copy-start | bytes 6291460
  161.4 11.8 %collective-permute-start.3 = (bf16[128,1024]{1,0:T(8,128)(2,1)S(1)}, bf16[128,1024]{1,0:T(8,128)(2,1)S(1)}, u32[]{:S(2)}, u32[]{:S(2)}) collective-permute-start(bf16[128,1024]{1,0:T(8,128)(2,1)S(1)} %fusion.32), channel_id=1, source_target_pairs={{0,128},{32,160},{64,192},{96,224},{128,0},{160,32},{192,64},{224,... | collective-permute-start | bytes 786440 | tf_op jit(solution)/shard_map/ppermute | solution.py:46
  179.4 14.3 %copy-start.3 = (bf16[1,1024,1024]{2,1,0:T(8,128)(2,1)S(1)}, bf16[1,1024,1024]{2,1,0:T(8,128)(2,1)}, u32[]{:S(2)}) copy-start(bf16[1,1024,1024]{2,1,0:T(8,128)(2,1)} %param.4) | copy-start | bytes 6291460
  184.1 68.9 %all-to-all-start.1 = ((bf16[1,1,32,32,1024]{4,2,1,0,3:T(8,128)(2,1)}), bf16[1,1,32,32,1024]{4,2,1,0,3:T(8,128)(2,1)}, u32[]{:S(2)}, u32[]{:S(2)}) async-start(bf16[1,1,32,32,1024]{4,2,1,0,3:T(8,128)(2,1)} %copy.23), calls=%async_computation.1 | async-start | bytes 4194304 | tf_op jit(solution)/shard_map/all_to_all | solution.py:60
  197.8 30.4 %copy-start.8 = (bf16[1,1024,1024]{2,1,0:T(8,128)(2,1)S(1)}, bf16[1,1024,1024]{2,1,0:T(8,128)(2,1)}, u32[]{:S(2)}) copy-start(bf16[1,1024,1024]{2,1,0:T(8,128)(2,1)} %param.6) | copy-start | bytes 6291460
  197.9 16.1 %collective-permute-start.4 = (bf16[2,128,1024]{2,1,0:T(8,128)(2,1)S(1)}, bf16[2,128,1024]{2,1,0:T(8,128)(2,1)S(1)}, u32[]{:S(2)}, u32[]{:S(2)}) collective-permute-start(bf16[2,128,1024]{2,1,0:T(8,128)(2,1)S(1)} %get-tuple-element.10), channel_id=1, source_target_pairs={{0,32},{32,64},{64,96},{96,0},{128,160},{160,192},{192,224},{224,1... | collective-permute-start | bytes 1572872 | tf_op jit(solution)/shard_map/ppermute | solution.py:41
  199.1 24.7 %collective-permute-start.6 = (bf16[2,128,1024]{2,1,0:T(8,128)(2,1)S(1)}, bf16[2,128,1024]{2,1,0:T(8,128)(2,1)S(1)}, u32[]{:S(2)}, u32[]{:S(2)}) collective-permute-start(bf16[2,128,1024]{2,1,0:T(8,128)(2,1)S(1)} %get-tuple-element.11), channel_id=1, source_target_pairs={{0,96},{32,0},{64,32},{96,64},{128,224},{160,128},{192,160},{224,1... | collective-permute-start | bytes 1572872 | tf_op jit(solution)/shard_map/ppermute | solution.py:41
  201.4 23.3 %collective-permute-start.5 = (bf16[2,128,1024]{2,1,0:T(8,128)(2,1)S(1)}, bf16[2,128,1024]{2,1,0:T(8,128)(2,1)S(1)}, u32[]{:S(2)}, u32[]{:S(2)}) collective-permute-start(bf16[2,128,1024]{2,1,0:T(8,128)(2,1)S(1)} %get-tuple-element.12), channel_id=1, source_target_pairs={{0,64},{32,96},{64,0},{96,32},{128,192},{160,224},{192,128},{224,1... | collective-permute-start | bytes 1572872 | tf_op jit(solution)/shard_map/ppermute | solution.py:41
  225.1 13.5 %collective-permute-start.7 = (bf16[128,1024]{1,0:T(8,128)(2,1)S(1)}, bf16[128,1024]{1,0:T(8,128)(2,1)S(1)}, u32[]{:S(2)}, u32[]{:S(2)}) collective-permute-start(bf16[128,1024]{1,0:T(8,128)(2,1)S(1)} %fusion.33), channel_id=1, source_target_pairs={{0,128},{32,160},{64,192},{96,224},{128,0},{160,32},{192,64},{224,... | collective-permute-start | bytes 786440 | tf_op jit(solution)/shard_map/ppermute | solution.py:46
  252.9 8.0 %copy-start.1 = (bf16[1,1024,1024]{2,1,0:T(8,128)(2,1)S(1)}, bf16[1,1024,1024]{2,1,0:T(8,128)(2,1)}, u32[]{:S(2)}) copy-start(bf16[1,1024,1024]{2,1,0:T(8,128)(2,1)} %param.7) | copy-start | bytes 6291460

commit v6 on v5

--- a/solution.py
+++ b/solution.py
@@ -47,20 +47,9 @@
     return own
 
 
-def _to_moved(data, count, rows):
-    seqs, block, width = data.shape
-    out = lax.all_to_all(
-        data.reshape(seqs, count, rows, 1, width), "seq", split_axis=1, concat_axis=3, tiled=True
-    )
-    return out.reshape(seqs, block, width)
-
-
-def _from_moved(data, count, rows):
-    seqs, block, width = data.shape
-    out = lax.all_to_all(
-        data.reshape(seqs, 1, rows, count, width), "seq", split_axis=3, concat_axis=1, tiled=True
-    )
-    return out.reshape(seqs, block, width)
+def _exchange(data, count):
+    axis = data.ndim - 3
+    return lax.all_to_all(data, "seq", split_axis=axis, concat_axis=axis, tiled=True)
 
 
 def local(inputs, cotangent, factor_one, factor_two, ring):
@@ -68,29 +57,35 @@
     count = lax.axis_size("seq")
     rows = block // count
     fone = factor_one[0]
-    ftwo = factor_two[0]
+    ftwo = factor_two[0].reshape(rows, count, rows, count).transpose(1, 0, 3, 2).reshape(block, block)
     xfull = inputs.astype(jnp.float32)
     dyfull = cotangent.astype(jnp.float32)
     gated = _rowmajor((dyfull * xfull).astype(jnp.bfloat16))
     first = jnp.einsum("kj,sjc->skc", fone, inputs, preferred_element_type=jnp.float32).astype(
         jnp.bfloat16
     )
-    out1 = jnp.stack([first, gated]).reshape(2 * seqs, count, rows, 1, width)
-    in1 = lax.all_to_all(out1, "seq", split_axis=1, concat_axis=3, tiled=True)
-    in1 = in1.reshape(2, seqs, block, width)
+    out1 = jnp.stack([first, gated]).reshape(2 * seqs, count, rows, width)
+    in1 = _exchange(out1, count).reshape(2, seqs, block, width)
     moved = in1[0]
     gated_moved = in1[1]
     back_two = jnp.einsum(
         "pq,spc->sqc", ftwo, gated_moved, preferred_element_type=jnp.float32
     ).astype(jnp.bfloat16)
-    back_moved = _from_moved(back_two, count, rows)
+    back_moved = _exchange(back_two.reshape(seqs, count, rows, width), count)
+    back_moved = back_moved.reshape(seqs, block, width)
     second = jnp.einsum("pq,sqc->spc", ftwo, moved, preferred_element_type=jnp.float32).astype(
         jnp.bfloat16
     )
-    part_two = jnp.einsum("spc,sqc->pq", gated_moved, moved, preferred_element_type=jnp.float32)
+    part_two = jnp.einsum(
+        "smrc,sntc->rmtn",
+        gated_moved.reshape(seqs, count, rows, width),
+        moved.reshape(seqs, count, rows, width),
+        preferred_element_type=jnp.float32,
+    ).reshape(block, block)
     grad_two = _dp_reduce(part_two.astype(jnp.bfloat16), ring)
     second, grad_two = lax.optimization_barrier((second, grad_two))
-    monarch = _from_moved(second, count, rows)
+    monarch = _exchange(second.reshape(seqs, count, rows, width), count)
+    monarch = monarch.reshape(seqs, block, width)
     part_one = jnp.einsum("skc,sjc->kj", back_moved, inputs, preferred_element_type=jnp.float32)
     grad_one = _dp_reduce(part_one.astype(jnp.bfloat16), ring)
     spread = _rowmajor(jnp.einsum("kj,skc->sjc", fone, back_moved, preferred_element_type=jnp.float32))

time: 264 us -> 304 us (1.15)
  blocking collectives: 102 us -> 0 us
  local copies, waits for them, and re-layouts: 14.7 us -> 77.7 us
  waiting for transfers between devices: 71.3 us -> 123 us
  starting transfers between devices: 33.8 us -> 45.8 us
  matrix products: 23 us -> 34.5 us
    all_to_all x1 -> x0, blocking collectives: 102 us -> none  [local(): in1 = lax.all_to_all(out1, 'seq', split_axis=1, concat_axis=3, tiled=True)]
    all_to_all x2 -> x3, waiting for transfers between devices: 18.1 us -> 81.4 us  [_exchange(): lax.all_to_all(data, 'seq', split_axis=axis, concat_axis=axis, tiled=True)]
    convert_element_type x0 -> x2, local copies, waits for them, and re-layouts: none -> 30.8 us  [local(): grad_two = _dp_reduce(part_two.astype(jnp.bfloat16), ring)]
    another operation x0 -> x2, local copies, waits for them, and re-layouts: none -> 22.9 us  [local(): factor_two[0].reshape(rows, count, rows, count).transpose(1, 0, 3, 2)]
    all_to_all x2 -> x3, starting transfers between devices: 16.8 us -> 29.3 us  [_exchange(): lax.all_to_all(data, 'seq', split_axis=axis, concat_axis=axis, tiled=True)]
    dot_general x1, matrix products: 4.59 us -> 12.5 us  [local(): jnp.einsum('smrc,sntc->rmtn', gated_moved.reshape(seqs, count, rows, widt...]
    reshape x2 -> x1, local copies, waits for them, and re-layouts: 4.94 us -> 12.4 us  [local(): factor_two[0].reshape(rows, count, rows, count).transpose(1, 0, 3, 2)]
    ppermute x2, waiting for transfers between devices: 7.9 us -> 1.73 us  [_dp_reduce(): lax.ppermute(piece.astype(jnp.bfloat16), 'dp', perm).astype(jnp.float32)]
  transfers between devices with their start and end apart: 10 -> 11, of which waited for: 10 -> 7; matrix products, arithmetic and copies ran while one was open for 11% -> 38% of each run, Pallas kernels for 0% -> 0%
where the time goes in v6:
time: 304 us; the launch traced here: 299 us
  waiting for transfers between devices  123 us (40%)
  local copies, waits for them, and re-layouts  77.7 us (26%)
  starting transfers between devices  45.8 us (15%)
  matrix products  34.5 us (11%)
  other arithmetic  17.4 us (6%)
    all_to_all x3, waiting for transfers between devices, _exchange(): lax.all_to_all(data, 'seq', split_axis=axis, concat_axis=axis, tiled=True)  81.4 us
    ppermute x6, waiting for transfers between devices, _dp_reduce(): acc = acc + lax.ppermute(piece, 'dp', perm).astype(jnp.float32)  39.9 us
    convert_element_type x2, local copies, waits for them, and re-layouts, local(): grad_two = _dp_reduce(part_two.astype(jnp.bfloat16), ring)  30.8 us
    all_to_all x3, starting transfers between devices, _exchange(): lax.all_to_all(data, 'seq', split_axis=axis, concat_axis=axis, tiled=True)  29.3 us
    another operation x2, local copies, waits for them, and re-layouts, local(): factor_two[0].reshape(rows, count, rows, count).transpose(1, 0, 3, 2)  22.9 us
    dot_general x1, matrix products, local(): jnp.einsum('smrc,sntc->rmtn', gated_moved.reshape(seqs, count, rows, widt...  12.5 us
    reshape x1, local copies, waits for them, and re-layouts, local(): factor_two[0].reshape(rows, count, rows, count).transpose(1, 0, 3, 2)  12.4 us
    ppermute x6, starting transfers between devices, _dp_reduce(): acc = acc + lax.ppermute(piece, 'dp', perm).astype(jnp.float32)  8.37 us
  transfers between devices with their start and end apart: 11, of which 7 were waited for; matrix products, arithmetic and copies ran while one was open for 38% of the time, Pallas kernels for 0%

profile of v6, /device:TPU:8, one launch (start us, length us, event | category | flops | bytes accessed | tf_op | source)
XLA Modules:
  0.0 299.1 jit_solution(415146277777443347)
XLA Ops:
  0.6 0.0 copy-start
  0.6 0.0 copy-start.1
  0.7 3.3 %fusion = bf16[1,1024,1024]{2,1,0:T(8,128)(2,1)S(1)} fusion(bf16[1,1024,1024]{2,1,0:T(8,128)(2,1)} %param.4, bf16[1,1024,1024]{2,1,0:T(8,128)(2,1)} %param.5), kind=kLoop, calls=%fused_computation.4 | loop fusion | flops 4194304 | bytes 6291456 | tf_op jit(solution)/shard_map/convert_element_type | solution.py:63
  4.0 0.1 copy-done.1
  4.1 2.3 fusion.15
  6.5 2.4 pad_maximum_fusion
  8.8 9.2 %all-to-all-start = ((bf16[2,32,32,1024]{3,2,0,1:T(8,128)(2,1)}), bf16[2,32,32,1024]{3,2,0,1:T(8,128)(2,1)}, u32[]{:S(2)}, u32[]{:S(2)}) async-start(bf16[2,32,32,1024]{3,2,0,1:T(8,128)(2,1)} %pad_maximum_fusion), calls=%async_computation | async-start | bytes 8388608 | tf_op jit(solution)/shard_map/all_to_all | solution.py:52
  18.0 11.0 %reshape_squeeze.2 = bf16[32,32,32,32]{3,2,1,0:T(8,128)(2,1)} reshape(bf16[1,1024,1024]{2,1,0:T(8,128)(2,1)} %param.7) | data formatting | bytes 4194304 | tf_op jit(solution)/shard_map/reshape;squeeze | solution.py:60
  29.0 11.9 %copy.17 = bf16[32,32,32,32]{2,3,0,1:T(8,128)(2,1)} copy(bf16[32,32,32,32]{3,2,1,0:T(8,128)(2,1)} %reshape_squeeze.2) | data formatting | bytes 4194304 | tf_op jit(solution)/shard_map/reshape;squeeze | solution.py:60
  40.9 12.4 %reshape.91 = bf16[1024,1024]{1,0:T(8,128)(2,1)} reshape(bf16[32,32,32,32]{3,2,1,0:T(8,128)(2,1)} %bitcast.112) | data formatting | bytes 4194304 | tf_op jit(solution)/shard_map/reshape | solution.py:60
  53.3 57.9 %all-to-all-done = bf16[2,32,32,1024]{3,2,0,1:T(8,128)(2,1)} async-done(((bf16[2,32,32,1024]{3,2,0,1:T(8,128)(2,1)}), bf16[2,32,32,1024]{3,2,0,1:T(8,128)(2,1)}, u32[]{:S(2)}, u32[]{:S(2)}) %all-to-all-start) | async-done | bytes 4194336 | tf_op jit(solution)/shard_map/all_to_all | solution.py:52
  111.2 4.3 %fusion.29 = (bf16[1,32,32,1024]{3,2,0,1:T(8,128)(2,1)S(1)}, bf16[1,32,32,1024]{3,2,0,1:T(8,128)(2,1)}) fusion(bf16[2,32,32,1024]{3,2,0,1:T(8,128)(2,1)} %all-to-all-done), kind=kLoop, calls=%fused_computation.43 | loop fusion | bytes 8388608 | tf_op jit(solution)/shard_map/slice | solution.py:70
  115.5 3.8 %convolution_convert_fusion = bf16[1024,1024]{0,1:T(8,128)(2,1)} fusion(bf16[1024,1024]{1,0:T(8,128)(2,1)S(1)} %bitcast.119, bf16[1024,1024]{1,0:T(8,128)(2,1)S(1)} %copy-done.2), kind=kOutput, calls=%fused_computation.21 | convolution fusion | flops 2148532224 | bytes 6291456 | tf_op jit(solution)/shard_map/pq,spc->sqc/dot_general | solution.py:71
  119.3 6.8 %all-to-all-start.2 = ((bf16[1,32,32,1024]{3,2,0,1:T(8,128)(2,1)}), bf16[1,32,32,1024]{3,2,0,1:T(8,128)(2,1)}, u32[]{:S(2)}, u32[]{:S(2)}) async-start(bf16[1,32,32,1024]{3,2,0,1:T(8,128)(2,1)} %bitcast.115), calls=%async_computation.2 | async-start | bytes 4194304 | tf_op jit(solution)/shard_map/all_to_all | solution.py:52
  126.2 12.5 %convert_bitcast_fusion = bf16[32,32,32,32]{0,2,1,3:T(8,128)(2,1)} fusion(bf16[2,32,32,1024]{3,2,0,1:T(8,128)(2,1)} %all-to-all-done), kind=kOutput, calls=%fused_computation | convolution fusion | flops 2148532224 | bytes 6291456 | tf_op jit(solution)/shard_map/smrc,sntc->rmtn/dot_general | solution.py:79
  138.7 18.4 %copy.19 = bf16[32,32,32,32]{3,2,1,0:T(8,128)(2,1)} copy(bf16[32,32,32,32]{0,2,1,3:T(8,128)(2,1)} %convert_bitcast_fusion) | data formatting | bytes 4194304 | tf_op jit(solution)/shard_map/convert_element_type | solution.py:85
  157.1 12.4 %convert_element_type.128 = bf16[2,4,128,1024]{3,2,1,0:T(8,128)(2,1)} reshape(bf16[32,32,32,32]{3,2,1,0:T(8,128)(2,1)} %copy.19) | data formatting | bytes 4194304 | tf_op jit(solution)/shard_map/convert_element_type | solution.py:85
  169.5 2.3 dynamic-slice_bitcast_fusion.5
  171.8 1.5 collective-permute-start
  173.3 1.7 collective-permute-start.2
  175.0 1.8 collective-permute-start.1
  176.9 10.4 %collective-permute-done = bf16[2,128,1024]{2,1,0:T(8,128)(2,1)} collective-permute-done((bf16[2,128,1024]{2,1,0:T(8,128)(2,1)}, bf16[2,128,1024]{2,1,0:T(8,128)(2,1)}, u32[]{:S(2)}, u32[]{:S(2)}) %collective-permute-start) | collective-permute-done | bytes 524320 | tf_op jit(solution)/shard_map/ppermute | solution.py:41
  187.3 0.9 collective-permute-done.2
  188.2 11.3 %collective-permute-done.1 = bf16[2,128,1024]{2,1,0:T(8,128)(2,1)} collective-permute-done((bf16[2,128,1024]{2,1,0:T(8,128)(2,1)S(1)}, bf16[2,128,1024]{2,1,0:T(8,128)(2,1)}, u32[]{:S(2)}, u32[]{:S(2)}) %collective-permute-start.1) | collective-permute-done | bytes 524320 | tf_op jit(solution)/shard_map/ppermute | solution.py:41
  199.5 1.8 fusion.23
  201.4 4.6 %collective-permute-start.3 = (bf16[128,1024]{1,0:T(8,128)(2,1)S(1)}, bf16[128,1024]{1,0:T(8,128)(2,1)S(1)}, u32[]{:S(2)}, u32[]{:S(2)}) collective-permute-start(bf16[128,1024]{1,0:T(8,128)(2,1)S(1)} %fusion.25), channel_id=1, source_target_pairs={{0,128},{32,160},{64,192},{96,224},{128,0},{160,32},{192,64},{224,... | collective-permute-start | bytes 786440 | tf_op jit(solution)/shard_map/ppermute | solution.py:46
  206.0 5.3 %convert_bitcast_fusion.1 = bf16[1,1024,1024]{1,2,0:T(8,128)(2,1)} fusion(bf16[1024,1024]{1,0:T(8,128)(2,1)} %bitcast.118, bf16[1024,1024]{1,0:T(8,128)(2,1)S(1)} %copy-done.3), kind=kOutput, calls=%fused_computation.18 | convolution fusion | flops 2148532224 | bytes 6291456 | tf_op jit(solution)/shard_map/pq,sqc->spc/dot_general | solution.py:76
  211.3 1.7 collective-permute-done.3
  213.0 0.9 bitcast_add_fusion.1
  213.9 3.9 %copy.20 = bf16[1,1024,1024]{2,1,0:T(8,128)(2,1)} copy(bf16[1,1024,1024]{1,2,0:T(8,128)(2,1)} %convert_bitcast_fusion.1) | data formatting | bytes 4194304 | tf_op jit(solution)/shard_map/optimization_barrier | solution.py:86
  217.8 0.0 all-to-all-done.2
  217.8 13.3 %all-to-all-start.1 = ((bf16[1,32,32,1024]{3,2,0,1:T(8,128)(2,1)}), bf16[1,32,32,1024]{3,2,0,1:T(8,128)(2,1)}, u32[]{:S(2)}, u32[]{:S(2)}) async-start(bf16[1,32,32,1024]{3,2,0,1:T(8,128)(2,1)} %bitcast.113), calls=%async_computation.1 | async-start | bytes 4194304 | tf_op jit(solution)/shard_map/all_to_all | solution.py:52
  231.2 4.6 %fusion.12 = bf16[1024,1024]{1,0:T(8,128)(2,1)S(1)} fusion(bf16[1024,1024]{1,0:T(8,128)(2,1)} %bitcast.33, bf16[1,1024,1024]{2,1,0:T(8,128)(2,1)} %param.4), kind=kOutput, calls=%fused_computation.19 | convolution fusion | flops 2148532224 | bytes 6291456 | tf_op jit(solution)/shard_map/skc,sjc->kj/dot_general | solution.py:89
  235.7 0.1 dynamic-slice_bitcast_fusion.2
  235.9 0.7 collective-permute-start.4
  236.6 2.6 collective-permute-start.6
  239.2 0.0 collective-permute-start.5
  239.2 5.9 %convolution_bitcast_fusion = f32[1,1024,1024]{2,1,0:T(8,128)} fusion(bf16[1024,1024]{1,0:T(8,128)(2,1)} %bitcast.33, bf16[1,1024,1024]{2,1,0:T(8,128)(2,1)S(1)} %copy-done), kind=kOutput, calls=%fused_computation.9 | convolution fusion | flops 2147483648 | bytes 8388608 | tf_op jit(solution)/shard_map/kj,skc->sjc/dot_general | solution.py:91
  245.1 17.2 %collective-permute-done.4 = bf16[2,128,1024]{2,1,0:T(8,128)(2,1)S(1)} collective-permute-done((bf16[2,128,1024]{2,1,0:T(8,128)(2,1)S(1)}, bf16[2,128,1024]{2,1,0:T(8,128)(2,1)S(1)}, u32[]{:S(2)}, u32[]{:S(2)}) %collective-permute-start.4) | collective-permute-done | bytes 524320 | tf_op jit(solution)/shard_map/ppermute | solution.py:41
  262.4 0.0 collective-permute-done.6
  262.4 0.0 collective-permute-done.5
  262.4 0.3 fusion.21
  262.7 0.7 fusion.26
  263.5 3.5 %collective-permute-start.7 = (bf16[128,1024]{1,0:T(8,128)(2,1)}, bf16[128,1024]{1,0:T(8,128)(2,1)S(1)}, u32[]{:S(2)}, u32[]{:S(2)}) collective-permute-start(bf16[128,1024]{1,0:T(8,128)(2,1)} %fusion.26), channel_id=1, source_target_pairs={{0,128},{32,160},{64,192},{96,224},{128,0},{160,32},{192,64},{224,... | collective-permute-start | bytes 786440 | tf_op jit(solution)/shard_map/ppermute | solution.py:46
  267.0 23.5 %all-to-all-done.1 = bf16[1,32,32,1024]{3,2,0,1:T(8,128)(2,1)} async-done(((bf16[1,32,32,1024]{3,2,0,1:T(8,128)(2,1)}), bf16[1,32,32,1024]{3,2,0,1:T(8,128)(2,1)}, u32[]{:S(2)}, u32[]{:S(2)}) %all-to-all-start.1) | async-done | bytes 2097184 | tf_op jit(solution)/shard_map/all_to_all | solution.py:52
  290.5 7.8 %fusion.3 = (bf16[1,1024,1024]{2,1,0:T(8,128)(2,1)}, bf16[1,1024,1024]{2,1,0:T(8,128)(2,1)}) fusion(f32[1,1024,1024]{2,1,0:T(8,128)} %convolution_bitcast_fusion, bf16[1,1024,1024]{2,1,0:T(8,128)(2,1)} %bitcast.27, bf16[1,1024,1024]{2,1,0:T(8,128)(2,1)} %param.5, bf16[1,1024,1024]{2,1,0:T(8,128)(2,1)} %param.4), kind=kLoop, calls=%fused_computation.7 | loop fusion | flops 8388608 | bytes 14680064 | tf_op jit(solution)/shard_map/convert_element_type | solution.py:95
  298.3 0.0 collective-permute-done.7
  298.3 0.9 fusion.24
  (6 shorter events, 0.0 us)
Async XLA Ops:
  0.6 3.4 %copy-start = (bf16[1,1024,1024]{2,1,0:T(8,128)(2,1)S(1)}, bf16[1,1024,1024]{2,1,0:T(8,128)(2,1)}, u32[]{:S(2)}) copy-start(bf16[1,1024,1024]{2,1,0:T(8,128)(2,1)} %param.6) | copy-start | bytes 6291460
  0.6 3.5 %copy-start.1 = (bf16[1,1024,1024]{2,1,0:T(8,128)(2,1)S(1)}, bf16[1,1024,1024]{2,1,0:T(8,128)(2,1)}, u32[]{:S(2)}) copy-start(bf16[1,1024,1024]{2,1,0:T(8,128)(2,1)} %param.4) | copy-start | bytes 6291460
  8.8 102.4 %all-to-all-start = ((bf16[2,32,32,1024]{3,2,0,1:T(8,128)(2,1)}), bf16[2,32,32,1024]{3,2,0,1:T(8,128)(2,1)}, u32[]{:S(2)}, u32[]{:S(2)}) async-start(bf16[2,32,32,1024]{3,2,0,1:T(8,128)(2,1)} %pad_maximum_fusion), calls=%async_computation | async-start | bytes 8388608 | tf_op jit(solution)/shard_map/all_to_all | solution.py:52
  111.2 4.3 %copy-start.2 = (bf16[1024,1024]{1,0:T(8,128)(2,1)S(1)}, bf16[1024,1024]{1,0:T(8,128)(2,1)}, u32[]{:S(2)}) copy-start(bf16[1024,1024]{1,0:T(8,128)(2,1)} %reshape.91) | copy-start | bytes 6291460
  119.3 98.5 %all-to-all-start.2 = ((bf16[1,32,32,1024]{3,2,0,1:T(8,128)(2,1)}), bf16[1,32,32,1024]{3,2,0,1:T(8,128)(2,1)}, u32[]{:S(2)}, u32[]{:S(2)}) async-start(bf16[1,32,32,1024]{3,2,0,1:T(8,128)(2,1)} %bitcast.115), calls=%async_computation.2 | async-start | bytes 4194304 | tf_op jit(solution)/shard_map/all_to_all | solution.py:52
  171.8 15.5 %collective-permute-start = (bf16[2,128,1024]{2,1,0:T(8,128)(2,1)}, bf16[2,128,1024]{2,1,0:T(8,128)(2,1)}, u32[]{:S(2)}, u32[]{:S(2)}) collective-permute-start(bf16[2,128,1024]{2,1,0:T(8,128)(2,1)} %get-tuple-element.15), channel_id=1, source_target_pairs={{0,32},{32,64},{64,96},{96,0},{128,160},{160,192},{192,224},{224,1... | collective-permute-start | bytes 1572872 | tf_op jit(solution)/shard_map/ppermute | solution.py:41
  173.3 14.9 %collective-permute-start.2 = (bf16[2,128,1024]{2,1,0:T(8,128)(2,1)S(1)}, bf16[2,128,1024]{2,1,0:T(8,128)(2,1)}, u32[]{:S(2)}, u32[]{:S(2)}) collective-permute-start(bf16[2,128,1024]{2,1,0:T(8,128)(2,1)S(1)} %get-tuple-element.16), channel_id=1, source_target_pairs={{0,96},{32,0},{64,32},{96,64},{128,224},{160,128},{192,160},{224,1... | collective-permute-start | bytes 1572872 | tf_op jit(solution)/shard_map/ppermute | solution.py:41
  175.0 24.5 %collective-permute-start.1 = (bf16[2,128,1024]{2,1,0:T(8,128)(2,1)S(1)}, bf16[2,128,1024]{2,1,0:T(8,128)(2,1)}, u32[]{:S(2)}, u32[]{:S(2)}) collective-permute-start(bf16[2,128,1024]{2,1,0:T(8,128)(2,1)S(1)} %get-tuple-element.17), channel_id=1, source_target_pairs={{0,64},{32,96},{64,0},{96,32},{128,192},{160,224},{192,128},{224,1... | collective-permute-start | bytes 1572872 | tf_op jit(solution)/shard_map/ppermute | solution.py:41
  176.9 29.1 %copy-start.3 = (bf16[1024,1024]{1,0:T(8,128)(2,1)S(1)}, bf16[1024,1024]{1,0:T(8,128)(2,1)}, u32[]{:S(2)}) copy-start(bf16[1024,1024]{1,0:T(8,128)(2,1)} %reshape.91) | copy-start | bytes 6291460
  201.4 11.6 %collective-permute-start.3 = (bf16[128,1024]{1,0:T(8,128)(2,1)S(1)}, bf16[128,1024]{1,0:T(8,128)(2,1)S(1)}, u32[]{:S(2)}, u32[]{:S(2)}) collective-permute-start(bf16[128,1024]{1,0:T(8,128)(2,1)S(1)} %fusion.25), channel_id=1, source_target_pairs={{0,128},{32,160},{64,192},{96,224},{128,0},{160,32},{192,64},{224,... | collective-permute-start | bytes 786440 | tf_op jit(solution)/shard_map/ppermute | solution.py:46
  217.8 72.7 %all-to-all-start.1 = ((bf16[1,32,32,1024]{3,2,0,1:T(8,128)(2,1)}), bf16[1,32,32,1024]{3,2,0,1:T(8,128)(2,1)}, u32[]{:S(2)}, u32[]{:S(2)}) async-start(bf16[1,32,32,1024]{3,2,0,1:T(8,128)(2,1)} %bitcast.113), calls=%async_computation.1 | async-start | bytes 4194304 | tf_op jit(solution)/shard_map/all_to_all | solution.py:52
  235.9 26.5 %collective-permute-start.4 = (bf16[2,128,1024]{2,1,0:T(8,128)(2,1)S(1)}, bf16[2,128,1024]{2,1,0:T(8,128)(2,1)S(1)}, u32[]{:S(2)}, u32[]{:S(2)}) collective-permute-start(bf16[2,128,1024]{2,1,0:T(8,128)(2,1)S(1)} %get-tuple-element.10), channel_id=1, source_target_pairs={{0,32},{32,64},{64,96},{96,0},{128,160},{160,192},{192,224},{224,1... | collective-permute-start | bytes 1572872 | tf_op jit(solution)/shard_map/ppermute | solution.py:41
  236.6 25.7 %collective-permute-start.6 = (bf16[2,128,1024]{2,1,0:T(8,128)(2,1)S(1)}, bf16[2,128,1024]{2,1,0:T(8,128)(2,1)S(1)}, u32[]{:S(2)}, u32[]{:S(2)}) collective-permute-start(bf16[2,128,1024]{2,1,0:T(8,128)(2,1)S(1)} %get-tuple-element.11), channel_id=1, source_target_pairs={{0,96},{32,0},{64,32},{96,64},{128,224},{160,128},{192,160},{224,1... | collective-permute-start | bytes 1572872 | tf_op jit(solution)/shard_map/ppermute | solution.py:41
  239.2 23.2 %collective-permute-start.5 = (bf16[2,128,1024]{2,1,0:T(8,128)(2,1)S(1)}, bf16[2,128,1024]{2,1,0:T(8,128)(2,1)S(1)}, u32[]{:S(2)}, u32[]{:S(2)}) collective-permute-start(bf16[2,128,1024]{2,1,0:T(8,128)(2,1)S(1)} %get-tuple-element.12), channel_id=1, source_target_pairs={{0,64},{32,96},{64,0},{96,32},{128,192},{160,224},{192,128},{224,1... | collective-permute-start | bytes 1572872 | tf_op jit(solution)/shard_map/ppermute | solution.py:41
  263.5 34.8 %collective-permute-start.7 = (bf16[128,1024]{1,0:T(8,128)(2,1)}, bf16[128,1024]{1,0:T(8,128)(2,1)S(1)}, u32[]{:S(2)}, u32[]{:S(2)}) collective-permute-start(bf16[128,1024]{1,0:T(8,128)(2,1)} %fusion.26), channel_id=1, source_target_pairs={{0,128},{32,160},{64,192},{96,224},{128,0},{160,32},{192,64},{224,... | collective-permute-start | bytes 786440 | tf_op jit(solution)/shard_map/ppermute | solution.py:46

commit v7 on v5

--- a/solution.py
+++ b/solution.py
@@ -25,7 +25,38 @@
     return ring
 
 
-def _dp_reduce(part, ring):
+def _z_relays(mesh, ring):
+    devs = np.asarray(mesh.devices)
+    if tuple(mesh.axis_names) != ("dp", "seq") or devs.shape[0] != 2 * ring:
+        return None
+    try:
+        where = {}
+        for d in range(devs.shape[0]):
+            for q in range(devs.shape[1]):
+                dev = devs[d, q]
+                where[tuple(dev.coords) + (dev.core_on_chip,)] = d * devs.shape[1] + q
+        nz = 1 + max(k[2] for k in where)
+        half = nz // 2
+        for d in range(devs.shape[0]):
+            for q in range(devs.shape[1]):
+                a, b = devs[d, q], devs[(d + ring) % devs.shape[0], q]
+                ca, cb = tuple(a.coords), tuple(b.coords)
+                if ca[:2] != cb[:2] or a.core_on_chip != b.core_on_chip or (cb[2] - ca[2]) % nz != half:
+                    return None
+
+        def shift(step):
+            out = []
+            for k, i in where.items():
+                t = (k[0], k[1], (k[2] + step) % nz, k[3])
+                out.append((i, where[t]))
+            return out
+
+        return (shift(1), shift(half - 1), shift(-1), shift(1 - half))
+    except Exception:
+        return None
+
+
+def _dp_reduce(part, ring, relays=None):
     ndp = lax.axis_size("dp")
     groups = ndp // ring
     rows = part.shape[0] // ndp
@@ -40,6 +71,14 @@
         perm = [(g * ring + t, g * ring + (t + s) % ring) for g in range(groups) for t in range(ring)]
         acc = acc + lax.ppermute(piece, "dp", perm).astype(jnp.float32)
     own = lax.dynamic_index_in_dim(acc, hi, axis=0, keepdims=False)
+    if relays is not None and groups == 2:
+        piece = lax.dynamic_index_in_dim(acc, 1 - hi, axis=0, keepdims=False).astype(jnp.bfloat16)
+        cut = rows // 2
+        up = lax.ppermute(piece[:cut], ("dp", "seq"), relays[0])
+        up = lax.ppermute(up, ("dp", "seq"), relays[1])
+        down = lax.ppermute(piece[cut:], ("dp", "seq"), relays[2])
+        down = lax.ppermute(down, ("dp", "seq"), relays[3])
+        return own + jnp.concatenate([up, down]).astype(jnp.float32)
     for s in range(1, groups):
         piece = lax.dynamic_index_in_dim(acc, (hi + s) % groups, axis=0, keepdims=False)
         perm = [(g * ring + t, ((g + s) % groups) * ring + t) for g in range(groups) for t in range(ring)]
@@ -57,13 +96,21 @@
 
 def _from_moved(data, count, rows):
     seqs, block, width = data.shape
-    out = lax.all_to_all(
-        data.reshape(seqs, 1, rows, count, width), "seq", split_axis=3, concat_axis=1, tiled=True
-    )
-    return out.reshape(seqs, block, width)
+    return _from_sendbuf(_sendbuf(data, count, rows), count)
 
 
-def local(inputs, cotangent, factor_one, factor_two, ring):
+def _sendbuf(data, count, rows):
+    seqs, block, width = data.shape
+    return jnp.swapaxes(data.reshape(seqs, rows, count, width), 1, 2)
+
+
+def _from_sendbuf(buf, count):
+    seqs, _, rows, width = buf.shape
+    out = lax.all_to_all(buf, "seq", split_axis=1, concat_axis=1, tiled=True)
+    return out.reshape(seqs, count * rows, width)
+
+
+def local(inputs, cotangent, factor_one, factor_two, ring, relays):
     seqs, block, width = inputs.shape
     count = lax.axis_size("seq")
     rows = block // count
@@ -88,11 +135,12 @@
         jnp.bfloat16
     )
     part_two = jnp.einsum("spc,sqc->pq", gated_moved, moved, preferred_element_type=jnp.float32)
-    grad_two = _dp_reduce(part_two.astype(jnp.bfloat16), ring)
-    second, grad_two = lax.optimization_barrier((second, grad_two))
-    monarch = _from_moved(second, count, rows)
+    grad_two = _dp_reduce(part_two.astype(jnp.bfloat16), ring, relays)
+    second = _sendbuf(second, count, rows)
+    second, back_moved, grad_two = lax.optimization_barrier((second, back_moved, grad_two))
+    monarch = _from_sendbuf(second, count)
     part_one = jnp.einsum("skc,sjc->kj", back_moved, inputs, preferred_element_type=jnp.float32)
-    grad_one = _dp_reduce(part_one.astype(jnp.bfloat16), ring)
+    grad_one = _dp_reduce(part_one.astype(jnp.bfloat16), ring, relays)
     spread = _rowmajor(jnp.einsum("kj,skc->sjc", fone, back_moved, preferred_element_type=jnp.float32))
     spread = lax.optimization_barrier(spread)
     mfull = monarch.astype(jnp.float32)
@@ -103,6 +151,7 @@
 
 def solution(mesh):
     ring = _dp_rings(mesh)
+    relays = _z_relays(mesh, ring)
     in_specs = (
         P("dp", "seq", None),
         P("dp", "seq", None),
@@ -115,5 +164,5 @@
         P("seq", "dp", None),
         P("seq", "dp", None),
     )
-    body = lambda a, b, c, d: local(a, b, c, d, ring)
+    body = lambda a, b, c, d: local(a, b, c, d, ring, relays)
     return jax.shard_map(body, mesh=mesh, in_specs=in_specs, out_specs=out_specs, check_vma=False)

time: 264 us -> 276 us (1.045)
  starting transfers between devices: 33.8 us -> 61.5 us
  waiting for transfers between devices: 71.3 us -> 59.3 us
  local copies, waits for them, and re-layouts: 14.7 us -> 11.8 us
    ppermute x2 -> x8, starting transfers between devices: 7.72 us -> 35.4 us  [the longest x2 20.4 us: _dp_reduce(): down = lax.ppermute(down, ('dp', 'seq'), relays[3])]
    all_to_all x2, waiting for transfers between devices: 18.1 us -> 0.01 us  [_from_sendbuf(): out = lax.all_to_all(buf, 'seq', split_axis=1, concat_axis=1, tiled=True)]
    ppermute x2 -> x8, waiting for transfers between devices: 7.9 us -> 14.3 us  [the longest x2 8.5 us: _dp_reduce(): down = lax.ppermute(down, ('dp', 'seq'), relays[3])]
    optimization_barrier x1 -> x0, local copies, waits for them, and re-layouts: 2.85 us -> none  [local(): second, grad_two = lax.optimization_barrier((second, grad_two))]
  transfers between devices with their start and end apart: 10 -> 16, of which waited for: 10 -> 10; matrix products, arithmetic and copies ran while one was open for 11% -> 10% of each run, Pallas kernels for 0% -> 0%
where the time goes in v7:
time: 276 us; the launch traced here: 274 us
  blocking collectives  102 us (37%)
  starting transfers between devices  61.5 us (22%)
  waiting for transfers between devices  59.3 us (21%)
  matrix products  23.9 us (9%)
  other arithmetic  15.5 us (6%)
  local copies, waits for them, and re-layouts  11.8 us (4%)
    all_to_all x1, blocking collectives, local(): in1 = lax.all_to_all(out1, 'seq', split_axis=1, concat_axis=3, tiled=True)  102 us
    ppermute x6, waiting for transfers between devices, _dp_reduce(): acc = acc + lax.ppermute(piece, 'dp', perm).astype(jnp.float32)  45 us
    ppermute x2, starting transfers between devices, _dp_reduce(): down = lax.ppermute(down, ('dp', 'seq'), relays[3])  20.4 us
    all_to_all x2, starting transfers between devices, _from_sendbuf(): out = lax.all_to_all(buf, 'seq', split_axis=1, concat_axis=1, tiled=True)  16 us
    ppermute x6, starting transfers between devices, _dp_reduce(): acc = acc + lax.ppermute(piece, 'dp', perm).astype(jnp.float32)  10.2 us
    ppermute x2, waiting for transfers between devices, _dp_reduce(): down = lax.ppermute(down, ('dp', 'seq'), relays[3])  8.5 us
    convert_element_type x1, other arithmetic, local(): grad_input = _rowmajor((dyfull * mfull + spread).astype(jnp.bfloat16))  7.82 us
    ppermute x2, starting transfers between devices, _dp_reduce(): up = lax.ppermute(up, ('dp', 'seq'), relays[1])  6.6 us
  transfers between devices with their start and end apart: 16, of which 10 were waited for; matrix products, arithmetic and copies ran while one was open for 10% of the time, Pallas kernels for 0%

profile of v7, /device:TPU:8, one launch (start us, length us, event | category | flops | bytes accessed | tf_op | source)
XLA Modules:
  0.0 274.5 jit_solution(9089810852601414104)
XLA Ops:
  0.7 3.4 %fusion = bf16[1,1024,1024]{2,1,0:T(8,128)(2,1)S(1)} fusion(bf16[1,1024,1024]{2,1,0:T(8,128)(2,1)} %param.4, bf16[1,1024,1024]{2,1,0:T(8,128)(2,1)} %param.5), kind=kLoop, calls=%fused_computation.3 | loop fusion | flops 4194304 | bytes 6291456 | tf_op jit(solution)/shard_map/convert_element_type | solution.py:121
  4.0 0.2 copy-done.4
  4.3 2.3 fusion.16
  6.6 0.4 pad_maximum_fusion
  7.0 101.7 %all_to_all.25 = bf16[2,32,32,1,1024]{4,2,0,3,1:T(8,128)(2,1)S(1)} all-to-all(bf16[2,32,32,1,1024]{4,2,0,3,1:T(8,128)(2,1)S(1)} %pad_maximum_fusion), channel_id=1, replica_groups=mesh['dp'=8,'seq'=32] {'seq'}, dimensions={1} | all-to-all | bytes 8388608 | tf_op jit(solution)/shard_map/all_to_all | solution.py:126
  108.7 2.3 copy.29
  111.0 1.8 fusion.36
  112.8 2.5 fusion.24
  115.2 2.5 copy.30
  117.7 7.2 %all-to-all-start.1 = ((bf16[1,32,32,1024]{3,2,0,1:T(8,128)(2,1)}), bf16[1,32,32,1024]{3,2,0,1:T(8,128)(2,1)}, u32[]{:S(2)}, u32[]{:S(2)}) async-start(bf16[1,32,32,1024]{3,2,0,1:T(8,128)(2,1)} %bitcast.114), calls=%async_computation.1 | async-start | bytes 4194304 | tf_op jit(solution)/shard_map/all_to_all | solution.py:109
  125.0 4.6 %convolution_convert_fusion = bf16[1024,1024]{1,0:T(8,128)(2,1)S(1)} fusion(bf16[1024,1024]{1,0:T(8,128)(2,1)} %bitcast.126, bf16[1024,1024]{1,0:T(8,128)(2,1)} %bitcast.123), kind=kOutput, calls=%fused_computation.28 | convolution fusion | flops 2148532224 | bytes 6291456 | tf_op jit(solution)/shard_map/spc,sqc->pq/dot_general | solution.py:137
  129.6 1.3 copy-done.2
  130.9 0.9 dynamic-slice_bitcast_fusion.5
  131.8 1.5 collective-permute-start
  133.3 1.7 collective-permute-start.2
  135.1 1.8 collective-permute-start.1
  136.9 10.4 %collective-permute-done = bf16[2,128,1024]{2,1,0:T(8,128)(2,1)} collective-permute-done((bf16[2,128,1024]{2,1,0:T(8,128)(2,1)}, bf16[2,128,1024]{2,1,0:T(8,128)(2,1)}, u32[]{:S(2)}, u32[]{:S(2)}) %collective-permute-start) | collective-permute-done | bytes 524320 | tf_op jit(solution)/shard_map/ppermute | solution.py:72
  147.3 10.2 %collective-permute-done.2 = bf16[2,128,1024]{2,1,0:T(8,128)(2,1)} collective-permute-done((bf16[2,128,1024]{2,1,0:T(8,128)(2,1)S(1)}, bf16[2,128,1024]{2,1,0:T(8,128)(2,1)}, u32[]{:S(2)}, u32[]{:S(2)}) %collective-permute-start.2) | collective-permute-done | bytes 524320 | tf_op jit(solution)/shard_map/ppermute | solution.py:72
  157.5 2.0 collective-permute-done.1
  159.5 1.8 fusion.35
  161.5 1.6 collective-permute-start.3
  163.0 3.1 %collective-permute-start.5 = (bf16[64,1024]{1,0:T(8,128)(2,1)S(1)}, bf16[64,1024]{1,0:T(8,128)(2,1)}, u32[]{:S(2)}, u32[]{:S(2)}) collective-permute-start(bf16[64,1024]{1,0:T(8,128)(2,1)S(1)} %get-tuple-element.23), channel_id=1, source_target_pairs={{0,134},{1,135},{2,0},{3,1},{4,2},{5,3},{6,4},{7,5},{8,142},{9,143... | collective-permute-start | bytes 393224 | tf_op jit(solution)/shard_map/ppermute | solution.py:79
  166.2 2.9 %collective-permute-done.3 = bf16[64,1024]{1,0:T(8,128)(2,1)S(1)} collective-permute-done((bf16[64,1024]{1,0:T(8,128)(2,1)S(1)}, bf16[64,1024]{1,0:T(8,128)(2,1)S(1)}, u32[]{:S(2)}, u32[]{:S(2)}) %collective-permute-start.3) | collective-permute-done | bytes 131104 | tf_op jit(solution)/shard_map/ppermute | solution.py:77
  169.0 2.4 collective-permute-start.4
  171.4 9.1 %collective-permute-start.6 = (bf16[64,1024]{1,0:T(8,128)(2,1)}, bf16[64,1024]{1,0:T(8,128)(2,1)S(1)}, u32[]{:S(2)}, u32[]{:S(2)}) collective-permute-start(bf16[64,1024]{1,0:T(8,128)(2,1)} %collective-permute-done.5), channel_id=1, source_target_pairs={{0,130},{1,131},{2,132},{3,133},{4,134},{5,135},{6,0},{7,1},{8,138... | collective-permute-start | bytes 393224 | tf_op jit(solution)/shard_map/ppermute | solution.py:80
  180.6 3.9 %fusion.21 = bf16[1024,1024]{0,1:T(8,128)(2,1)S(1)} fusion(bf16[1024,1024]{1,0:T(8,128)(2,1)} %bitcast.124, bf16[1,1024,1024]{2,1,0:T(8,128)(2,1)S(1)} %copy-done), kind=kOutput, calls=%fused_computation.25 | convolution fusion | flops 2148532224 | bytes 6291456 | tf_op jit(solution)/shard_map/pq,sqc->spc/dot_general | solution.py:134
  184.5 2.5 copy.31
  187.0 3.6 %collective-permute-done.6 = bf16[64,1024]{1,0:T(8,128)(2,1)S(1)} collective-permute-done((bf16[64,1024]{1,0:T(8,128)(2,1)}, bf16[64,1024]{1,0:T(8,128)(2,1)S(1)}, u32[]{:S(2)}, u32[]{:S(2)}) %collective-permute-start.6) | collective-permute-done | bytes 131104 | tf_op jit(solution)/shard_map/ppermute | solution.py:80
  190.6 0.9 bitcast_add_fusion
  191.5 8.8 %all-to-all-start.2 = ((bf16[1,32,32,1024]{3,2,0,1:T(8,128)(2,1)}), bf16[1,32,32,1024]{3,2,0,1:T(8,128)(2,1)}, u32[]{:S(2)}, u32[]{:S(2)}) async-start(bf16[1,32,32,1024]{3,2,0,1:T(8,128)(2,1)} %bitcast.115), calls=%async_computation.2 | async-start | bytes 4194304 | tf_op jit(solution)/shard_map/all_to_all | solution.py:109
  200.3 4.6 %fusion.27 = bf16[1024,1024]{1,0:T(8,128)(2,1)S(1)} fusion(bf16[1,1024,1024]{2,1,0:T(8,128)(2,1)} %param.4, bf16[1,1024,1024]{2,1,0:T(8,128)(2,1)} %bitcast.22), kind=kOutput, calls=%fused_computation.27 | convolution fusion | flops 2148532224 | bytes 6291456 | tf_op jit(solution)/shard_map/skc,sjc->kj/dot_general | solution.py:142
  204.9 0.1 dynamic-slice_bitcast_fusion.2
  205.0 1.6 collective-permute-start.7
  206.6 1.7 collective-permute-start.9
  208.3 1.8 collective-permute-start.8
  210.1 10.1 %collective-permute-done.7 = bf16[2,128,1024]{2,1,0:T(8,128)(2,1)S(1)} collective-permute-done((bf16[2,128,1024]{2,1,0:T(8,128)(2,1)S(1)}, bf16[2,128,1024]{2,1,0:T(8,128)(2,1)S(1)}, u32[]{:S(2)}, u32[]{:S(2)}) %collective-permute-start.7) | collective-permute-done | bytes 524320 | tf_op jit(solution)/shard_map/ppermute | solution.py:72
  220.2 1.1 collective-permute-done.9
  221.4 11.1 %collective-permute-done.8 = bf16[2,128,1024]{2,1,0:T(8,128)(2,1)S(1)} collective-permute-done((bf16[2,128,1024]{2,1,0:T(8,128)(2,1)S(1)}, bf16[2,128,1024]{2,1,0:T(8,128)(2,1)S(1)}, u32[]{:S(2)}, u32[]{:S(2)}) %collective-permute-start.8) | collective-permute-done | bytes 524320 | tf_op jit(solution)/shard_map/ppermute | solution.py:72
  232.5 0.3 fusion.33
  232.9 1.5 collective-permute-start.10
  234.4 2.1 collective-permute-start.12
  236.5 2.9 %collective-permute-done.10 = bf16[64,1024]{1,0:T(8,128)(2,1)S(1)} collective-permute-done((bf16[64,1024]{1,0:T(8,128)(2,1)S(1)}, bf16[64,1024]{1,0:T(8,128)(2,1)S(1)}, u32[]{:S(2)}, u32[]{:S(2)}) %collective-permute-start.10) | collective-permute-done | bytes 131104 | tf_op jit(solution)/shard_map/ppermute | solution.py:77
  239.4 4.2 %collective-permute-start.11 = (bf16[64,1024]{1,0:T(8,128)(2,1)S(1)}, bf16[64,1024]{1,0:T(8,128)(2,1)S(1)}, u32[]{:S(2)}, u32[]{:S(2)}) collective-permute-start(bf16[64,1024]{1,0:T(8,128)(2,1)S(1)} %collective-permute-done.10), channel_id=1, source_target_pairs={{0,6},{1,7},{2,128},{3,129},{4,130},{5,131},{6,132},{7,133},{8,14}... | collective-permute-start | bytes 393224 | tf_op jit(solution)/shard_map/ppermute | solution.py:78
  243.6 11.3 %collective-permute-start.13 = (bf16[64,1024]{1,0:T(8,128)(2,1)S(1)}, bf16[64,1024]{1,0:T(8,128)(2,1)S(1)}, u32[]{:S(2)}, u32[]{:S(2)}) collective-permute-start(bf16[64,1024]{1,0:T(8,128)(2,1)S(1)} %collective-permute-done.12), channel_id=1, source_target_pairs={{0,130},{1,131},{2,132},{3,133},{4,134},{5,135},{6,0},{7,1},{8,138... | collective-permute-start | bytes 393224 | tf_op jit(solution)/shard_map/ppermute | solution.py:80
  254.9 6.0 %convolution_bitcast_fusion = f32[1,1024,1024]{2,1,0:T(8,128)} fusion(bf16[1,1024,1024]{2,1,0:T(8,128)(2,1)} %bitcast.22, bf16[1,1024,1024]{2,1,0:T(8,128)(2,1)S(1)} %copy-done.5), kind=kOutput, calls=%fused_computation.9 | convolution fusion | flops 2147483648 | bytes 8388608 | tf_op jit(solution)/shard_map/kj,skc->sjc/dot_general | solution.py:144
  260.9 4.9 %collective-permute-done.13 = bf16[64,1024]{1,0:T(8,128)(2,1)S(1)} collective-permute-done((bf16[64,1024]{1,0:T(8,128)(2,1)S(1)}, bf16[64,1024]{1,0:T(8,128)(2,1)S(1)}, u32[]{:S(2)}, u32[]{:S(2)}) %collective-permute-start.13) | collective-permute-done | bytes 131104 | tf_op jit(solution)/shard_map/ppermute | solution.py:80
  265.8 0.9 convert_add_fusion.2
  266.6 7.8 %fusion.3 = (bf16[1,1024,1024]{2,1,0:T(8,128)(2,1)}, bf16[1,1024,1024]{2,1,0:T(8,128)(2,1)}) fusion(f32[1,1024,1024]{2,1,0:T(8,128)} %convolution_bitcast_fusion, bf16[1,1024,1024]{2,1,0:T(8,128)(2,1)} %bitcast.32, bf16[1,1024,1024]{2,1,0:T(8,128)(2,1)} %param.5, bf16[1,1024,1024]{2,1,0:T(8,128)(2,1)} %param.4), kind=kLoop, calls=%fused_computation.6 | loop fusion | flops 8388608 | bytes 14680064 | tf_op jit(solution)/shard_map/convert_element_type | solution.py:148
  (20 shorter events, 0.2 us)
Async XLA Ops:
  0.6 112.1 %copy-start = (bf16[1,1024,1024]{2,1,0:T(8,128)(2,1)S(1)}, bf16[1,1024,1024]{2,1,0:T(8,128)(2,1)}, u32[]{:S(2)}) copy-start(bf16[1,1024,1024]{2,1,0:T(8,128)(2,1)} %param.7) | copy-start | bytes 6291460
  0.6 3.4 %copy-start.1 = (bf16[1,1024,1024]{2,1,0:T(8,128)(2,1)S(1)}, bf16[1,1024,1024]{2,1,0:T(8,128)(2,1)}, u32[]{:S(2)}) copy-start(bf16[1,1024,1024]{2,1,0:T(8,128)(2,1)} %param.4) | copy-start | bytes 6291460
  0.7 3.6 %copy-start.4 = (bf16[1,1024,1024]{2,1,0:T(8,128)(2,1)S(1)}, bf16[1,1024,1024]{2,1,0:T(8,128)(2,1)}, u32[]{:S(2)}) copy-start(bf16[1,1024,1024]{2,1,0:T(8,128)(2,1)} %param.6) | copy-start | bytes 6291460
  112.8 2.5 copy-start.3
  117.7 73.7 %all-to-all-start.1 = ((bf16[1,32,32,1024]{3,2,0,1:T(8,128)(2,1)}), bf16[1,32,32,1024]{3,2,0,1:T(8,128)(2,1)}, u32[]{:S(2)}, u32[]{:S(2)}) async-start(bf16[1,32,32,1024]{3,2,0,1:T(8,128)(2,1)} %bitcast.114), calls=%async_computation.1 | async-start | bytes 4194304 | tf_op jit(solution)/shard_map/all_to_all | solution.py:109
  129.6 1.3 copy-start.2
  131.8 15.5 %collective-permute-start = (bf16[2,128,1024]{2,1,0:T(8,128)(2,1)}, bf16[2,128,1024]{2,1,0:T(8,128)(2,1)}, u32[]{:S(2)}, u32[]{:S(2)}) collective-permute-start(bf16[2,128,1024]{2,1,0:T(8,128)(2,1)} %get-tuple-element.17), channel_id=1, source_target_pairs={{0,32},{32,64},{64,96},{96,0},{128,160},{160,192},{192,224},{224,1... | collective-permute-start | bytes 1572872 | tf_op jit(solution)/shard_map/ppermute | solution.py:72
  133.3 24.2 %collective-permute-start.2 = (bf16[2,128,1024]{2,1,0:T(8,128)(2,1)S(1)}, bf16[2,128,1024]{2,1,0:T(8,128)(2,1)}, u32[]{:S(2)}, u32[]{:S(2)}) collective-permute-start(bf16[2,128,1024]{2,1,0:T(8,128)(2,1)S(1)} %get-tuple-element.18), channel_id=1, source_target_pairs={{0,96},{32,0},{64,32},{96,64},{128,224},{160,128},{192,160},{224,1... | collective-permute-start | bytes 1572872 | tf_op jit(solution)/shard_map/ppermute | solution.py:72
  135.1 24.5 %collective-permute-start.1 = (bf16[2,128,1024]{2,1,0:T(8,128)(2,1)S(1)}, bf16[2,128,1024]{2,1,0:T(8,128)(2,1)}, u32[]{:S(2)}, u32[]{:S(2)}) collective-permute-start(bf16[2,128,1024]{2,1,0:T(8,128)(2,1)S(1)} %get-tuple-element.19), channel_id=1, source_target_pairs={{0,64},{32,96},{64,0},{96,32},{128,192},{160,224},{192,128},{224,1... | collective-permute-start | bytes 1572872 | tf_op jit(solution)/shard_map/ppermute | solution.py:72
  161.5 7.6 %collective-permute-start.3 = (bf16[64,1024]{1,0:T(8,128)(2,1)S(1)}, bf16[64,1024]{1,0:T(8,128)(2,1)S(1)}, u32[]{:S(2)}, u32[]{:S(2)}) collective-permute-start(bf16[64,1024]{1,0:T(8,128)(2,1)S(1)} %get-tuple-element.22), channel_id=1, source_target_pairs={{0,2},{1,3},{2,4},{3,5},{4,6},{5,7},{6,128},{7,129},{8,10},{9,11},... | collective-permute-start | bytes 393224 | tf_op jit(solution)/shard_map/ppermute | solution.py:77
  163.0 8.4 %collective-permute-start.5 = (bf16[64,1024]{1,0:T(8,128)(2,1)S(1)}, bf16[64,1024]{1,0:T(8,128)(2,1)}, u32[]{:S(2)}, u32[]{:S(2)}) collective-permute-start(bf16[64,1024]{1,0:T(8,128)(2,1)S(1)} %get-tuple-element.23), channel_id=1, source_target_pairs={{0,134},{1,135},{2,0},{3,1},{4,2},{5,3},{6,4},{7,5},{8,142},{9,143... | collective-permute-start | bytes 393224 | tf_op jit(solution)/shard_map/ppermute | solution.py:79
  169.0 17.9 %collective-permute-start.4 = (bf16[64,1024]{1,0:T(8,128)(2,1)S(1)}, bf16[64,1024]{1,0:T(8,128)(2,1)S(1)}, u32[]{:S(2)}, u32[]{:S(2)}) collective-permute-start(bf16[64,1024]{1,0:T(8,128)(2,1)S(1)} %collective-permute-done.3), channel_id=1, source_target_pairs={{0,6},{1,7},{2,128},{3,129},{4,130},{5,131},{6,132},{7,133},{8,14}... | collective-permute-start | bytes 393224 | tf_op jit(solution)/shard_map/ppermute | solution.py:78
  171.4 19.2 %collective-permute-start.6 = (bf16[64,1024]{1,0:T(8,128)(2,1)}, bf16[64,1024]{1,0:T(8,128)(2,1)S(1)}, u32[]{:S(2)}, u32[]{:S(2)}) collective-permute-start(bf16[64,1024]{1,0:T(8,128)(2,1)} %collective-permute-done.5), channel_id=1, source_target_pairs={{0,130},{1,131},{2,132},{3,133},{4,134},{5,135},{6,0},{7,1},{8,138... | collective-permute-start | bytes 393224 | tf_op jit(solution)/shard_map/ppermute | solution.py:80
  191.5 75.2 %all-to-all-start.2 = ((bf16[1,32,32,1024]{3,2,0,1:T(8,128)(2,1)}), bf16[1,32,32,1024]{3,2,0,1:T(8,128)(2,1)}, u32[]{:S(2)}, u32[]{:S(2)}) async-start(bf16[1,32,32,1024]{3,2,0,1:T(8,128)(2,1)} %bitcast.115), calls=%async_computation.2 | async-start | bytes 4194304 | tf_op jit(solution)/shard_map/all_to_all | solution.py:109
  205.0 15.2 %collective-permute-start.7 = (bf16[2,128,1024]{2,1,0:T(8,128)(2,1)S(1)}, bf16[2,128,1024]{2,1,0:T(8,128)(2,1)S(1)}, u32[]{:S(2)}, u32[]{:S(2)}) collective-permute-start(bf16[2,128,1024]{2,1,0:T(8,128)(2,1)S(1)} %get-tuple-element.12), channel_id=1, source_target_pairs={{0,32},{32,64},{64,96},{96,0},{128,160},{160,192},{192,224},{224,1... | collective-permute-start | bytes 1572872 | tf_op jit(solution)/shard_map/ppermute | solution.py:72
  206.6 14.8 %collective-permute-start.9 = (bf16[2,128,1024]{2,1,0:T(8,128)(2,1)S(1)}, bf16[2,128,1024]{2,1,0:T(8,128)(2,1)S(1)}, u32[]{:S(2)}, u32[]{:S(2)}) collective-permute-start(bf16[2,128,1024]{2,1,0:T(8,128)(2,1)S(1)} %get-tuple-element.13), channel_id=1, source_target_pairs={{0,96},{32,0},{64,32},{96,64},{128,224},{160,128},{192,160},{224,1... | collective-permute-start | bytes 1572872 | tf_op jit(solution)/shard_map/ppermute | solution.py:72
  208.3 46.6 %copy-start.5 = (bf16[1,1024,1024]{2,1,0:T(8,128)(2,1)S(1)}, bf16[1,1024,1024]{2,1,0:T(8,128)(2,1)}, u32[]{:S(2)}) copy-start(bf16[1,1024,1024]{2,1,0:T(8,128)(2,1)} %param.6) | copy-start | bytes 6291460
  208.3 24.1 %collective-permute-start.8 = (bf16[2,128,1024]{2,1,0:T(8,128)(2,1)S(1)}, bf16[2,128,1024]{2,1,0:T(8,128)(2,1)S(1)}, u32[]{:S(2)}, u32[]{:S(2)}) collective-permute-start(bf16[2,128,1024]{2,1,0:T(8,128)(2,1)S(1)} %get-tuple-element.14), channel_id=1, source_target_pairs={{0,64},{32,96},{64,0},{96,32},{128,192},{160,224},{192,128},{224,1... | collective-permute-start | bytes 1572872 | tf_op jit(solution)/shard_map/ppermute | solution.py:72
  232.9 6.6 %collective-permute-start.10 = (bf16[64,1024]{1,0:T(8,128)(2,1)S(1)}, bf16[64,1024]{1,0:T(8,128)(2,1)S(1)}, u32[]{:S(2)}, u32[]{:S(2)}) collective-permute-start(bf16[64,1024]{1,0:T(8,128)(2,1)S(1)} %get-tuple-element.20), channel_id=1, source_target_pairs={{0,2},{1,3},{2,4},{3,5},{4,6},{5,7},{6,128},{7,129},{8,10},{9,11},... | collective-permute-start | bytes 393224 | tf_op jit(solution)/shard_map/ppermute | solution.py:77
  234.4 9.2 %collective-permute-start.12 = (bf16[64,1024]{1,0:T(8,128)(2,1)S(1)}, bf16[64,1024]{1,0:T(8,128)(2,1)S(1)}, u32[]{:S(2)}, u32[]{:S(2)}) collective-permute-start(bf16[64,1024]{1,0:T(8,128)(2,1)S(1)} %get-tuple-element.21), channel_id=1, source_target_pairs={{0,134},{1,135},{2,0},{3,1},{4,2},{5,3},{6,4},{7,5},{8,142},{9,143... | collective-permute-start | bytes 393224 | tf_op jit(solution)/shard_map/ppermute | solution.py:79
  239.4 21.5 %collective-permute-start.11 = (bf16[64,1024]{1,0:T(8,128)(2,1)S(1)}, bf16[64,1024]{1,0:T(8,128)(2,1)S(1)}, u32[]{:S(2)}, u32[]{:S(2)}) collective-permute-start(bf16[64,1024]{1,0:T(8,128)(2,1)S(1)} %collective-permute-done.10), channel_id=1, source_target_pairs={{0,6},{1,7},{2,128},{3,129},{4,130},{5,131},{6,132},{7,133},{8,14}... | collective-permute-start | bytes 393224 | tf_op jit(solution)/shard_map/ppermute | solution.py:78
  243.6 22.1 %collective-permute-start.13 = (bf16[64,1024]{1,0:T(8,128)(2,1)S(1)}, bf16[64,1024]{1,0:T(8,128)(2,1)S(1)}, u32[]{:S(2)}, u32[]{:S(2)}) collective-permute-start(bf16[64,1024]{1,0:T(8,128)(2,1)S(1)} %collective-permute-done.12), channel_id=1, source_target_pairs={{0,130},{1,131},{2,132},{3,133},{4,134},{5,135},{6,0},{7,1},{8,138... | collective-permute-start | bytes 393224 | tf_op jit(solution)/shard_map/ppermute | solution.py:80

commit v8 on v6

--- a/solution.py
+++ b/solution.py
@@ -57,7 +57,10 @@
     count = lax.axis_size("seq")
     rows = block // count
     fone = factor_one[0]
-    ftwo = factor_two[0].reshape(rows, count, rows, count).transpose(1, 0, 3, 2).reshape(block, block)
+    pp = jnp.arange(block)
+    pick = (pp[None, :] == ((pp % rows) * count + pp // rows)[:, None]).astype(jnp.bfloat16)
+    ftwo = jnp.dot(pick, factor_two[0], preferred_element_type=jnp.float32).astype(jnp.bfloat16)
+    ftwo = jnp.dot(ftwo, pick.T, preferred_element_type=jnp.float32).astype(jnp.bfloat16)
     xfull = inputs.astype(jnp.float32)
     dyfull = cotangent.astype(jnp.float32)
     gated = _rowmajor((dyfull * xfull).astype(jnp.bfloat16))
@@ -76,12 +79,9 @@
     second = jnp.einsum("pq,sqc->spc", ftwo, moved, preferred_element_type=jnp.float32).astype(
         jnp.bfloat16
     )
-    part_two = jnp.einsum(
-        "smrc,sntc->rmtn",
-        gated_moved.reshape(seqs, count, rows, width),
-        moved.reshape(seqs, count, rows, width),
-        preferred_element_type=jnp.float32,
-    ).reshape(block, block)
+    part_two = jnp.einsum("spc,sqc->pq", gated_moved, moved, preferred_element_type=jnp.float32)
+    part_two = jnp.dot(pick.T, part_two.astype(jnp.bfloat16), preferred_element_type=jnp.float32)
+    part_two = jnp.dot(part_two.astype(jnp.bfloat16), pick, preferred_element_type=jnp.float32)
     grad_two = _dp_reduce(part_two.astype(jnp.bfloat16), ring)
     second, grad_two = lax.optimization_barrier((second, grad_two))
     monarch = _exchange(second.reshape(seqs, count, rows, width), count)

time: 304 us -> 273 us (0.90)
  local copies, waits for them, and re-layouts: 77.7 us -> 11.6 us
  waiting for transfers between devices: 123 us -> 151 us
  matrix products: 34.5 us -> 43 us
    convert_element_type x2 -> x0, local copies, waits for them, and re-layouts: 30.8 us -> none  [local(): grad_two = _dp_reduce(part_two.astype(jnp.bfloat16), ring)]
    all_to_all x3, waiting for transfers between devices: 81.4 us -> 109 us  [_exchange(): lax.all_to_all(data, 'seq', split_axis=axis, concat_axis=axis, tiled=True)]
    another operation x2 -> x0, local copies, waits for them, and re-layouts: 22.9 us -> none  [local(): factor_two[0].reshape(rows, count, rows, count).transpose(1, 0, 3, 2)]
    reshape x1 -> x0, local copies, waits for them, and re-layouts: 12.4 us -> none  [local(): factor_two[0].reshape(rows, count, rows, count).transpose(1, 0, 3, 2)]
    dot_general x1 -> x3, matrix products: 12.5 us -> 21.1 us  [the longest x1 7.58 us: local(): jnp.dot(part_two.astype(jnp.bfloat16), pick, preferred_element_type=jnp.f...]
  transfers between devices with their start and end apart: 11 -> 11, of which waited for: 7 -> 7; matrix products, arithmetic and copies ran while one was open for 38% -> 20% of each run, Pallas kernels for 0% -> 0%
where the time goes in v8:
time: 273 us; the launch traced here: 269 us
  waiting for transfers between devices  151 us (55%)
  starting transfers between devices  46.1 us (17%)
  matrix products  43 us (16%)
  other arithmetic  17.4 us (6%)
  local copies, waits for them, and re-layouts  11.6 us (4%)
    all_to_all x3, waiting for transfers between devices, _exchange(): lax.all_to_all(data, 'seq', split_axis=axis, concat_axis=axis, tiled=True)  109 us
    ppermute x6, waiting for transfers between devices, _dp_reduce(): acc = acc + lax.ppermute(piece, 'dp', perm).astype(jnp.float32)  39.9 us
    all_to_all x3, starting transfers between devices, _exchange(): lax.all_to_all(data, 'seq', split_axis=axis, concat_axis=axis, tiled=True)  29.6 us
    ppermute x6, starting transfers between devices, _dp_reduce(): acc = acc + lax.ppermute(piece, 'dp', perm).astype(jnp.float32)  8.37 us
    ppermute x2, starting transfers between devices, _dp_reduce(): lax.ppermute(piece.astype(jnp.bfloat16), 'dp', perm).astype(jnp.float32)  8.15 us
    convert_element_type x1, other arithmetic, local(): grad_input = _rowmajor((dyfull * mfull + spread).astype(jnp.bfloat16))  7.82 us
    dot_general x1, matrix products, local(): jnp.dot(part_two.astype(jnp.bfloat16), pick, preferred_element_type=jnp.f...  7.58 us
    dot_general x1, matrix products, local(): jnp.dot(ftwo, pick.T, preferred_element_type=jnp.float32)  7.52 us
  transfers between devices with their start and end apart: 11, of which 7 were waited for; matrix products, arithmetic and copies ran while one was open for 20% of the time, Pallas kernels for 0%

profile of v8, /device:TPU:8, one launch (start us, length us, event | category | flops | bytes accessed | tf_op | source)
XLA Modules:
  0.0 269.5 jit_solution(515963432070963073)
XLA Ops:
  0.6 0.0 copy-start
  0.6 0.0 copy-start.1
  0.7 3.3 %fusion = bf16[1,1024,1024]{2,1,0:T(8,128)(2,1)S(1)} fusion(bf16[1,1024,1024]{2,1,0:T(8,128)(2,1)} %param.4, bf16[1,1024,1024]{2,1,0:T(8,128)(2,1)} %param.5), kind=kLoop, calls=%fused_computation.3 | loop fusion | flops 4194304 | bytes 6291456 | tf_op jit(solution)/shard_map/convert_element_type | solution.py:66
  4.0 0.0 copy-done
  4.0 0.1 copy-done.1
  4.1 2.3 fusion.25
  6.5 2.4 pad_maximum_fusion
  8.8 9.2 %all-to-all-start = ((bf16[2,32,32,1024]{3,2,0,1:T(8,128)(2,1)}), bf16[2,32,32,1024]{3,2,0,1:T(8,128)(2,1)}, u32[]{:S(2)}, u32[]{:S(2)}) async-start(bf16[2,32,32,1024]{3,2,0,1:T(8,128)(2,1)} %pad_maximum_fusion), calls=%async_computation | async-start | bytes 8388608 | tf_op jit(solution)/shard_map/all_to_all | solution.py:52
  18.0 7.5 %fusion.30 = bf16[1024,1024]{1,0:T(8,128)(2,1)} fusion(s32[1024]{0:T(1024)S(1)} %fusion.57, bf16[1,1024,1024]{2,1,0:T(8,128)(2,1)} %param.7), kind=kOutput, calls=%fused_computation.31 | convolution fusion | flops 4299161600 | bytes 4198400 | tf_op jit(solution)/shard_map/dot_general | solution.py:63
  25.6 85.6 %all-to-all-done = bf16[2,32,32,1024]{3,2,0,1:T(8,128)(2,1)} async-done(((bf16[2,32,32,1024]{3,2,0,1:T(8,128)(2,1)}), bf16[2,32,32,1024]{3,2,0,1:T(8,128)(2,1)}, u32[]{:S(2)}, u32[]{:S(2)}) %all-to-all-start) | async-done | bytes 4194336 | tf_op jit(solution)/shard_map/all_to_all | solution.py:52
  111.2 4.3 %fusion.60 = (bf16[1,32,32,1024]{3,2,0,1:T(8,128)(2,1)S(1)}, bf16[1,32,32,1024]{3,2,0,1:T(8,128)(2,1)}) fusion(bf16[2,32,32,1024]{3,2,0,1:T(8,128)(2,1)} %all-to-all-done), kind=kLoop, calls=%fused_computation.66 | loop fusion | bytes 8388608 | tf_op jit(solution)/shard_map/slice | solution.py:73
  115.5 0.0 copy-done.4
  115.5 3.8 %convolution_convert_fusion = bf16[1024,1024]{0,1:T(8,128)(2,1)} fusion(bf16[1024,1024]{1,0:T(8,128)(2,1)S(1)} %bitcast.111, bf16[1024,1024]{1,0:T(8,128)(2,1)S(1)} %copy-done.4), kind=kOutput, calls=%fused_computation.33 | convolution fusion | flops 2148532224 | bytes 6291456 | tf_op jit(solution)/shard_map/pq,spc->sqc/dot_general | solution.py:74
  119.3 0.0 copy-done.3
  119.3 6.8 %all-to-all-start.2 = ((bf16[1,32,32,1024]{3,2,0,1:T(8,128)(2,1)}), bf16[1,32,32,1024]{3,2,0,1:T(8,128)(2,1)}, u32[]{:S(2)}, u32[]{:S(2)}) async-start(bf16[1,32,32,1024]{3,2,0,1:T(8,128)(2,1)} %bitcast.104), calls=%async_computation.2 | async-start | bytes 4194304 | tf_op jit(solution)/shard_map/all_to_all | solution.py:52
  126.2 6.0 %fusion.61 = bf16[1024,1024]{1,0:T(8,128)(2,1)} fusion(bf16[1024,1024]{1,0:T(8,128)(2,1)} %bitcast.112, bf16[1024,1024]{1,0:T(8,128)(2,1)} %bitcast.109), kind=kOutput, calls=%fused_computation.67 | convolution fusion | flops 2147483648 | bytes 6291456 | tf_op jit(solution)/shard_map/spc,sqc->pq/dot_general | solution.py:82
  132.1 7.6 %fusion.33 = bf16[1024,1024]{1,0:T(8,128)(2,1)} fusion(s32[1024]{0:T(1024)S(1)} %fusion.57, bf16[1024,1024]{1,0:T(8,128)(2,1)} %fusion.61), kind=kOutput, calls=%fused_computation.32 | convolution fusion | flops 4299161600 | bytes 4198400 | tf_op jit(solution)/shard_map/dot_general | solution.py:84
  139.7 2.3 dynamic-slice_bitcast_fusion.5
  142.0 1.5 collective-permute-start
  143.5 1.7 collective-permute-start.2
  145.3 1.8 collective-permute-start.1
  147.1 10.4 %collective-permute-done = bf16[2,128,1024]{2,1,0:T(8,128)(2,1)} collective-permute-done((bf16[2,128,1024]{2,1,0:T(8,128)(2,1)}, bf16[2,128,1024]{2,1,0:T(8,128)(2,1)}, u32[]{:S(2)}, u32[]{:S(2)}) %collective-permute-start) | collective-permute-done | bytes 524320 | tf_op jit(solution)/shard_map/ppermute | solution.py:41
  157.5 0.9 collective-permute-done.2
  158.4 11.3 %collective-permute-done.1 = bf16[2,128,1024]{2,1,0:T(8,128)(2,1)} collective-permute-done((bf16[2,128,1024]{2,1,0:T(8,128)(2,1)S(1)}, bf16[2,128,1024]{2,1,0:T(8,128)(2,1)}, u32[]{:S(2)}, u32[]{:S(2)}) %collective-permute-start.1) | collective-permute-done | bytes 524320 | tf_op jit(solution)/shard_map/ppermute | solution.py:41
  169.7 1.8 fusion.47
  171.6 4.6 %collective-permute-start.3 = (bf16[128,1024]{1,0:T(8,128)(2,1)S(1)}, bf16[128,1024]{1,0:T(8,128)(2,1)S(1)}, u32[]{:S(2)}, u32[]{:S(2)}) collective-permute-start(bf16[128,1024]{1,0:T(8,128)(2,1)S(1)} %fusion.49), channel_id=1, source_target_pairs={{0,128},{32,160},{64,192},{96,224},{128,0},{160,32},{192,64},{224,... | collective-permute-start | bytes 786440 | tf_op jit(solution)/shard_map/ppermute | solution.py:46
  176.2 5.3 %convert_bitcast_fusion = bf16[1,1024,1024]{1,2,0:T(8,128)(2,1)} fusion(bf16[1024,1024]{1,0:T(8,128)(2,1)S(1)} %bitcast.110, bf16[1024,1024]{1,0:T(8,128)(2,1)} %fusion.30), kind=kOutput, calls=%fused_computation.23 | convolution fusion | flops 2148532224 | bytes 6291456 | tf_op jit(solution)/shard_map/pq,sqc->spc/dot_general | solution.py:79
  181.5 1.7 collective-permute-done.3
  183.2 0.9 bitcast_add_fusion.1
  184.1 3.9 %copy.17 = bf16[1,1024,1024]{2,1,0:T(8,128)(2,1)} copy(bf16[1,1024,1024]{1,2,0:T(8,128)(2,1)} %convert_bitcast_fusion) | data formatting | bytes 4194304 | tf_op jit(solution)/shard_map/optimization_barrier | solution.py:86
  188.0 0.0 all-to-all-done.2
  188.0 13.6 %all-to-all-start.1 = ((bf16[1,32,32,1024]{3,2,0,1:T(8,128)(2,1)}), bf16[1,32,32,1024]{3,2,0,1:T(8,128)(2,1)}, u32[]{:S(2)}, u32[]{:S(2)}) async-start(bf16[1,32,32,1024]{3,2,0,1:T(8,128)(2,1)} %bitcast.102), calls=%async_computation.1 | async-start | bytes 4194304 | tf_op jit(solution)/shard_map/all_to_all | solution.py:52
  201.6 4.6 %fusion.22 = bf16[1024,1024]{1,0:T(8,128)(2,1)S(1)} fusion(bf16[1024,1024]{1,0:T(8,128)(2,1)} %bitcast.28, bf16[1,1024,1024]{2,1,0:T(8,128)(2,1)} %param.4), kind=kOutput, calls=%fused_computation.29 | convolution fusion | flops 2148532224 | bytes 6291456 | tf_op jit(solution)/shard_map/skc,sjc->kj/dot_general | solution.py:89
  206.2 0.1 dynamic-slice_bitcast_fusion.2
  206.3 0.7 collective-permute-start.4
  207.1 2.6 collective-permute-start.6
  209.6 0.0 collective-permute-start.5
  209.6 5.9 %convolution_bitcast_fusion = f32[1,1024,1024]{2,1,0:T(8,128)} fusion(bf16[1024,1024]{1,0:T(8,128)(2,1)} %bitcast.28, bf16[1,1024,1024]{2,1,0:T(8,128)(2,1)S(1)} %copy-done), kind=kOutput, calls=%fused_computation.13 | convolution fusion | flops 2147483648 | bytes 8388608 | tf_op jit(solution)/shard_map/kj,skc->sjc/dot_general | solution.py:91
  215.6 17.2 %collective-permute-done.4 = bf16[2,128,1024]{2,1,0:T(8,128)(2,1)S(1)} collective-permute-done((bf16[2,128,1024]{2,1,0:T(8,128)(2,1)S(1)}, bf16[2,128,1024]{2,1,0:T(8,128)(2,1)S(1)}, u32[]{:S(2)}, u32[]{:S(2)}) %collective-permute-start.4) | collective-permute-done | bytes 524320 | tf_op jit(solution)/shard_map/ppermute | solution.py:41
  232.8 0.0 collective-permute-done.6
  232.8 0.0 collective-permute-done.5
  232.8 0.3 fusion.45
  233.1 0.7 fusion.50
  233.9 3.6 %collective-permute-start.7 = (bf16[128,1024]{1,0:T(8,128)(2,1)}, bf16[128,1024]{1,0:T(8,128)(2,1)S(1)}, u32[]{:S(2)}, u32[]{:S(2)}) collective-permute-start(bf16[128,1024]{1,0:T(8,128)(2,1)} %fusion.50), channel_id=1, source_target_pairs={{0,128},{32,160},{64,192},{96,224},{128,0},{160,32},{192,64},{224,... | collective-permute-start | bytes 786440 | tf_op jit(solution)/shard_map/ppermute | solution.py:46
  237.5 23.4 %all-to-all-done.1 = bf16[1,32,32,1024]{3,2,0,1:T(8,128)(2,1)} async-done(((bf16[1,32,32,1024]{3,2,0,1:T(8,128)(2,1)}), bf16[1,32,32,1024]{3,2,0,1:T(8,128)(2,1)}, u32[]{:S(2)}, u32[]{:S(2)}) %all-to-all-start.1) | async-done | bytes 2097184 | tf_op jit(solution)/shard_map/all_to_all | solution.py:52
  260.8 7.8 %fusion.3 = (bf16[1,1024,1024]{2,1,0:T(8,128)(2,1)}, bf16[1,1024,1024]{2,1,0:T(8,128)(2,1)}) fusion(f32[1,1024,1024]{2,1,0:T(8,128)} %convolution_bitcast_fusion, bf16[1,1024,1024]{2,1,0:T(8,128)(2,1)} %bitcast.23, bf16[1,1024,1024]{2,1,0:T(8,128)(2,1)} %param.5, bf16[1,1024,1024]{2,1,0:T(8,128)(2,1)} %param.4), kind=kLoop, calls=%fused_computation.6 | loop fusion | flops 8388608 | bytes 14680064 | tf_op jit(solution)/shard_map/convert_element_type | solution.py:95
  268.6 0.0 collective-permute-done.7
  268.6 0.9 fusion.48
  (6 shorter events, 0.1 us)
Async XLA Ops:
  0.6 3.4 %copy-start = (bf16[1,1024,1024]{2,1,0:T(8,128)(2,1)S(1)}, bf16[1,1024,1024]{2,1,0:T(8,128)(2,1)}, u32[]{:S(2)}) copy-start(bf16[1,1024,1024]{2,1,0:T(8,128)(2,1)} %param.6) | copy-start | bytes 6291460
  0.6 3.5 %copy-start.1 = (bf16[1,1024,1024]{2,1,0:T(8,128)(2,1)S(1)}, bf16[1,1024,1024]{2,1,0:T(8,128)(2,1)}, u32[]{:S(2)}) copy-start(bf16[1,1024,1024]{2,1,0:T(8,128)(2,1)} %param.4) | copy-start | bytes 6291460
  8.8 102.4 %all-to-all-start = ((bf16[2,32,32,1024]{3,2,0,1:T(8,128)(2,1)}), bf16[2,32,32,1024]{3,2,0,1:T(8,128)(2,1)}, u32[]{:S(2)}, u32[]{:S(2)}) async-start(bf16[2,32,32,1024]{3,2,0,1:T(8,128)(2,1)} %pad_maximum_fusion), calls=%async_computation | async-start | bytes 8388608 | tf_op jit(solution)/shard_map/all_to_all | solution.py:52
  111.2 4.3 %copy-start.4 = (bf16[1024,1024]{1,0:T(8,128)(2,1)S(1)}, bf16[1024,1024]{1,0:T(8,128)(2,1)}, u32[]{:S(2)}) copy-start(bf16[1024,1024]{1,0:T(8,128)(2,1)} %fusion.30) | copy-start | bytes 6291460
  115.5 3.8 %copy-start.3 = (bf16[1,32,32,1024]{3,2,0,1:T(8,128)(2,1)}, bf16[1,32,32,1024]{3,2,0,1:T(8,128)(2,1)S(1)}, u32[]{:S(2)}) copy-start(bf16[1,32,32,1024]{3,2,0,1:T(8,128)(2,1)S(1)} %get-tuple-element.8) | copy-start | bytes 6291460
  119.3 68.7 %all-to-all-start.2 = ((bf16[1,32,32,1024]{3,2,0,1:T(8,128)(2,1)}), bf16[1,32,32,1024]{3,2,0,1:T(8,128)(2,1)}, u32[]{:S(2)}, u32[]{:S(2)}) async-start(bf16[1,32,32,1024]{3,2,0,1:T(8,128)(2,1)} %bitcast.104), calls=%async_computation.2 | async-start | bytes 4194304 | tf_op jit(solution)/shard_map/all_to_all | solution.py:52
  142.0 15.5 %collective-permute-start = (bf16[2,128,1024]{2,1,0:T(8,128)(2,1)}, bf16[2,128,1024]{2,1,0:T(8,128)(2,1)}, u32[]{:S(2)}, u32[]{:S(2)}) collective-permute-start(bf16[2,128,1024]{2,1,0:T(8,128)(2,1)} %get-tuple-element.15), channel_id=1, source_target_pairs={{0,32},{32,64},{64,96},{96,0},{128,160},{160,192},{192,224},{224,1... | collective-permute-start | bytes 1572872 | tf_op jit(solution)/shard_map/ppermute | solution.py:41
  143.5 14.9 %collective-permute-start.2 = (bf16[2,128,1024]{2,1,0:T(8,128)(2,1)S(1)}, bf16[2,128,1024]{2,1,0:T(8,128)(2,1)}, u32[]{:S(2)}, u32[]{:S(2)}) collective-permute-start(bf16[2,128,1024]{2,1,0:T(8,128)(2,1)S(1)} %get-tuple-element.16), channel_id=1, source_target_pairs={{0,96},{32,0},{64,32},{96,64},{128,224},{160,128},{192,160},{224,1... | collective-permute-start | bytes 1572872 | tf_op jit(solution)/shard_map/ppermute | solution.py:41
  145.3 24.5 %collective-permute-start.1 = (bf16[2,128,1024]{2,1,0:T(8,128)(2,1)S(1)}, bf16[2,128,1024]{2,1,0:T(8,128)(2,1)}, u32[]{:S(2)}, u32[]{:S(2)}) collective-permute-start(bf16[2,128,1024]{2,1,0:T(8,128)(2,1)S(1)} %get-tuple-element.17), channel_id=1, source_target_pairs={{0,64},{32,96},{64,0},{96,32},{128,192},{160,224},{192,128},{224,1... | collective-permute-start | bytes 1572872 | tf_op jit(solution)/shard_map/ppermute | solution.py:41
  147.1 29.1 %copy-start.2 = (bf16[1,32,32,1024]{3,2,0,1:T(8,128)(2,1)S(1)}, bf16[1,32,32,1024]{3,2,0,1:T(8,128)(2,1)}, u32[]{:S(2)}) copy-start(bf16[1,32,32,1024]{3,2,0,1:T(8,128)(2,1)} %get-tuple-element.9) | copy-start | bytes 6291460
  171.6 11.6 %collective-permute-start.3 = (bf16[128,1024]{1,0:T(8,128)(2,1)S(1)}, bf16[128,1024]{1,0:T(8,128)(2,1)S(1)}, u32[]{:S(2)}, u32[]{:S(2)}) collective-permute-start(bf16[128,1024]{1,0:T(8,128)(2,1)S(1)} %fusion.49), channel_id=1, source_target_pairs={{0,128},{32,160},{64,192},{96,224},{128,0},{160,32},{192,64},{224,... | collective-permute-start | bytes 786440 | tf_op jit(solution)/shard_map/ppermute | solution.py:46
  188.0 72.8 %all-to-all-start.1 = ((bf16[1,32,32,1024]{3,2,0,1:T(8,128)(2,1)}), bf16[1,32,32,1024]{3,2,0,1:T(8,128)(2,1)}, u32[]{:S(2)}, u32[]{:S(2)}) async-start(bf16[1,32,32,1024]{3,2,0,1:T(8,128)(2,1)} %bitcast.102), calls=%async_computation.1 | async-start | bytes 4194304 | tf_op jit(solution)/shard_map/all_to_all | solution.py:52
  206.3 26.5 %collective-permute-start.4 = (bf16[2,128,1024]{2,1,0:T(8,128)(2,1)S(1)}, bf16[2,128,1024]{2,1,0:T(8,128)(2,1)S(1)}, u32[]{:S(2)}, u32[]{:S(2)}) collective-permute-start(bf16[2,128,1024]{2,1,0:T(8,128)(2,1)S(1)} %get-tuple-element.10), channel_id=1, source_target_pairs={{0,32},{32,64},{64,96},{96,0},{128,160},{160,192},{192,224},{224,1... | collective-permute-start | bytes 1572872 | tf_op jit(solution)/shard_map/ppermute | solution.py:41
  207.1 25.7 %collective-permute-start.6 = (bf16[2,128,1024]{2,1,0:T(8,128)(2,1)S(1)}, bf16[2,128,1024]{2,1,0:T(8,128)(2,1)S(1)}, u32[]{:S(2)}, u32[]{:S(2)}) collective-permute-start(bf16[2,128,1024]{2,1,0:T(8,128)(2,1)S(1)} %get-tuple-element.11), channel_id=1, source_target_pairs={{0,96},{32,0},{64,32},{96,64},{128,224},{160,128},{192,160},{224,1... | collective-permute-start | bytes 1572872 | tf_op jit(solution)/shard_map/ppermute | solution.py:41
  209.6 23.2 %collective-permute-start.5 = (bf16[2,128,1024]{2,1,0:T(8,128)(2,1)S(1)}, bf16[2,128,1024]{2,1,0:T(8,128)(2,1)S(1)}, u32[]{:S(2)}, u32[]{:S(2)}) collective-permute-start(bf16[2,128,1024]{2,1,0:T(8,128)(2,1)S(1)} %get-tuple-element.12), channel_id=1, source_target_pairs={{0,64},{32,96},{64,0},{96,32},{128,192},{160,224},{192,128},{224,1... | collective-permute-start | bytes 1572872 | tf_op jit(solution)/shard_map/ppermute | solution.py:41
  233.9 34.8 %collective-permute-start.7 = (bf16[128,1024]{1,0:T(8,128)(2,1)}, bf16[128,1024]{1,0:T(8,128)(2,1)S(1)}, u32[]{:S(2)}, u32[]{:S(2)}) collective-permute-start(bf16[128,1024]{1,0:T(8,128)(2,1)} %fusion.50), channel_id=1, source_target_pairs={{0,128},{32,160},{64,192},{96,224},{128,0},{160,32},{192,64},{224,... | collective-permute-start | bytes 786440 | tf_op jit(solution)/shard_map/ppermute | solution.py:46

commit v9 on v5

--- a/solution.py
+++ b/solution.py
@@ -39,6 +39,13 @@
         piece = lax.dynamic_index_in_dim(chunks, (lo + s) % ring, axis=1, keepdims=False)
         perm = [(g * ring + t, g * ring + (t + s) % ring) for g in range(groups) for t in range(ring)]
         acc = acc + lax.ppermute(piece, "dp", perm).astype(jnp.float32)
+    return acc
+
+
+def _dp_finish(acc, ring):
+    ndp = lax.axis_size("dp")
+    groups = ndp // ring
+    hi = lax.axis_index("dp") // ring
     own = lax.dynamic_index_in_dim(acc, hi, axis=0, keepdims=False)
     for s in range(1, groups):
         piece = lax.dynamic_index_in_dim(acc, (hi + s) % groups, axis=0, keepdims=False)
@@ -88,11 +95,14 @@
         jnp.bfloat16
     )
     part_two = jnp.einsum("spc,sqc->pq", gated_moved, moved, preferred_element_type=jnp.float32)
-    grad_two = _dp_reduce(part_two.astype(jnp.bfloat16), ring)
-    second, grad_two = lax.optimization_barrier((second, grad_two))
+    acc_two = _dp_reduce(part_two.astype(jnp.bfloat16), ring)
+    second, acc_two = lax.optimization_barrier((second, acc_two))
     monarch = _from_moved(second, count, rows)
     part_one = jnp.einsum("skc,sjc->kj", back_moved, inputs, preferred_element_type=jnp.float32)
-    grad_one = _dp_reduce(part_one.astype(jnp.bfloat16), ring)
+    acc_one = _dp_reduce(part_one.astype(jnp.bfloat16), ring)
+    monarch, acc_one, acc_two = lax.optimization_barrier((monarch, acc_one, acc_two))
+    grad_one = _dp_finish(acc_one, ring)
+    grad_two = _dp_finish(acc_two, ring)
     spread = _rowmajor(jnp.einsum("kj,skc->sjc", fone, back_moved, preferred_element_type=jnp.float32))
     spread = lax.optimization_barrier(spread)
     mfull = monarch.astype(jnp.float32)

time: 264 us -> 261 us (0.989)
  waiting for transfers between devices: 71.3 us -> 75.6 us
  starting transfers between devices: 33.8 us -> 30.7 us
    ppermute x6, waiting for transfers between devices: 45.3 us -> 35 us  [_dp_reduce(): acc = acc + lax.ppermute(piece, 'dp', perm).astype(jnp.float32)]
    all_to_all x2, waiting for transfers between devices: 18.1 us -> 25.9 us  [_from_moved(): lax.all_to_all(data.reshape(seqs, 1, rows, count, width), 'seq', split_ax...]
    ppermute x2, waiting for transfers between devices: 7.9 us -> 14.7 us  [_dp_finish(): lax.ppermute(piece.astype(jnp.bfloat16), 'dp', perm).astype(jnp.float32)]
  transfers between devices with their start and end apart: 10 -> 10, of which waited for: 10 -> 10; matrix products, arithmetic and copies ran while one was open for 11% -> 13% of each run, Pallas kernels for 0% -> 0%
where the time goes in v9:
time: 261 us; the launch traced here: 259 us
  blocking collectives  102 us (39%)
  waiting for transfers between devices  75.6 us (29%)
  starting transfers between devices  30.7 us (12%)
  matrix products  23 us (9%)
  other arithmetic  14.1 us (5%)
  local copies, waits for them, and re-layouts  12.6 us (5%)
    all_to_all x1, blocking collectives, local(): in1 = lax.all_to_all(out1, 'seq', split_axis=1, concat_axis=3, tiled=True)  102 us
    ppermute x6, waiting for transfers between devices, _dp_reduce(): acc = acc + lax.ppermute(piece, 'dp', perm).astype(jnp.float32)  35 us
    all_to_all x2, waiting for transfers between devices, _from_moved(): lax.all_to_all(data.reshape(seqs, 1, rows, count, width), 'seq', split_ax...  25.9 us
    ppermute x2, waiting for transfers between devices, _dp_finish(): lax.ppermute(piece.astype(jnp.bfloat16), 'dp', perm).astype(jnp.float32)  14.7 us
    all_to_all x2, starting transfers between devices, _from_moved(): lax.all_to_all(data.reshape(seqs, 1, rows, count, width), 'seq', split_ax...  14.4 us
    ppermute x6, starting transfers between devices, _dp_reduce(): acc = acc + lax.ppermute(piece, 'dp', perm).astype(jnp.float32)  10.3 us
    convert_element_type x1, other arithmetic, local(): grad_input = _rowmajor((dyfull * mfull + spread).astype(jnp.bfloat16))  7.96 us
    ppermute x2, starting transfers between devices, _dp_finish(): lax.ppermute(piece.astype(jnp.bfloat16), 'dp', perm).astype(jnp.float32)  6.02 us
  transfers between devices with their start and end apart: 10, of which 10 were waited for; matrix products, arithmetic and copies ran while one was open for 13% of the time, Pallas kernels for 0%

profile of v9, /device:TPU:8, one launch (start us, length us, event | category | flops | bytes accessed | tf_op | source)
XLA Modules:
  0.0 258.5 jit_solution(1677235002293348042)
XLA Ops:
  0.6 0.0 copy-start
  0.6 0.0 copy-start.2
  0.7 0.0 copy-start.8
  0.7 3.4 %fusion = bf16[1,1024,1024]{2,1,0:T(8,128)(2,1)S(1)} fusion(bf16[1,1024,1024]{2,1,0:T(8,128)(2,1)} %param.4, bf16[1,1024,1024]{2,1,0:T(8,128)(2,1)} %param.5), kind=kLoop, calls=%fused_computation.3 | loop fusion | flops 4194304 | bytes 6291456 | tf_op jit(solution)/shard_map/convert_element_type | solution.py:81
  4.0 0.0 copy-done.2
  4.0 0.2 copy-done.8
  4.3 2.3 fusion.17
  6.6 0.4 pad_maximum_fusion
  7.0 101.7 %all_to_all.45 = bf16[2,32,32,1,1024]{4,2,0,3,1:T(8,128)(2,1)S(1)} all-to-all(bf16[2,32,32,1,1024]{4,2,0,3,1:T(8,128)(2,1)S(1)} %pad_maximum_fusion), channel_id=1, replica_groups=mesh['dp'=8,'seq'=32] {'seq'}, dimensions={1} | all-to-all | bytes 8388608 | tf_op jit(solution)/shard_map/all_to_all | solution.py:86
  108.7 2.3 copy.29
  111.0 1.8 fusion.35
  112.8 2.5 fusion.24
  115.2 2.5 copy.24
  117.7 7.2 %all-to-all-start.2 = ((bf16[1,1,32,32,1024]{4,2,1,0,3:T(8,128)(2,1)}), bf16[1,1,32,32,1024]{4,2,1,0,3:T(8,128)(2,1)}, u32[]{:S(2)}, u32[]{:S(2)}) async-start(bf16[1,1,32,32,1024]{4,2,1,0,3:T(8,128)(2,1)} %copy.24), calls=%async_computation.2 | async-start | bytes 4194304 | tf_op jit(solution)/shard_map/all_to_all | solution.py:67
  125.0 4.6 %convolution_convert_fusion = bf16[1024,1024]{1,0:T(8,128)(2,1)S(1)} fusion(bf16[1024,1024]{1,0:T(8,128)(2,1)} %bitcast.123, bf16[1024,1024]{1,0:T(8,128)(2,1)} %bitcast.120), kind=kOutput, calls=%fused_computation.24 | convolution fusion | flops 2148532224 | bytes 6291456 | tf_op jit(solution)/shard_map/spc,sqc->pq/dot_general | solution.py:97
  129.6 0.0 copy-start.6
  129.6 0.2 dynamic-slice_bitcast_fusion.5
  129.8 1.6 collective-permute-start
  131.3 1.7 collective-permute-start.2
  133.1 1.8 collective-permute-start.1
  134.9 3.7 %convert_bitcast_fusion = bf16[1,1024,1024]{1,2,0:T(8,128)(2,1)} fusion(bf16[1024,1024]{1,0:T(8,128)(2,1)S(1)} %bitcast.121, bf16[1,1024,1024]{2,1,0:T(8,128)(2,1)S(1)} %copy-done), kind=kOutput, calls=%fused_computation.20 | convolution fusion | flops 2148532224 | bytes 6291456 | tf_op jit(solution)/shard_map/pq,sqc->spc/dot_general | solution.py:94
  138.6 6.4 %collective-permute-done = bf16[2,128,1024]{2,1,0:T(8,128)(2,1)S(1)} collective-permute-done((bf16[2,128,1024]{2,1,0:T(8,128)(2,1)S(1)}, bf16[2,128,1024]{2,1,0:T(8,128)(2,1)S(1)}, u32[]{:S(2)}, u32[]{:S(2)}) %collective-permute-start) | collective-permute-done | bytes 524320 | tf_op jit(solution)/shard_map/ppermute | solution.py:41
  145.0 10.5 %collective-permute-done.2 = bf16[2,128,1024]{2,1,0:T(8,128)(2,1)S(1)} collective-permute-done((bf16[2,128,1024]{2,1,0:T(8,128)(2,1)S(1)}, bf16[2,128,1024]{2,1,0:T(8,128)(2,1)S(1)}, u32[]{:S(2)}, u32[]{:S(2)}) %collective-permute-start.2) | collective-permute-done | bytes 524320 | tf_op jit(solution)/shard_map/ppermute | solution.py:41
  155.5 1.7 collective-permute-done.1
  157.2 0.3 fusion.30
  157.6 2.9 %copy.22 = bf16[1,1024,1024]{2,1,0:T(8,128)(2,1)S(1)} copy(bf16[1,1024,1024]{1,2,0:T(8,128)(2,1)} %convert_bitcast_fusion) | data formatting | bytes 4194304 | tf_op jit(solution)/shard_map/optimization_barrier | solution.py:99
  160.4 2.5 copy.23
  162.9 9.9 %all-to-all-done.2 = bf16[1,1,32,32,1024]{4,2,1,0,3:T(8,128)(2,1)} async-done(((bf16[1,1,32,32,1024]{4,2,1,0,3:T(8,128)(2,1)}), bf16[1,1,32,32,1024]{4,2,1,0,3:T(8,128)(2,1)}, u32[]{:S(2)}, u32[]{:S(2)}) %all-to-all-start.2) | async-done | bytes 2097184 | tf_op jit(solution)/shard_map/all_to_all | solution.py:67
  172.8 7.2 %all-to-all-start.1 = ((bf16[1,1,32,32,1024]{4,2,1,0,3:T(8,128)(2,1)}), bf16[1,1,32,32,1024]{4,2,1,0,3:T(8,128)(2,1)}, u32[]{:S(2)}, u32[]{:S(2)}) async-start(bf16[1,1,32,32,1024]{4,2,1,0,3:T(8,128)(2,1)} %copy.23), calls=%async_computation.1 | async-start | bytes 4194304 | tf_op jit(solution)/shard_map/all_to_all | solution.py:67
  180.1 4.0 %fusion.14 = bf16[1024,1024]{1,0:T(8,128)(2,1)S(1)} fusion(bf16[1024,1024]{1,0:T(8,128)(2,1)} %bitcast.30, bf16[1,1024,1024]{2,1,0:T(8,128)(2,1)S(1)} %copy-done.3), kind=kOutput, calls=%fused_computation.21 | convolution fusion | flops 2148532224 | bytes 6291456 | tf_op jit(solution)/shard_map/skc,sjc->kj/dot_general | solution.py:101
  184.1 0.0 copy-start.9
  184.1 0.1 dynamic-slice_bitcast_fusion.2
  184.2 1.6 collective-permute-start.3
  185.8 1.7 collective-permute-start.5
  187.5 1.8 collective-permute-start.4
  189.4 6.0 %convolution_bitcast_fusion = f32[1,1024,1024]{2,1,0:T(8,128)} fusion(bf16[1024,1024]{1,0:T(8,128)(2,1)} %bitcast.30, bf16[1,1024,1024]{2,1,0:T(8,128)(2,1)S(1)} %copy-done.9), kind=kOutput, calls=%fused_computation.9 | convolution fusion | flops 2147483648 | bytes 8388608 | tf_op jit(solution)/shard_map/kj,skc->sjc/dot_general | solution.py:106
  195.3 4.1 %collective-permute-done.3 = bf16[2,128,1024]{2,1,0:T(8,128)(2,1)S(1)} collective-permute-done((bf16[2,128,1024]{2,1,0:T(8,128)(2,1)S(1)}, bf16[2,128,1024]{2,1,0:T(8,128)(2,1)S(1)}, u32[]{:S(2)}, u32[]{:S(2)}) %collective-permute-start.3) | collective-permute-done | bytes 524320 | tf_op jit(solution)/shard_map/ppermute | solution.py:41
  199.5 10.6 %collective-permute-done.5 = bf16[2,128,1024]{2,1,0:T(8,128)(2,1)S(1)} collective-permute-done((bf16[2,128,1024]{2,1,0:T(8,128)(2,1)S(1)}, bf16[2,128,1024]{2,1,0:T(8,128)(2,1)S(1)}, u32[]{:S(2)}, u32[]{:S(2)}) %collective-permute-start.5) | collective-permute-done | bytes 524320 | tf_op jit(solution)/shard_map/ppermute | solution.py:41
  210.1 1.6 collective-permute-done.4
  211.7 0.3 fusion.28
  212.0 16.0 %all-to-all-done.1 = bf16[1,1,32,32,1024]{4,2,1,0,3:T(8,128)(2,1)} async-done(((bf16[1,1,32,32,1024]{4,2,1,0,3:T(8,128)(2,1)}), bf16[1,1,32,32,1024]{4,2,1,0,3:T(8,128)(2,1)}, u32[]{:S(2)}, u32[]{:S(2)}) %all-to-all-start.1) | async-done | bytes 2097184 | tf_op jit(solution)/shard_map/all_to_all | solution.py:67
  228.1 4.5 %collective-permute-start.7 = (bf16[128,1024]{1,0:T(8,128)(2,1)S(1)}, bf16[128,1024]{1,0:T(8,128)(2,1)S(1)}, u32[]{:S(2)}, u32[]{:S(2)}) collective-permute-start(bf16[128,1024]{1,0:T(8,128)(2,1)S(1)} %fusion.34), channel_id=1, source_target_pairs={{0,128},{32,160},{64,192},{96,224},{128,0},{160,32},{192,64},{224,... | collective-permute-start | bytes 786440 | tf_op jit(solution)/shard_map/ppermute | solution.py:53
  232.6 1.5 collective-permute-start.6
  234.1 8.0 %fusion.3 = (bf16[1,1024,1024]{2,1,0:T(8,128)(2,1)}, bf16[1,1024,1024]{2,1,0:T(8,128)(2,1)}) fusion(f32[1,1024,1024]{2,1,0:T(8,128)} %convolution_bitcast_fusion, bf16[1,1024,1024]{2,1,0:T(8,128)(2,1)} %bitcast.24, bf16[1,1024,1024]{2,1,0:T(8,128)(2,1)} %param.5, bf16[1,1024,1024]{2,1,0:T(8,128)(2,1)} %param.4), kind=kLoop, calls=%fused_computation.6 | loop fusion | flops 8388608 | bytes 14680064 | tf_op jit(solution)/shard_map/convert_element_type | solution.py:110
  242.1 5.8 %collective-permute-done.7 = bf16[128,1024]{1,0:T(8,128)(2,1)S(1)} collective-permute-done((bf16[128,1024]{1,0:T(8,128)(2,1)S(1)}, bf16[128,1024]{1,0:T(8,128)(2,1)S(1)}, u32[]{:S(2)}, u32[]{:S(2)}) %collective-permute-start.7) | collective-permute-done | bytes 262176 | tf_op jit(solution)/shard_map/ppermute | solution.py:53
  247.9 0.9 fusion.31
  248.7 8.9 %collective-permute-done.6 = bf16[128,1024]{1,0:T(8,128)(2,1)S(1)} collective-permute-done((bf16[128,1024]{1,0:T(8,128)(2,1)S(1)}, bf16[128,1024]{1,0:T(8,128)(2,1)S(1)}, u32[]{:S(2)}, u32[]{:S(2)}) %collective-permute-start.6) | collective-permute-done | bytes 262176 | tf_op jit(solution)/shard_map/ppermute | solution.py:53
  257.7 0.9 fusion.32
  (15 shorter events, 0.1 us)
Async XLA Ops:
  0.6 112.1 %copy-start = (bf16[1,1024,1024]{2,1,0:T(8,128)(2,1)S(1)}, bf16[1,1024,1024]{2,1,0:T(8,128)(2,1)}, u32[]{:S(2)}) copy-start(bf16[1,1024,1024]{2,1,0:T(8,128)(2,1)} %param.7) | copy-start | bytes 6291460
  0.6 3.4 %copy-start.2 = (bf16[1,1024,1024]{2,1,0:T(8,128)(2,1)S(1)}, bf16[1,1024,1024]{2,1,0:T(8,128)(2,1)}, u32[]{:S(2)}) copy-start(bf16[1,1024,1024]{2,1,0:T(8,128)(2,1)} %param.4) | copy-start | bytes 6291460
  0.7 3.6 %copy-start.8 = (bf16[1,1024,1024]{2,1,0:T(8,128)(2,1)S(1)}, bf16[1,1024,1024]{2,1,0:T(8,128)(2,1)}, u32[]{:S(2)}) copy-start(bf16[1,1024,1024]{2,1,0:T(8,128)(2,1)} %param.6) | copy-start | bytes 6291460
  112.8 2.5 copy-start.7
  117.7 55.1 %all-to-all-start.2 = ((bf16[1,1,32,32,1024]{4,2,1,0,3:T(8,128)(2,1)}), bf16[1,1,32,32,1024]{4,2,1,0,3:T(8,128)(2,1)}, u32[]{:S(2)}, u32[]{:S(2)}) async-start(bf16[1,1,32,32,1024]{4,2,1,0,3:T(8,128)(2,1)} %copy.24), calls=%async_computation.2 | async-start | bytes 4194304 | tf_op jit(solution)/shard_map/all_to_all | solution.py:67
  129.6 5.4 %copy-start.6 = (bf16[1,1,32,32,1,1024]{5,3,2,4,1,0:T(8,128)(2,1)S(1)}, bf16[1,1,32,32,1,1024]{5,3,2,4,1,0:T(8,128)(2,1)}, u32[]{:S(2)}) copy-start(bf16[1,1,32,32,1,1024]{5,3,2,4,1,0:T(8,128)(2,1)} %get-tuple-element.15) | copy-start | bytes 6291460
  129.8 15.2 %collective-permute-start = (bf16[2,128,1024]{2,1,0:T(8,128)(2,1)S(1)}, bf16[2,128,1024]{2,1,0:T(8,128)(2,1)S(1)}, u32[]{:S(2)}, u32[]{:S(2)}) collective-permute-start(bf16[2,128,1024]{2,1,0:T(8,128)(2,1)S(1)} %get-tuple-element.21), channel_id=1, source_target_pairs={{0,32},{32,64},{64,96},{96,0},{128,160},{160,192},{192,224},{224,1... | collective-permute-start | bytes 1572872 | tf_op jit(solution)/shard_map/ppermute | solution.py:41
  131.3 24.2 %collective-permute-start.2 = (bf16[2,128,1024]{2,1,0:T(8,128)(2,1)S(1)}, bf16[2,128,1024]{2,1,0:T(8,128)(2,1)S(1)}, u32[]{:S(2)}, u32[]{:S(2)}) collective-permute-start(bf16[2,128,1024]{2,1,0:T(8,128)(2,1)S(1)} %get-tuple-element.22), channel_id=1, source_target_pairs={{0,96},{32,0},{64,32},{96,64},{128,224},{160,128},{192,160},{224,1... | collective-permute-start | bytes 1572872 | tf_op jit(solution)/shard_map/ppermute | solution.py:41
  133.1 24.1 %collective-permute-start.1 = (bf16[2,128,1024]{2,1,0:T(8,128)(2,1)S(1)}, bf16[2,128,1024]{2,1,0:T(8,128)(2,1)S(1)}, u32[]{:S(2)}, u32[]{:S(2)}) collective-permute-start(bf16[2,128,1024]{2,1,0:T(8,128)(2,1)S(1)} %get-tuple-element.23), channel_id=1, source_target_pairs={{0,64},{32,96},{64,0},{96,32},{128,192},{160,224},{192,128},{224,1... | collective-permute-start | bytes 1572872 | tf_op jit(solution)/shard_map/ppermute | solution.py:41
  162.9 17.2 %copy-start.3 = (bf16[1,1024,1024]{2,1,0:T(8,128)(2,1)S(1)}, bf16[1,1024,1024]{2,1,0:T(8,128)(2,1)}, u32[]{:S(2)}) copy-start(bf16[1,1024,1024]{2,1,0:T(8,128)(2,1)} %param.4) | copy-start | bytes 6291460
  172.8 55.2 %all-to-all-start.1 = ((bf16[1,1,32,32,1024]{4,2,1,0,3:T(8,128)(2,1)}), bf16[1,1,32,32,1024]{4,2,1,0,3:T(8,128)(2,1)}, u32[]{:S(2)}, u32[]{:S(2)}) async-start(bf16[1,1,32,32,1024]{4,2,1,0,3:T(8,128)(2,1)} %copy.23), calls=%async_computation.1 | async-start | bytes 4194304 | tf_op jit(solution)/shard_map/all_to_all | solution.py:67
  184.1 5.3 %copy-start.9 = (bf16[1,1024,1024]{2,1,0:T(8,128)(2,1)S(1)}, bf16[1,1024,1024]{2,1,0:T(8,128)(2,1)}, u32[]{:S(2)}) copy-start(bf16[1,1024,1024]{2,1,0:T(8,128)(2,1)} %param.6) | copy-start | bytes 6291460
  184.2 15.2 %collective-permute-start.3 = (bf16[2,128,1024]{2,1,0:T(8,128)(2,1)S(1)}, bf16[2,128,1024]{2,1,0:T(8,128)(2,1)S(1)}, u32[]{:S(2)}, u32[]{:S(2)}) collective-permute-start(bf16[2,128,1024]{2,1,0:T(8,128)(2,1)S(1)} %get-tuple-element.18), channel_id=1, source_target_pairs={{0,32},{32,64},{64,96},{96,0},{128,160},{160,192},{192,224},{224,1... | collective-permute-start | bytes 1572872 | tf_op jit(solution)/shard_map/ppermute | solution.py:41
  185.8 24.3 %collective-permute-start.5 = (bf16[2,128,1024]{2,1,0:T(8,128)(2,1)S(1)}, bf16[2,128,1024]{2,1,0:T(8,128)(2,1)S(1)}, u32[]{:S(2)}, u32[]{:S(2)}) collective-permute-start(bf16[2,128,1024]{2,1,0:T(8,128)(2,1)S(1)} %get-tuple-element.19), channel_id=1, source_target_pairs={{0,96},{32,0},{64,32},{96,64},{128,224},{160,128},{192,160},{224,1... | collective-permute-start | bytes 1572872 | tf_op jit(solution)/shard_map/ppermute | solution.py:41
  187.5 24.1 %collective-permute-start.4 = (bf16[2,128,1024]{2,1,0:T(8,128)(2,1)S(1)}, bf16[2,128,1024]{2,1,0:T(8,128)(2,1)S(1)}, u32[]{:S(2)}, u32[]{:S(2)}) collective-permute-start(bf16[2,128,1024]{2,1,0:T(8,128)(2,1)S(1)} %get-tuple-element.20), channel_id=1, source_target_pairs={{0,64},{32,96},{64,0},{96,32},{128,192},{160,224},{192,128},{224,1... | collective-permute-start | bytes 1572872 | tf_op jit(solution)/shard_map/ppermute | solution.py:41
  212.0 16.0 %copy-start.4 = (f32[2,128,1024]{2,1,0:T(8,128)}, f32[2,128,1024]{2,1,0:T(8,128)S(1)}, u32[]{:S(2)}) copy-start(f32[2,128,1024]{2,1,0:T(8,128)S(1)} %fusion.28) | copy-start | bytes 3145732
  228.1 29.6 %copy-start.5 = (f32[2,128,1024]{2,1,0:T(8,128)S(1)}, f32[2,128,1024]{2,1,0:T(8,128)}, u32[]{:S(2)}) copy-start(f32[2,128,1024]{2,1,0:T(8,128)} %copy-done.4) | copy-start | bytes 3145732
  228.1 19.8 %collective-permute-start.7 = (bf16[128,1024]{1,0:T(8,128)(2,1)S(1)}, bf16[128,1024]{1,0:T(8,128)(2,1)S(1)}, u32[]{:S(2)}, u32[]{:S(2)}) collective-permute-start(bf16[128,1024]{1,0:T(8,128)(2,1)S(1)} %fusion.34), channel_id=1, source_target_pairs={{0,128},{32,160},{64,192},{96,224},{128,0},{160,32},{192,64},{224,... | collective-permute-start | bytes 786440 | tf_op jit(solution)/shard_map/ppermute | solution.py:53
  232.6 25.1 %collective-permute-start.6 = (bf16[128,1024]{1,0:T(8,128)(2,1)S(1)}, bf16[128,1024]{1,0:T(8,128)(2,1)S(1)}, u32[]{:S(2)}, u32[]{:S(2)}) collective-permute-start(bf16[128,1024]{1,0:T(8,128)(2,1)S(1)} %fusion.33), channel_id=1, source_target_pairs={{0,128},{32,160},{64,192},{96,224},{128,0},{160,32},{192,64},{224,... | collective-permute-start | bytes 786440 | tf_op jit(solution)/shard_map/ppermute | solution.py:53
  234.1 24.4 %copy-start.1 = (bf16[1,1024,1024]{2,1,0:T(8,128)(2,1)S(1)}, bf16[1,1024,1024]{2,1,0:T(8,128)(2,1)}, u32[]{:S(2)}) copy-start(bf16[1,1024,1024]{2,1,0:T(8,128)(2,1)} %param.7) | copy-start | bytes 6291460

commit v10 on v9

--- a/solution.py
+++ b/solution.py
@@ -101,8 +101,9 @@
     part_one = jnp.einsum("skc,sjc->kj", back_moved, inputs, preferred_element_type=jnp.float32)
     acc_one = _dp_reduce(part_one.astype(jnp.bfloat16), ring)
     monarch, acc_one, acc_two = lax.optimization_barrier((monarch, acc_one, acc_two))
-    grad_one = _dp_finish(acc_one, ring)
-    grad_two = _dp_finish(acc_two, ring)
+    both = _dp_finish(jnp.concatenate([acc_one, acc_two], axis=1), ring)
+    grad_one = both[: acc_one.shape[1]]
+    grad_two = both[acc_one.shape[1] :]
     spread = _rowmajor(jnp.einsum("kj,skc->sjc", fone, back_moved, preferred_element_type=jnp.float32))
     spread = lax.optimization_barrier(spread)
     mfull = monarch.astype(jnp.float32)

time: 261 us -> 262 us (level)
  waiting for transfers between devices: 75.6 us -> 79 us
    ppermute x2 -> x1, waiting for transfers between devices: 14.7 us -> 18.1 us  [_dp_finish(): lax.ppermute(piece.astype(jnp.bfloat16), 'dp', perm).astype(jnp.float32)]
    ppermute x2 -> x1, starting transfers between devices: 6.02 us -> 4.51 us  [_dp_finish(): lax.ppermute(piece.astype(jnp.bfloat16), 'dp', perm).astype(jnp.float32)]
  transfers between devices with their start and end apart: 10 -> 9, of which waited for: 10 -> 9; matrix products, arithmetic and copies ran while one was open for 13% -> 12% of each run, Pallas kernels for 0% -> 0%
where the time goes in v10:
time: 262 us; the launch traced here: 259 us
  blocking collectives  102 us (39%)
  waiting for transfers between devices  79 us (30%)
  starting transfers between devices  29.2 us (11%)
  matrix products  23 us (9%)
  local copies, waits for them, and re-layouts  13.8 us (5%)
  other arithmetic  11.5 us (4%)
    all_to_all x1, blocking collectives, local(): in1 = lax.all_to_all(out1, 'seq', split_axis=1, concat_axis=3, tiled=True)  102 us
    ppermute x6, waiting for transfers between devices, _dp_reduce(): acc = acc + lax.ppermute(piece, 'dp', perm).astype(jnp.float32)  35 us
    all_to_all x2, waiting for transfers between devices, _from_moved(): lax.all_to_all(data.reshape(seqs, 1, rows, count, width), 'seq', split_ax...  25.9 us
    ppermute x1, waiting for transfers between devices, _dp_finish(): lax.ppermute(piece.astype(jnp.bfloat16), 'dp', perm).astype(jnp.float32)  18.1 us
    all_to_all x2, starting transfers between devices, _from_moved(): lax.all_to_all(data.reshape(seqs, 1, rows, count, width), 'seq', split_ax...  14.4 us
    ppermute x6, starting transfers between devices, _dp_reduce(): acc = acc + lax.ppermute(piece, 'dp', perm).astype(jnp.float32)  10.3 us
    convert_element_type x1, other arithmetic, local(): grad_input = _rowmajor((dyfull * mfull + spread).astype(jnp.bfloat16))  6.93 us
    dot_general x1, matrix products, local(): jnp.einsum('kj,skc->sjc', fone, back_moved, preferred_element_type=jnp.fl...  5.96 us
  transfers between devices with their start and end apart: 9, of which 9 were waited for; matrix products, arithmetic and copies ran while one was open for 12% of the time, Pallas kernels for 0%

profile of v10, /device:TPU:8, one launch (start us, length us, event | category | flops | bytes accessed | tf_op | source)
XLA Modules:
  0.0 259.1 jit_solution(6125778890281568808)
XLA Ops:
  0.6 0.0 copy-start
  0.6 0.0 copy-start.2
  0.7 0.0 copy-start.8
  0.7 3.4 %fusion = bf16[1,1024,1024]{2,1,0:T(8,128)(2,1)S(1)} fusion(bf16[1,1024,1024]{2,1,0:T(8,128)(2,1)} %param.4, bf16[1,1024,1024]{2,1,0:T(8,128)(2,1)} %param.5), kind=kLoop, calls=%fused_computation.3 | loop fusion | flops 4194304 | bytes 6291456 | tf_op jit(solution)/shard_map/convert_element_type | solution.py:81
  4.0 0.2 copy-done.8
  4.3 2.3 fusion.17
  6.6 0.4 pad_maximum_fusion
  7.0 101.7 %all_to_all.45 = bf16[2,32,32,1,1024]{4,2,0,3,1:T(8,128)(2,1)S(1)} all-to-all(bf16[2,32,32,1,1024]{4,2,0,3,1:T(8,128)(2,1)S(1)} %pad_maximum_fusion), channel_id=1, replica_groups=mesh['dp'=8,'seq'=32] {'seq'}, dimensions={1} | all-to-all | bytes 8388608 | tf_op jit(solution)/shard_map/all_to_all | solution.py:86
  108.7 2.3 copy.29
  111.0 1.8 fusion.32
  112.8 2.5 fusion.24
  115.3 2.5 copy.24
  117.7 7.2 %all-to-all-start.2 = ((bf16[1,1,32,32,1024]{4,2,1,0,3:T(8,128)(2,1)}), bf16[1,1,32,32,1024]{4,2,1,0,3:T(8,128)(2,1)}, u32[]{:S(2)}, u32[]{:S(2)}) async-start(bf16[1,1,32,32,1024]{4,2,1,0,3:T(8,128)(2,1)} %copy.24), calls=%async_computation.2 | async-start | bytes 4194304 | tf_op jit(solution)/shard_map/all_to_all | solution.py:67
  125.0 4.6 %convolution_convert_fusion = bf16[1024,1024]{1,0:T(8,128)(2,1)S(1)} fusion(bf16[1024,1024]{1,0:T(8,128)(2,1)} %bitcast.115, bf16[1024,1024]{1,0:T(8,128)(2,1)} %bitcast.112), kind=kOutput, calls=%fused_computation.24 | convolution fusion | flops 2148532224 | bytes 6291456 | tf_op jit(solution)/shard_map/spc,sqc->pq/dot_general | solution.py:97
  129.6 0.0 copy-start.6
  129.6 0.2 dynamic-slice_bitcast_fusion.5
  129.8 1.6 collective-permute-start
  131.4 1.7 collective-permute-start.2
  133.1 1.8 collective-permute-start.1
  134.9 3.7 %convert_bitcast_fusion = bf16[1,1024,1024]{1,2,0:T(8,128)(2,1)} fusion(bf16[1024,1024]{1,0:T(8,128)(2,1)S(1)} %bitcast.113, bf16[1,1024,1024]{2,1,0:T(8,128)(2,1)S(1)} %copy-done), kind=kOutput, calls=%fused_computation.20 | convolution fusion | flops 2148532224 | bytes 6291456 | tf_op jit(solution)/shard_map/pq,sqc->spc/dot_general | solution.py:94
  138.6 6.4 %collective-permute-done = bf16[2,128,1024]{2,1,0:T(8,128)(2,1)S(1)} collective-permute-done((bf16[2,128,1024]{2,1,0:T(8,128)(2,1)S(1)}, bf16[2,128,1024]{2,1,0:T(8,128)(2,1)S(1)}, u32[]{:S(2)}, u32[]{:S(2)}) %collective-permute-start) | collective-permute-done | bytes 524320 | tf_op jit(solution)/shard_map/ppermute | solution.py:41
  145.0 1.1 collective-permute-done.2
  146.2 11.1 %collective-permute-done.1 = bf16[2,128,1024]{2,1,0:T(8,128)(2,1)S(1)} collective-permute-done((bf16[2,128,1024]{2,1,0:T(8,128)(2,1)S(1)}, bf16[2,128,1024]{2,1,0:T(8,128)(2,1)S(1)}, u32[]{:S(2)}, u32[]{:S(2)}) %collective-permute-start.1) | collective-permute-done | bytes 524320 | tf_op jit(solution)/shard_map/ppermute | solution.py:41
  157.2 0.3 fusion.30
  157.6 2.9 %copy.22 = bf16[1,1024,1024]{2,1,0:T(8,128)(2,1)S(1)} copy(bf16[1,1024,1024]{1,2,0:T(8,128)(2,1)} %convert_bitcast_fusion) | data formatting | bytes 4194304 | tf_op jit(solution)/shard_map/optimization_barrier | solution.py:99
  160.5 2.5 copy.23
  162.9 9.9 %all-to-all-done.2 = bf16[1,1,32,32,1024]{4,2,1,0,3:T(8,128)(2,1)} async-done(((bf16[1,1,32,32,1024]{4,2,1,0,3:T(8,128)(2,1)}), bf16[1,1,32,32,1024]{4,2,1,0,3:T(8,128)(2,1)}, u32[]{:S(2)}, u32[]{:S(2)}) %all-to-all-start.2) | async-done | bytes 2097184 | tf_op jit(solution)/shard_map/all_to_all | solution.py:67
  172.8 7.2 %all-to-all-start.1 = ((bf16[1,1,32,32,1024]{4,2,1,0,3:T(8,128)(2,1)}), bf16[1,1,32,32,1024]{4,2,1,0,3:T(8,128)(2,1)}, u32[]{:S(2)}, u32[]{:S(2)}) async-start(bf16[1,1,32,32,1024]{4,2,1,0,3:T(8,128)(2,1)} %copy.23), calls=%async_computation.1 | async-start | bytes 4194304 | tf_op jit(solution)/shard_map/all_to_all | solution.py:67
  180.1 4.0 %fusion.14 = bf16[1024,1024]{1,0:T(8,128)(2,1)S(1)} fusion(bf16[1024,1024]{1,0:T(8,128)(2,1)} %bitcast.30, bf16[1,1024,1024]{2,1,0:T(8,128)(2,1)S(1)} %copy-done.3), kind=kOutput, calls=%fused_computation.21 | convolution fusion | flops 2148532224 | bytes 6291456 | tf_op jit(solution)/shard_map/skc,sjc->kj/dot_general | solution.py:101
  184.1 0.0 copy-start.9
  184.1 0.1 dynamic-slice_bitcast_fusion.2
  184.2 1.6 collective-permute-start.3
  185.8 1.7 collective-permute-start.5
  187.6 1.8 collective-permute-start.4
  189.4 6.0 %convolution_bitcast_fusion = f32[1,1024,1024]{2,1,0:T(8,128)} fusion(bf16[1024,1024]{1,0:T(8,128)(2,1)} %bitcast.30, bf16[1,1024,1024]{2,1,0:T(8,128)(2,1)S(1)} %copy-done.9), kind=kOutput, calls=%fused_computation.9 | convolution fusion | flops 2147483648 | bytes 8388608 | tf_op jit(solution)/shard_map/kj,skc->sjc/dot_general | solution.py:107
  195.3 4.1 %collective-permute-done.3 = bf16[2,128,1024]{2,1,0:T(8,128)(2,1)S(1)} collective-permute-done((bf16[2,128,1024]{2,1,0:T(8,128)(2,1)S(1)}, bf16[2,128,1024]{2,1,0:T(8,128)(2,1)S(1)}, u32[]{:S(2)}, u32[]{:S(2)}) %collective-permute-start.3) | collective-permute-done | bytes 524320 | tf_op jit(solution)/shard_map/ppermute | solution.py:41
  199.5 10.6 %collective-permute-done.5 = bf16[2,128,1024]{2,1,0:T(8,128)(2,1)S(1)} collective-permute-done((bf16[2,128,1024]{2,1,0:T(8,128)(2,1)S(1)}, bf16[2,128,1024]{2,1,0:T(8,128)(2,1)S(1)}, u32[]{:S(2)}, u32[]{:S(2)}) %collective-permute-start.5) | collective-permute-done | bytes 524320 | tf_op jit(solution)/shard_map/ppermute | solution.py:41
  210.1 1.6 collective-permute-done.4
  211.7 0.3 fusion.28
  212.0 16.0 %all-to-all-done.1 = bf16[1,1,32,32,1024]{4,2,1,0,3:T(8,128)(2,1)} async-done(((bf16[1,1,32,32,1024]{4,2,1,0,3:T(8,128)(2,1)}), bf16[1,1,32,32,1024]{4,2,1,0,3:T(8,128)(2,1)}, u32[]{:S(2)}, u32[]{:S(2)}) %all-to-all-start.1) | async-done | bytes 2097184 | tf_op jit(solution)/shard_map/all_to_all | solution.py:67
  228.0 0.1 constant_dynamic-update-slice_fusion.1
  228.1 0.1 constant_dynamic-update-slice_fusion
  228.2 0.1 fusion.31
  228.3 4.5 %collective-permute-start.6 = (bf16[256,1024]{1,0:T(8,128)(2,1)S(1)}, bf16[256,1024]{1,0:T(8,128)(2,1)S(1)}, u32[]{:S(2)}, u32[]{:S(2)}) collective-permute-start(bf16[256,1024]{1,0:T(8,128)(2,1)S(1)} %fusion.31), channel_id=1, source_target_pairs={{0,128},{32,160},{64,192},{96,224},{128,0},{160,32},{192,64},{224,... | collective-permute-start | bytes 1572872 | tf_op jit(solution)/shard_map/ppermute | solution.py:53
  232.8 6.9 %fusion.3 = (bf16[1,1024,1024]{2,1,0:T(8,128)(2,1)}, bf16[1,1024,1024]{2,1,0:T(8,128)(2,1)}) fusion(f32[1,1024,1024]{2,1,0:T(8,128)} %convolution_bitcast_fusion, bf16[1,1024,1024]{2,1,0:T(8,128)(2,1)} %bitcast.24, bf16[1,1024,1024]{2,1,0:T(8,128)(2,1)S(1)} %copy-done.5, bf16[1,1024,1024]{2,1,0:T(8,128)(2,1)S(1)} %copy-done.4), kind=kLoop, calls=%fused_computation.6 | loop fusion | flops 8388608 | bytes 14680064 | tf_op jit(solution)/shard_map/convert_element_type | solution.py:111
  239.7 18.1 %collective-permute-done.6 = bf16[256,1024]{1,0:T(8,128)(2,1)S(1)} collective-permute-done((bf16[256,1024]{1,0:T(8,128)(2,1)S(1)}, bf16[256,1024]{1,0:T(8,128)(2,1)S(1)}, u32[]{:S(2)}, u32[]{:S(2)}) %collective-permute-start.6) | collective-permute-done | bytes 524320 | tf_op jit(solution)/shard_map/ppermute | solution.py:53
  257.9 0.2 bitcast_add_fusion
  258.0 1.0 slice_bitcast_fusion
  (14 shorter events, 0.0 us)
Async XLA Ops:
  0.6 112.2 %copy-start = (bf16[1,1024,1024]{2,1,0:T(8,128)(2,1)S(1)}, bf16[1,1024,1024]{2,1,0:T(8,128)(2,1)}, u32[]{:S(2)}) copy-start(bf16[1,1024,1024]{2,1,0:T(8,128)(2,1)} %param.7) | copy-start | bytes 6291460
  0.6 3.4 %copy-start.2 = (bf16[1,1024,1024]{2,1,0:T(8,128)(2,1)S(1)}, bf16[1,1024,1024]{2,1,0:T(8,128)(2,1)}, u32[]{:S(2)}) copy-start(bf16[1,1024,1024]{2,1,0:T(8,128)(2,1)} %param.4) | copy-start | bytes 6291460
  0.7 3.6 %copy-start.8 = (bf16[1,1024,1024]{2,1,0:T(8,128)(2,1)S(1)}, bf16[1,1024,1024]{2,1,0:T(8,128)(2,1)}, u32[]{:S(2)}) copy-start(bf16[1,1024,1024]{2,1,0:T(8,128)(2,1)} %param.6) | copy-start | bytes 6291460
  112.8 2.5 copy-start.7
  117.7 55.1 %all-to-all-start.2 = ((bf16[1,1,32,32,1024]{4,2,1,0,3:T(8,128)(2,1)}), bf16[1,1,32,32,1024]{4,2,1,0,3:T(8,128)(2,1)}, u32[]{:S(2)}, u32[]{:S(2)}) async-start(bf16[1,1,32,32,1024]{4,2,1,0,3:T(8,128)(2,1)} %copy.24), calls=%async_computation.2 | async-start | bytes 4194304 | tf_op jit(solution)/shard_map/all_to_all | solution.py:67
  129.6 5.3 %copy-start.6 = (bf16[1,1,32,32,1,1024]{5,3,2,4,1,0:T(8,128)(2,1)S(1)}, bf16[1,1,32,32,1,1024]{5,3,2,4,1,0:T(8,128)(2,1)}, u32[]{:S(2)}) copy-start(bf16[1,1,32,32,1,1024]{5,3,2,4,1,0:T(8,128)(2,1)} %get-tuple-element.15) | copy-start | bytes 6291460
  129.8 15.2 %collective-permute-start = (bf16[2,128,1024]{2,1,0:T(8,128)(2,1)S(1)}, bf16[2,128,1024]{2,1,0:T(8,128)(2,1)S(1)}, u32[]{:S(2)}, u32[]{:S(2)}) collective-permute-start(bf16[2,128,1024]{2,1,0:T(8,128)(2,1)S(1)} %get-tuple-element.21), channel_id=1, source_target_pairs={{0,32},{32,64},{64,96},{96,0},{128,160},{160,192},{192,224},{224,1... | collective-permute-start | bytes 1572872 | tf_op jit(solution)/shard_map/ppermute | solution.py:41
  131.4 14.8 %collective-permute-start.2 = (bf16[2,128,1024]{2,1,0:T(8,128)(2,1)S(1)}, bf16[2,128,1024]{2,1,0:T(8,128)(2,1)S(1)}, u32[]{:S(2)}, u32[]{:S(2)}) collective-permute-start(bf16[2,128,1024]{2,1,0:T(8,128)(2,1)S(1)} %get-tuple-element.22), channel_id=1, source_target_pairs={{0,96},{32,0},{64,32},{96,64},{128,224},{160,128},{192,160},{224,1... | collective-permute-start | bytes 1572872 | tf_op jit(solution)/shard_map/ppermute | solution.py:41
  133.1 24.1 %collective-permute-start.1 = (bf16[2,128,1024]{2,1,0:T(8,128)(2,1)S(1)}, bf16[2,128,1024]{2,1,0:T(8,128)(2,1)S(1)}, u32[]{:S(2)}, u32[]{:S(2)}) collective-permute-start(bf16[2,128,1024]{2,1,0:T(8,128)(2,1)S(1)} %get-tuple-element.23), channel_id=1, source_target_pairs={{0,64},{32,96},{64,0},{96,32},{128,192},{160,224},{192,128},{224,1... | collective-permute-start | bytes 1572872 | tf_op jit(solution)/shard_map/ppermute | solution.py:41
  162.9 17.2 %copy-start.3 = (bf16[1,1024,1024]{2,1,0:T(8,128)(2,1)S(1)}, bf16[1,1024,1024]{2,1,0:T(8,128)(2,1)}, u32[]{:S(2)}) copy-start(bf16[1,1024,1024]{2,1,0:T(8,128)(2,1)} %param.4) | copy-start | bytes 6291460
  172.8 55.2 %all-to-all-start.1 = ((bf16[1,1,32,32,1024]{4,2,1,0,3:T(8,128)(2,1)}), bf16[1,1,32,32,1024]{4,2,1,0,3:T(8,128)(2,1)}, u32[]{:S(2)}, u32[]{:S(2)}) async-start(bf16[1,1,32,32,1024]{4,2,1,0,3:T(8,128)(2,1)} %copy.23), calls=%async_computation.1 | async-start | bytes 4194304 | tf_op jit(solution)/shard_map/all_to_all | solution.py:67
  184.1 5.3 %copy-start.9 = (bf16[1,1024,1024]{2,1,0:T(8,128)(2,1)S(1)}, bf16[1,1024,1024]{2,1,0:T(8,128)(2,1)}, u32[]{:S(2)}) copy-start(bf16[1,1024,1024]{2,1,0:T(8,128)(2,1)} %param.6) | copy-start | bytes 6291460
  184.2 15.2 %collective-permute-start.3 = (bf16[2,128,1024]{2,1,0:T(8,128)(2,1)S(1)}, bf16[2,128,1024]{2,1,0:T(8,128)(2,1)S(1)}, u32[]{:S(2)}, u32[]{:S(2)}) collective-permute-start(bf16[2,128,1024]{2,1,0:T(8,128)(2,1)S(1)} %get-tuple-element.18), channel_id=1, source_target_pairs={{0,32},{32,64},{64,96},{96,0},{128,160},{160,192},{192,224},{224,1... | collective-permute-start | bytes 1572872 | tf_op jit(solution)/shard_map/ppermute | solution.py:41
  185.8 24.3 %collective-permute-start.5 = (bf16[2,128,1024]{2,1,0:T(8,128)(2,1)S(1)}, bf16[2,128,1024]{2,1,0:T(8,128)(2,1)S(1)}, u32[]{:S(2)}, u32[]{:S(2)}) collective-permute-start(bf16[2,128,1024]{2,1,0:T(8,128)(2,1)S(1)} %get-tuple-element.19), channel_id=1, source_target_pairs={{0,96},{32,0},{64,32},{96,64},{128,224},{160,128},{192,160},{224,1... | collective-permute-start | bytes 1572872 | tf_op jit(solution)/shard_map/ppermute | solution.py:41
  187.6 24.1 %collective-permute-start.4 = (bf16[2,128,1024]{2,1,0:T(8,128)(2,1)S(1)}, bf16[2,128,1024]{2,1,0:T(8,128)(2,1)S(1)}, u32[]{:S(2)}, u32[]{:S(2)}) collective-permute-start(bf16[2,128,1024]{2,1,0:T(8,128)(2,1)S(1)} %get-tuple-element.20), channel_id=1, source_target_pairs={{0,64},{32,96},{64,0},{96,32},{128,192},{160,224},{192,128},{224,1... | collective-permute-start | bytes 1572872 | tf_op jit(solution)/shard_map/ppermute | solution.py:41
  228.0 4.8 %copy-start.5 = (bf16[1,1024,1024]{2,1,0:T(8,128)(2,1)S(1)}, bf16[1,1024,1024]{2,1,0:T(8,128)(2,1)}, u32[]{:S(2)}) copy-start(bf16[1,1024,1024]{2,1,0:T(8,128)(2,1)} %param.5) | copy-start | bytes 6291460
  228.1 4.7 %copy-start.4 = (bf16[1,1024,1024]{2,1,0:T(8,128)(2,1)S(1)}, bf16[1,1024,1024]{2,1,0:T(8,128)(2,1)}, u32[]{:S(2)}) copy-start(bf16[1,1024,1024]{2,1,0:T(8,128)(2,1)} %param.4) | copy-start | bytes 6291460
  228.3 29.6 %collective-permute-start.6 = (bf16[256,1024]{1,0:T(8,128)(2,1)S(1)}, bf16[256,1024]{1,0:T(8,128)(2,1)S(1)}, u32[]{:S(2)}, u32[]{:S(2)}) collective-permute-start(bf16[256,1024]{1,0:T(8,128)(2,1)S(1)} %fusion.31), channel_id=1, source_target_pairs={{0,128},{32,160},{64,192},{96,224},{128,0},{160,32},{192,64},{224,... | collective-permute-start | bytes 1572872 | tf_op jit(solution)/shard_map/ppermute | solution.py:53
  232.8 26.3 %copy-start.1 = (bf16[1,1024,1024]{2,1,0:T(8,128)(2,1)S(1)}, bf16[1,1024,1024]{2,1,0:T(8,128)(2,1)}, u32[]{:S(2)}) copy-start(bf16[1,1024,1024]{2,1,0:T(8,128)(2,1)} %param.7) | copy-start | bytes 6291460

commit v11 on v7

--- a/solution.py
+++ b/solution.py
@@ -56,7 +56,7 @@
         return None
 
 
-def _dp_reduce(part, ring, relays=None):
+def _dp_reduce(part, ring):
     ndp = lax.axis_size("dp")
     groups = ndp // ring
     rows = part.shape[0] // ndp
@@ -70,13 +70,20 @@
         piece = lax.dynamic_index_in_dim(chunks, (lo + s) % ring, axis=1, keepdims=False)
         perm = [(g * ring + t, g * ring + (t + s) % ring) for g in range(groups) for t in range(ring)]
         acc = acc + lax.ppermute(piece, "dp", perm).astype(jnp.float32)
+    return acc
+
+
+def _dp_finish(acc, ring, relays=None):
+    ndp = lax.axis_size("dp")
+    groups = ndp // ring
+    hi = lax.axis_index("dp") // ring
     own = lax.dynamic_index_in_dim(acc, hi, axis=0, keepdims=False)
     if relays is not None and groups == 2:
         piece = lax.dynamic_index_in_dim(acc, 1 - hi, axis=0, keepdims=False).astype(jnp.bfloat16)
-        cut = rows // 2
+        cut = piece.shape[0] // 2
         up = lax.ppermute(piece[:cut], ("dp", "seq"), relays[0])
+        down = lax.ppermute(piece[cut:], ("dp", "seq"), relays[2])
         up = lax.ppermute(up, ("dp", "seq"), relays[1])
-        down = lax.ppermute(piece[cut:], ("dp", "seq"), relays[2])
         down = lax.ppermute(down, ("dp", "seq"), relays[3])
         return own + jnp.concatenate([up, down]).astype(jnp.float32)
     for s in range(1, groups):
@@ -96,18 +103,10 @@
 
 def _from_moved(data, count, rows):
     seqs, block, width = data.shape
-    return _from_sendbuf(_sendbuf(data, count, rows), count)
-
-
-def _sendbuf(data, count, rows):
-    seqs, block, width = data.shape
-    return jnp.swapaxes(data.reshape(seqs, rows, count, width), 1, 2)
-
-
-def _from_sendbuf(buf, count):
-    seqs, _, rows, width = buf.shape
-    out = lax.all_to_all(buf, "seq", split_axis=1, concat_axis=1, tiled=True)
-    return out.reshape(seqs, count * rows, width)
+    out = lax.all_to_all(
+        data.reshape(seqs, 1, rows, count, width), "seq", split_axis=3, concat_axis=1, tiled=True
+    )
+    return out.reshape(seqs, block, width)
 
 
 def local(inputs, cotangent, factor_one, factor_two, ring, relays):
@@ -135,12 +134,15 @@
         jnp.bfloat16
     )
     part_two = jnp.einsum("spc,sqc->pq", gated_moved, moved, preferred_element_type=jnp.float32)
-    grad_two = _dp_reduce(part_two.astype(jnp.bfloat16), ring, relays)
-    second = _sendbuf(second, count, rows)
-    second, back_moved, grad_two = lax.optimization_barrier((second, back_moved, grad_two))
-    monarch = _from_sendbuf(second, count)
+    acc_two = _dp_reduce(part_two.astype(jnp.bfloat16), ring)
+    second, acc_two = lax.optimization_barrier((second, acc_two))
+    monarch = _from_moved(second, count, rows)
     part_one = jnp.einsum("skc,sjc->kj", back_moved, inputs, preferred_element_type=jnp.float32)
-    grad_one = _dp_reduce(part_one.astype(jnp.bfloat16), ring, relays)
+    acc_one = _dp_reduce(part_one.astype(jnp.bfloat16), ring)
+    monarch, acc_one, acc_two = lax.optimization_barrier((monarch, acc_one, acc_two))
+    both = _dp_finish(jnp.concatenate([acc_one, acc_two], axis=1), ring, relays)
+    grad_one = both[: acc_one.shape[1]]
+    grad_two = both[acc_one.shape[1] :]
     spread = _rowmajor(jnp.einsum("kj,skc->sjc", fone, back_moved, preferred_element_type=jnp.float32))
     spread = lax.optimization_barrier(spread)
     mfull = monarch.astype(jnp.float32)

time: 276 us -> 266 us (0.964); the launches traced: 274 us -> 261 us
  starting transfers between devices: 61.5 us -> 33 us
  waiting for transfers between devices: 59.3 us -> 76.3 us
  other arithmetic: 15.5 us -> 11.6 us
  local copies, waits for them, and re-layouts: 11.8 us -> 15.2 us
    ppermute x8 -> x4, starting transfers between devices: 35.4 us -> 8.39 us  [the longest x1 3.82 us: _dp_finish(): down = lax.ppermute(down, ('dp', 'seq'), relays[3])]
    all_to_all x2, waiting for transfers between devices: 0.01 us -> 21.7 us  [_from_moved(): lax.all_to_all(data.reshape(seqs, 1, rows, count, width), 'seq', split_ax...]
    ppermute x6, waiting for transfers between devices: 45 us -> 41 us  [_dp_reduce(): acc = acc + lax.ppermute(piece, 'dp', perm).astype(jnp.float32)]
    optimization_barrier x0 -> x1, local copies, waits for them, and re-layouts: none -> 2.86 us  [local(): second, acc_two = lax.optimization_barrier((second, acc_two))]
    ppermute x8 -> x4, waiting for transfers between devices: 14.3 us -> 13.6 us  [the longest x1 11.1 us: _dp_finish(): up = lax.ppermute(up, ('dp', 'seq'), relays[1])]
  transfers between devices with their start and end apart: 16 -> 12, of which waited for: 10 -> 10; matrix products, arithmetic and copies ran while one was open for 10% -> 12% of each run, Pallas kernels for 0% -> 0%
where the time goes in v11:
time: 266 us; the launch traced here: 261 us
  blocking collectives  102 us (38%)
  waiting for transfers between devices  76.3 us (29%)
  starting transfers between devices  33 us (12%)
  matrix products  22.4 us (8%)
  local copies, waits for them, and re-layouts  15.2 us (6%)
  other arithmetic  11.6 us (4%)
    all_to_all x1, blocking collectives, local(): in1 = lax.all_to_all(out1, 'seq', split_axis=1, concat_axis=3, tiled=True)  102 us
    ppermute x6, waiting for transfers between devices, _dp_reduce(): acc = acc + lax.ppermute(piece, 'dp', perm).astype(jnp.float32)  41 us
    all_to_all x2, waiting for transfers between devices, _from_moved(): lax.all_to_all(data.reshape(seqs, 1, rows, count, width), 'seq', split_ax...  21.7 us
    all_to_all x2, starting transfers between devices, _from_moved(): lax.all_to_all(data.reshape(seqs, 1, rows, count, width), 'seq', split_ax...  14.4 us
    ppermute x1, waiting for transfers between devices, _dp_finish(): up = lax.ppermute(up, ('dp', 'seq'), relays[1])  11.1 us
    ppermute x6, starting transfers between devices, _dp_reduce(): acc = acc + lax.ppermute(piece, 'dp', perm).astype(jnp.float32)  10.3 us
    convert_element_type x1, other arithmetic, local(): grad_input = _rowmajor((dyfull * mfull + spread).astype(jnp.bfloat16))  5.62 us
  transfers between devices with their start and end apart: 12, of which 10 were waited for; matrix products, arithmetic and copies ran while one was open for 12% of the time, Pallas kernels for 0%

profile of v11, /device:TPU:8, one launch (start us, length us, event | category | flops | bytes accessed | tf_op | source)
XLA Modules:
  0.0 261.2 jit_solution(13342319863687927403)
XLA Ops:
  0.6 0.0 copy-start
  0.7 3.4 %fusion = bf16[1,1024,1024]{2,1,0:T(8,128)(2,1)S(1)} fusion(bf16[1,1024,1024]{2,1,0:T(8,128)(2,1)} %param.4, bf16[1,1024,1024]{2,1,0:T(8,128)(2,1)} %param.5), kind=kLoop, calls=%fused_computation.3 | loop fusion | flops 4194304 | bytes 6291456 | tf_op jit(solution)/shard_map/convert_element_type | solution.py:120
  4.0 0.2 copy-done.8
  4.3 2.3 fusion.17
  6.6 0.4 pad_maximum_fusion
  7.0 101.7 %all_to_all.45 = bf16[2,32,32,1,1024]{4,2,0,3,1:T(8,128)(2,1)S(1)} all-to-all(bf16[2,32,32,1,1024]{4,2,0,3,1:T(8,128)(2,1)S(1)} %pad_maximum_fusion), channel_id=1, replica_groups=mesh['dp'=8,'seq'=32] {'seq'}, dimensions={1} | all-to-all | bytes 8388608 | tf_op jit(solution)/shard_map/all_to_all | solution.py:125
  108.7 2.3 copy.29
  111.0 1.8 fusion.31
  112.8 2.5 fusion.24
  115.2 2.5 copy.24
  117.7 7.2 %all-to-all-start.2 = ((bf16[1,1,32,32,1024]{4,2,1,0,3:T(8,128)(2,1)}), bf16[1,1,32,32,1024]{4,2,1,0,3:T(8,128)(2,1)}, u32[]{:S(2)}, u32[]{:S(2)}) async-start(bf16[1,1,32,32,1024]{4,2,1,0,3:T(8,128)(2,1)} %copy.24), calls=%async_computation.2 | async-start | bytes 4194304 | tf_op jit(solution)/shard_map/all_to_all | solution.py:106
  125.0 4.6 %convolution_convert_fusion = bf16[1024,1024]{1,0:T(8,128)(2,1)S(1)} fusion(bf16[1024,1024]{1,0:T(8,128)(2,1)} %bitcast.115, bf16[1024,1024]{1,0:T(8,128)(2,1)} %bitcast.112), kind=kOutput, calls=%fused_computation.24 | convolution fusion | flops 2148532224 | bytes 6291456 | tf_op jit(solution)/shard_map/spc,sqc->pq/dot_general | solution.py:136
  129.6 0.2 dynamic-slice_bitcast_fusion.5
  129.8 1.6 collective-permute-start
  131.3 1.7 collective-permute-start.2
  133.1 1.8 collective-permute-start.1
  134.9 3.7 %convert_bitcast_fusion = bf16[1,1024,1024]{1,2,0:T(8,128)(2,1)} fusion(bf16[1024,1024]{1,0:T(8,128)(2,1)S(1)} %bitcast.113, bf16[1,1024,1024]{2,1,0:T(8,128)(2,1)S(1)} %copy-done), kind=kOutput, calls=%fused_computation.20 | convolution fusion | flops 2148532224 | bytes 6291456 | tf_op jit(solution)/shard_map/pq,sqc->spc/dot_general | solution.py:133
  138.6 6.4 %collective-permute-done = bf16[2,128,1024]{2,1,0:T(8,128)(2,1)S(1)} collective-permute-done((bf16[2,128,1024]{2,1,0:T(8,128)(2,1)S(1)}, bf16[2,128,1024]{2,1,0:T(8,128)(2,1)S(1)}, u32[]{:S(2)}, u32[]{:S(2)}) %collective-permute-start) | collective-permute-done | bytes 524320 | tf_op jit(solution)/shard_map/ppermute | solution.py:72
  145.0 10.5 %collective-permute-done.2 = bf16[2,128,1024]{2,1,0:T(8,128)(2,1)S(1)} collective-permute-done((bf16[2,128,1024]{2,1,0:T(8,128)(2,1)S(1)}, bf16[2,128,1024]{2,1,0:T(8,128)(2,1)S(1)}, u32[]{:S(2)}, u32[]{:S(2)}) %collective-permute-start.2) | collective-permute-done | bytes 524320 | tf_op jit(solution)/shard_map/ppermute | solution.py:72
  155.5 1.7 collective-permute-done.1
  157.2 0.3 fusion.30
  157.6 2.9 %copy.22 = bf16[1,1024,1024]{2,1,0:T(8,128)(2,1)S(1)} copy(bf16[1,1024,1024]{1,2,0:T(8,128)(2,1)} %convert_bitcast_fusion) | data formatting | bytes 4194304 | tf_op jit(solution)/shard_map/optimization_barrier | solution.py:138
  160.4 2.5 copy.23
  162.9 9.9 %all-to-all-done.2 = bf16[1,1,32,32,1024]{4,2,1,0,3:T(8,128)(2,1)} async-done(((bf16[1,1,32,32,1024]{4,2,1,0,3:T(8,128)(2,1)}), bf16[1,1,32,32,1024]{4,2,1,0,3:T(8,128)(2,1)}, u32[]{:S(2)}, u32[]{:S(2)}) %all-to-all-start.2) | async-done | bytes 2097184 | tf_op jit(solution)/shard_map/all_to_all | solution.py:106
  172.8 7.2 %all-to-all-start.1 = ((bf16[1,1,32,32,1024]{4,2,1,0,3:T(8,128)(2,1)}), bf16[1,1,32,32,1024]{4,2,1,0,3:T(8,128)(2,1)}, u32[]{:S(2)}, u32[]{:S(2)}) async-start(bf16[1,1,32,32,1024]{4,2,1,0,3:T(8,128)(2,1)} %copy.23), calls=%async_computation.1 | async-start | bytes 4194304 | tf_op jit(solution)/shard_map/all_to_all | solution.py:106
  180.1 5.3 %fusion.14 = bf16[1024,1024]{1,0:T(8,128)(2,1)} fusion(bf16[1024,1024]{1,0:T(8,128)(2,1)} %bitcast.30, bf16[1,1024,1024]{2,1,0:T(8,128)(2,1)S(1)} %copy-done.3), kind=kOutput, calls=%fused_computation.21 | convolution fusion | flops 2148532224 | bytes 6291456 | tf_op jit(solution)/shard_map/skc,sjc->kj/dot_general | solution.py:140
  185.3 1.6 dynamic-slice_bitcast_fusion.2
  186.9 1.6 collective-permute-start.3
  188.5 1.7 collective-permute-start.5
  190.2 1.8 collective-permute-start.4
  192.0 10.1 %collective-permute-done.3 = bf16[2,128,1024]{2,1,0:T(8,128)(2,1)S(1)} collective-permute-done((bf16[2,128,1024]{2,1,0:T(8,128)(2,1)S(1)}, bf16[2,128,1024]{2,1,0:T(8,128)(2,1)S(1)}, u32[]{:S(2)}, u32[]{:S(2)}) %collective-permute-start.3) | collective-permute-done | bytes 524320 | tf_op jit(solution)/shard_map/ppermute | solution.py:72
  202.1 10.6 %collective-permute-done.5 = bf16[2,128,1024]{2,1,0:T(8,128)(2,1)} collective-permute-done((bf16[2,128,1024]{2,1,0:T(8,128)(2,1)S(1)}, bf16[2,128,1024]{2,1,0:T(8,128)(2,1)}, u32[]{:S(2)}, u32[]{:S(2)}) %collective-permute-start.5) | collective-permute-done | bytes 524320 | tf_op jit(solution)/shard_map/ppermute | solution.py:72
  212.8 1.7 collective-permute-done.4
  214.5 1.7 fusion.28
  216.2 11.8 %all-to-all-done.1 = bf16[1,1,32,32,1024]{4,2,1,0,3:T(8,128)(2,1)} async-done(((bf16[1,1,32,32,1024]{4,2,1,0,3:T(8,128)(2,1)}), bf16[1,1,32,32,1024]{4,2,1,0,3:T(8,128)(2,1)}, u32[]{:S(2)}, u32[]{:S(2)}) %all-to-all-start.1) | async-done | bytes 2097184 | tf_op jit(solution)/shard_map/all_to_all | solution.py:106
  228.0 0.1 constant_dynamic-update-slice_fusion.1
  228.1 0.1 constant_dynamic-update-slice_fusion
  228.2 0.1 dynamic-slice_convert_fusion
  228.3 0.2 collective-permute-start.6
  228.5 3.2 %collective-permute-start.8 = (bf16[128,1024]{1,0:T(8,128)(2,1)S(1)}, bf16[128,1024]{1,0:T(8,128)(2,1)S(1)}, u32[]{:S(2)}, u32[]{:S(2)}) collective-permute-start(bf16[128,1024]{1,0:T(8,128)(2,1)S(1)} %get-tuple-element.27), channel_id=1, source_target_pairs={{0,134},{1,135},{2,0},{3,1},{4,2},{5,3},{6,4},{7,5},{8,142},{9,143... | collective-permute-start | bytes 786440 | tf_op jit(solution)/shard_map/ppermute | solution.py:85
  231.7 4.1 %convolution_bitcast_fusion = f32[1,1024,1024]{2,1,0:T(8,128)S(1)} fusion(bf16[1024,1024]{1,0:T(8,128)(2,1)} %bitcast.30, bf16[1,1024,1024]{2,1,0:T(8,128)(2,1)S(1)} %copy-done.9), kind=kOutput, calls=%fused_computation.9 | convolution fusion | flops 2147483648 | bytes 8388608 | tf_op jit(solution)/shard_map/kj,skc->sjc/dot_general | solution.py:146
  235.7 2.4 collective-permute-done.6
  238.2 1.2 collective-permute-start.7
  239.4 3.8 %collective-permute-start.9 = (bf16[128,1024]{1,0:T(8,128)(2,1)S(1)}, bf16[128,1024]{1,0:T(8,128)(2,1)S(1)}, u32[]{:S(2)}, u32[]{:S(2)}) collective-permute-start(bf16[128,1024]{1,0:T(8,128)(2,1)S(1)} %collective-permute-done.8), channel_id=1, source_target_pairs={{0,130},{1,131},{2,132},{3,133},{4,134},{5,135},{6,0},{7,1},{8,138... | collective-permute-start | bytes 786440 | tf_op jit(solution)/shard_map/ppermute | solution.py:87
  243.2 5.6 %fusion.3 = (bf16[1,1024,1024]{2,1,0:T(8,128)(2,1)}, bf16[1,1024,1024]{2,1,0:T(8,128)(2,1)}) fusion(f32[1,1024,1024]{2,1,0:T(8,128)S(1)} %convolution_bitcast_fusion, bf16[1,1024,1024]{2,1,0:T(8,128)(2,1)} %bitcast.24, bf16[1,1024,1024]{2,1,0:T(8,128)(2,1)S(1)} %copy-done.5, bf16[1,1024,1024]{2,1,0:T(8,128)(2,1)S(1)} %copy-done.4), kind=kLoop, calls=%fused_computation.6 | loop fusion | flops 8388608 | bytes 14680064 | tf_op jit(solution)/shard_map/convert_element_type | solution.py:150
  248.8 11.1 %collective-permute-done.7 = bf16[128,1024]{1,0:T(8,128)(2,1)S(1)} collective-permute-done((bf16[128,1024]{1,0:T(8,128)(2,1)S(1)}, bf16[128,1024]{1,0:T(8,128)(2,1)S(1)}, u32[]{:S(2)}, u32[]{:S(2)}) %collective-permute-start.7) | collective-permute-done | bytes 262176 | tf_op jit(solution)/shard_map/ppermute | solution.py:86
  260.0 0.2 bitcast_add_fusion
  260.1 1.0 slice_bitcast_fusion
  (21 shorter events, 0.1 us)
Async XLA Ops:
  0.6 112.1 %copy-start = (bf16[1,1024,1024]{2,1,0:T(8,128)(2,1)S(1)}, bf16[1,1024,1024]{2,1,0:T(8,128)(2,1)}, u32[]{:S(2)}) copy-start(bf16[1,1024,1024]{2,1,0:T(8,128)(2,1)} %param.7) | copy-start | bytes 6291460
  0.6 3.4 %copy-start.2 = (bf16[1,1024,1024]{2,1,0:T(8,128)(2,1)S(1)}, bf16[1,1024,1024]{2,1,0:T(8,128)(2,1)}, u32[]{:S(2)}) copy-start(bf16[1,1024,1024]{2,1,0:T(8,128)(2,1)} %param.4) | copy-start | bytes 6291460
  0.7 3.6 %copy-start.8 = (bf16[1,1024,1024]{2,1,0:T(8,128)(2,1)S(1)}, bf16[1,1024,1024]{2,1,0:T(8,128)(2,1)}, u32[]{:S(2)}) copy-start(bf16[1,1024,1024]{2,1,0:T(8,128)(2,1)} %param.6) | copy-start | bytes 6291460
  112.8 2.5 copy-start.7
  117.7 55.1 %all-to-all-start.2 = ((bf16[1,1,32,32,1024]{4,2,1,0,3:T(8,128)(2,1)}), bf16[1,1,32,32,1024]{4,2,1,0,3:T(8,128)(2,1)}, u32[]{:S(2)}, u32[]{:S(2)}) async-start(bf16[1,1,32,32,1024]{4,2,1,0,3:T(8,128)(2,1)} %copy.24), calls=%async_computation.2 | async-start | bytes 4194304 | tf_op jit(solution)/shard_map/all_to_all | solution.py:106
  129.6 5.3 %copy-start.6 = (bf16[1,1,32,32,1,1024]{5,3,2,4,1,0:T(8,128)(2,1)S(1)}, bf16[1,1,32,32,1,1024]{5,3,2,4,1,0:T(8,128)(2,1)}, u32[]{:S(2)}) copy-start(bf16[1,1,32,32,1,1024]{5,3,2,4,1,0:T(8,128)(2,1)} %get-tuple-element.15) | copy-start | bytes 6291460
  129.8 15.2 %collective-permute-start = (bf16[2,128,1024]{2,1,0:T(8,128)(2,1)S(1)}, bf16[2,128,1024]{2,1,0:T(8,128)(2,1)S(1)}, u32[]{:S(2)}, u32[]{:S(2)}) collective-permute-start(bf16[2,128,1024]{2,1,0:T(8,128)(2,1)S(1)} %get-tuple-element.21), channel_id=1, source_target_pairs={{0,32},{32,64},{64,96},{96,0},{128,160},{160,192},{192,224},{224,1... | collective-permute-start | bytes 1572872 | tf_op jit(solution)/shard_map/ppermute | solution.py:72
  131.3 24.2 %collective-permute-start.2 = (bf16[2,128,1024]{2,1,0:T(8,128)(2,1)S(1)}, bf16[2,128,1024]{2,1,0:T(8,128)(2,1)S(1)}, u32[]{:S(2)}, u32[]{:S(2)}) collective-permute-start(bf16[2,128,1024]{2,1,0:T(8,128)(2,1)S(1)} %get-tuple-element.22), channel_id=1, source_target_pairs={{0,96},{32,0},{64,32},{96,64},{128,224},{160,128},{192,160},{224,1... | collective-permute-start | bytes 1572872 | tf_op jit(solution)/shard_map/ppermute | solution.py:72
  133.1 24.1 %collective-permute-start.1 = (bf16[2,128,1024]{2,1,0:T(8,128)(2,1)S(1)}, bf16[2,128,1024]{2,1,0:T(8,128)(2,1)S(1)}, u32[]{:S(2)}, u32[]{:S(2)}) collective-permute-start(bf16[2,128,1024]{2,1,0:T(8,128)(2,1)S(1)} %get-tuple-element.23), channel_id=1, source_target_pairs={{0,64},{32,96},{64,0},{96,32},{128,192},{160,224},{192,128},{224,1... | collective-permute-start | bytes 1572872 | tf_op jit(solution)/shard_map/ppermute | solution.py:72
  162.9 17.1 %copy-start.3 = (bf16[1,1024,1024]{2,1,0:T(8,128)(2,1)S(1)}, bf16[1,1024,1024]{2,1,0:T(8,128)(2,1)}, u32[]{:S(2)}) copy-start(bf16[1,1024,1024]{2,1,0:T(8,128)(2,1)} %param.4) | copy-start | bytes 6291460
  172.8 55.2 %all-to-all-start.1 = ((bf16[1,1,32,32,1024]{4,2,1,0,3:T(8,128)(2,1)}), bf16[1,1,32,32,1024]{4,2,1,0,3:T(8,128)(2,1)}, u32[]{:S(2)}, u32[]{:S(2)}) async-start(bf16[1,1,32,32,1024]{4,2,1,0,3:T(8,128)(2,1)} %copy.23), calls=%async_computation.1 | async-start | bytes 4194304 | tf_op jit(solution)/shard_map/all_to_all | solution.py:106
  186.9 15.2 %collective-permute-start.3 = (bf16[2,128,1024]{2,1,0:T(8,128)(2,1)S(1)}, bf16[2,128,1024]{2,1,0:T(8,128)(2,1)S(1)}, u32[]{:S(2)}, u32[]{:S(2)}) collective-permute-start(bf16[2,128,1024]{2,1,0:T(8,128)(2,1)S(1)} %get-tuple-element.18), channel_id=1, source_target_pairs={{0,32},{32,64},{64,96},{96,0},{128,160},{160,192},{192,224},{224,1... | collective-permute-start | bytes 1572872 | tf_op jit(solution)/shard_map/ppermute | solution.py:72
  188.5 24.3 %collective-permute-start.5 = (bf16[2,128,1024]{2,1,0:T(8,128)(2,1)S(1)}, bf16[2,128,1024]{2,1,0:T(8,128)(2,1)}, u32[]{:S(2)}, u32[]{:S(2)}) collective-permute-start(bf16[2,128,1024]{2,1,0:T(8,128)(2,1)S(1)} %get-tuple-element.19), channel_id=1, source_target_pairs={{0,96},{32,0},{64,32},{96,64},{128,224},{160,128},{192,160},{224,1... | collective-permute-start | bytes 1572872 | tf_op jit(solution)/shard_map/ppermute | solution.py:72
  190.2 24.2 %collective-permute-start.4 = (bf16[2,128,1024]{2,1,0:T(8,128)(2,1)S(1)}, bf16[2,128,1024]{2,1,0:T(8,128)(2,1)}, u32[]{:S(2)}, u32[]{:S(2)}) collective-permute-start(bf16[2,128,1024]{2,1,0:T(8,128)(2,1)S(1)} %get-tuple-element.20), channel_id=1, source_target_pairs={{0,64},{32,96},{64,0},{96,32},{128,192},{160,224},{192,128},{224,1... | collective-permute-start | bytes 1572872 | tf_op jit(solution)/shard_map/ppermute | solution.py:72
  228.1 3.6 %copy-start.9 = (bf16[1,1024,1024]{2,1,0:T(8,128)(2,1)S(1)}, bf16[1,1024,1024]{2,1,0:T(8,128)(2,1)}, u32[]{:S(2)}) copy-start(bf16[1,1024,1024]{2,1,0:T(8,128)(2,1)} %param.6) | copy-start | bytes 6291460
  228.3 9.9 %collective-permute-start.6 = (bf16[128,1024]{1,0:T(8,128)(2,1)S(1)}, bf16[128,1024]{1,0:T(8,128)(2,1)S(1)}, u32[]{:S(2)}, u32[]{:S(2)}) collective-permute-start(bf16[128,1024]{1,0:T(8,128)(2,1)S(1)} %get-tuple-element.26), channel_id=1, source_target_pairs={{0,2},{1,3},{2,4},{3,5},{4,6},{5,7},{6,128},{7,129},{8,10},{9,11},... | collective-permute-start | bytes 786440 | tf_op jit(solution)/shard_map/ppermute | solution.py:84
  228.5 14.8 %copy-start.4 = (bf16[1,1024,1024]{2,1,0:T(8,128)(2,1)S(1)}, bf16[1,1024,1024]{2,1,0:T(8,128)(2,1)}, u32[]{:S(2)}) copy-start(bf16[1,1024,1024]{2,1,0:T(8,128)(2,1)} %param.4) | copy-start | bytes 6291460
  228.5 14.8 %copy-start.5 = (bf16[1,1024,1024]{2,1,0:T(8,128)(2,1)S(1)}, bf16[1,1024,1024]{2,1,0:T(8,128)(2,1)}, u32[]{:S(2)}) copy-start(bf16[1,1024,1024]{2,1,0:T(8,128)(2,1)} %param.5) | copy-start | bytes 6291460
  228.5 10.9 %collective-permute-start.8 = (bf16[128,1024]{1,0:T(8,128)(2,1)S(1)}, bf16[128,1024]{1,0:T(8,128)(2,1)S(1)}, u32[]{:S(2)}, u32[]{:S(2)}) collective-permute-start(bf16[128,1024]{1,0:T(8,128)(2,1)S(1)} %get-tuple-element.27), channel_id=1, source_target_pairs={{0,134},{1,135},{2,0},{3,1},{4,2},{5,3},{6,4},{7,5},{8,142},{9,143... | collective-permute-start | bytes 786440 | tf_op jit(solution)/shard_map/ppermute | solution.py:85
  238.2 21.8 %collective-permute-start.7 = (bf16[128,1024]{1,0:T(8,128)(2,1)S(1)}, bf16[128,1024]{1,0:T(8,128)(2,1)S(1)}, u32[]{:S(2)}, u32[]{:S(2)}) collective-permute-start(bf16[128,1024]{1,0:T(8,128)(2,1)S(1)} %collective-permute-done.6), channel_id=1, source_target_pairs={{0,6},{1,7},{2,128},{3,129},{4,130},{5,131},{6,132},{7,133},{8,14}... | collective-permute-start | bytes 786440 | tf_op jit(solution)/shard_map/ppermute | solution.py:86
  239.4 20.6 %collective-permute-start.9 = (bf16[128,1024]{1,0:T(8,128)(2,1)S(1)}, bf16[128,1024]{1,0:T(8,128)(2,1)S(1)}, u32[]{:S(2)}, u32[]{:S(2)}) collective-permute-start(bf16[128,1024]{1,0:T(8,128)(2,1)S(1)} %collective-permute-done.8), channel_id=1, source_target_pairs={{0,130},{1,131},{2,132},{3,133},{4,134},{5,135},{6,0},{7,1},{8,138... | collective-permute-start | bytes 786440 | tf_op jit(solution)/shard_map/ppermute | solution.py:87
  243.2 17.9 %copy-start.1 = (bf16[1,1024,1024]{2,1,0:T(8,128)(2,1)S(1)}, bf16[1,1024,1024]{2,1,0:T(8,128)(2,1)}, u32[]{:S(2)}) copy-start(bf16[1,1024,1024]{2,1,0:T(8,128)(2,1)} %param.7) | copy-start | bytes 6291460

commit v12 on v9

--- a/solution.py
+++ b/solution.py
@@ -95,14 +95,13 @@
         jnp.bfloat16
     )
     part_two = jnp.einsum("spc,sqc->pq", gated_moved, moved, preferred_element_type=jnp.float32)
-    acc_two = _dp_reduce(part_two.astype(jnp.bfloat16), ring)
-    second, acc_two = lax.optimization_barrier((second, acc_two))
+    grad_two = _dp_finish(_dp_reduce(part_two.astype(jnp.bfloat16), ring), ring)
+    second, grad_two = lax.optimization_barrier((second, grad_two))
     monarch = _from_moved(second, count, rows)
     part_one = jnp.einsum("skc,sjc->kj", back_moved, inputs, preferred_element_type=jnp.float32)
     acc_one = _dp_reduce(part_one.astype(jnp.bfloat16), ring)
-    monarch, acc_one, acc_two = lax.optimization_barrier((monarch, acc_one, acc_two))
+    monarch, acc_one = lax.optimization_barrier((monarch, acc_one))
     grad_one = _dp_finish(acc_one, ring)
-    grad_two = _dp_finish(acc_two, ring)
     spread = _rowmajor(jnp.einsum("kj,skc->sjc", fone, back_moved, preferred_element_type=jnp.float32))
     spread = lax.optimization_barrier(spread)
     mfull = monarch.astype(jnp.float32)

time: 261 us -> 263 us (level)
  waiting for transfers between devices: 75.6 us -> 71.4 us
  starting transfers between devices: 30.7 us -> 33.9 us
    all_to_all x2, waiting for transfers between devices: 25.9 us -> 21.2 us  [_from_moved(): lax.all_to_all(data.reshape(seqs, 1, rows, count, width), 'seq', split_ax...]
    ppermute x6, waiting for transfers between devices: 35 us -> 39.4 us  [_dp_reduce(): acc = acc + lax.ppermute(piece, 'dp', perm).astype(jnp.float32)]
    ppermute x2, waiting for transfers between devices: 14.7 us -> 10.8 us  [_dp_finish(): lax.ppermute(piece.astype(jnp.bfloat16), 'dp', perm).astype(jnp.float32)]
  transfers between devices with their start and end apart: 10 -> 10, of which waited for: 10 -> 10; matrix products, arithmetic and copies ran while one was open for 13% -> 14% of each run, Pallas kernels for 0% -> 0%
where the time goes in v12:
time: 263 us; the launch traced here: 261 us
  blocking collectives  102 us (39%)
  waiting for transfers between devices  71.4 us (27%)
  starting transfers between devices  33.9 us (13%)
  matrix products  23 us (9%)
  other arithmetic  15.6 us (6%)
  local copies, waits for them, and re-layouts  14.6 us (6%)
    all_to_all x1, blocking collectives, local(): in1 = lax.all_to_all(out1, 'seq', split_axis=1, concat_axis=3, tiled=True)  102 us
    ppermute x6, waiting for transfers between devices, _dp_reduce(): acc = acc + lax.ppermute(piece, 'dp', perm).astype(jnp.float32)  39.4 us
    all_to_all x2, waiting for transfers between devices, _from_moved(): lax.all_to_all(data.reshape(seqs, 1, rows, count, width), 'seq', split_ax...  21.2 us
    all_to_all x2, starting transfers between devices, _from_moved(): lax.all_to_all(data.reshape(seqs, 1, rows, count, width), 'seq', split_ax...  16.8 us
    ppermute x2, waiting for transfers between devices, _dp_finish(): lax.ppermute(piece.astype(jnp.bfloat16), 'dp', perm).astype(jnp.float32)  10.8 us
    ppermute x6, starting transfers between devices, _dp_reduce(): acc = acc + lax.ppermute(piece, 'dp', perm).astype(jnp.float32)  9.2 us
    convert_element_type x1, other arithmetic, local(): grad_input = _rowmajor((dyfull * mfull + spread).astype(jnp.bfloat16))  7.96 us
    ppermute x2, starting transfers between devices, _dp_finish(): lax.ppermute(piece.astype(jnp.bfloat16), 'dp', perm).astype(jnp.float32)  7.82 us
  transfers between devices with their start and end apart: 10, of which 10 were waited for; matrix products, arithmetic and copies ran while one was open for 14% of the time, Pallas kernels for 0%

profile of v12, /device:TPU:8, one launch (start us, length us, event | category | flops | bytes accessed | tf_op | source)
XLA Modules:
  0.0 261.1 jit_solution(23326888040950240)
XLA Ops:
  0.6 0.0 copy-start
  0.6 0.0 copy-start.2
  0.7 0.0 copy-start.7
  0.7 3.4 %fusion = bf16[1,1024,1024]{2,1,0:T(8,128)(2,1)S(1)} fusion(bf16[1,1024,1024]{2,1,0:T(8,128)(2,1)} %param.4, bf16[1,1024,1024]{2,1,0:T(8,128)(2,1)} %param.5), kind=kLoop, calls=%fused_computation.3 | loop fusion | flops 4194304 | bytes 6291456 | tf_op jit(solution)/shard_map/convert_element_type | solution.py:81
  4.0 0.0 copy-done.2
  4.0 0.2 copy-done.7
  4.3 2.3 fusion.17
  6.6 0.4 pad_maximum_fusion
  7.0 101.7 %all_to_all.45 = bf16[2,32,32,1,1024]{4,2,0,3,1:T(8,128)(2,1)S(1)} all-to-all(bf16[2,32,32,1,1024]{4,2,0,3,1:T(8,128)(2,1)S(1)} %pad_maximum_fusion), channel_id=1, replica_groups=mesh['dp'=8,'seq'=32] {'seq'}, dimensions={1} | all-to-all | bytes 8388608 | tf_op jit(solution)/shard_map/all_to_all | solution.py:86
  108.7 2.3 copy.29
  111.0 1.8 fusion.34
  112.8 2.5 fusion.24
  115.2 2.5 copy.24
  117.7 7.2 %all-to-all-start.2 = ((bf16[1,1,32,32,1024]{4,2,1,0,3:T(8,128)(2,1)}), bf16[1,1,32,32,1024]{4,2,1,0,3:T(8,128)(2,1)}, u32[]{:S(2)}, u32[]{:S(2)}) async-start(bf16[1,1,32,32,1024]{4,2,1,0,3:T(8,128)(2,1)} %copy.24), calls=%async_computation.2 | async-start | bytes 4194304 | tf_op jit(solution)/shard_map/all_to_all | solution.py:67
  125.0 4.6 %convolution_convert_fusion = bf16[1024,1024]{1,0:T(8,128)(2,1)S(1)} fusion(bf16[1024,1024]{1,0:T(8,128)(2,1)} %bitcast.120, bf16[1024,1024]{1,0:T(8,128)(2,1)} %bitcast.117), kind=kOutput, calls=%fused_computation.24 | convolution fusion | flops 2148532224 | bytes 6291456 | tf_op jit(solution)/shard_map/spc,sqc->pq/dot_general | solution.py:97
  129.6 1.3 copy-done.4
  130.9 0.9 dynamic-slice_bitcast_fusion.5
  131.8 1.5 collective-permute-start
  133.3 1.7 collective-permute-start.2
  135.1 1.8 collective-permute-start.1
  136.9 10.4 %collective-permute-done = bf16[2,128,1024]{2,1,0:T(8,128)(2,1)} collective-permute-done((bf16[2,128,1024]{2,1,0:T(8,128)(2,1)}, bf16[2,128,1024]{2,1,0:T(8,128)(2,1)}, u32[]{:S(2)}, u32[]{:S(2)}) %collective-permute-start) | collective-permute-done | bytes 524320 | tf_op jit(solution)/shard_map/ppermute | solution.py:41
  147.3 10.2 %collective-permute-done.2 = bf16[2,128,1024]{2,1,0:T(8,128)(2,1)} collective-permute-done((bf16[2,128,1024]{2,1,0:T(8,128)(2,1)S(1)}, bf16[2,128,1024]{2,1,0:T(8,128)(2,1)}, u32[]{:S(2)}, u32[]{:S(2)}) %collective-permute-start.2) | collective-permute-done | bytes 524320 | tf_op jit(solution)/shard_map/ppermute | solution.py:41
  157.5 2.0 collective-permute-done.1
  159.5 1.8 fusion.30
  161.4 4.6 %collective-permute-start.3 = (bf16[128,1024]{1,0:T(8,128)(2,1)S(1)}, bf16[128,1024]{1,0:T(8,128)(2,1)S(1)}, u32[]{:S(2)}, u32[]{:S(2)}) collective-permute-start(bf16[128,1024]{1,0:T(8,128)(2,1)S(1)} %fusion.32), channel_id=1, source_target_pairs={{0,128},{32,160},{64,192},{96,224},{128,0},{160,32},{192,64},{224,... | collective-permute-start | bytes 786440 | tf_op jit(solution)/shard_map/ppermute | solution.py:53
  166.0 3.7 %convert_bitcast_fusion = bf16[1,1024,1024]{1,2,0:T(8,128)(2,1)} fusion(bf16[1024,1024]{1,0:T(8,128)(2,1)S(1)} %bitcast.118, bf16[1,1024,1024]{2,1,0:T(8,128)(2,1)S(1)} %copy-done), kind=kOutput, calls=%fused_computation.20 | convolution fusion | flops 2148532224 | bytes 6291456 | tf_op jit(solution)/shard_map/pq,sqc->spc/dot_general | solution.py:94
  169.7 3.5 %collective-permute-done.3 = bf16[128,1024]{1,0:T(8,128)(2,1)S(1)} collective-permute-done((bf16[128,1024]{1,0:T(8,128)(2,1)S(1)}, bf16[128,1024]{1,0:T(8,128)(2,1)S(1)}, u32[]{:S(2)}, u32[]{:S(2)}) %collective-permute-start.3) | collective-permute-done | bytes 262176 | tf_op jit(solution)/shard_map/ppermute | solution.py:53
  173.3 0.9 bitcast_add_fusion.1
  174.1 2.9 %copy.22 = bf16[1,1024,1024]{2,1,0:T(8,128)(2,1)S(1)} copy(bf16[1,1024,1024]{1,2,0:T(8,128)(2,1)} %convert_bitcast_fusion) | data formatting | bytes 4194304 | tf_op jit(solution)/shard_map/optimization_barrier | solution.py:99
  177.0 2.5 copy.23
  179.5 4.6 %all-to-all-done.2 = bf16[1,1,32,32,1024]{4,2,1,0,3:T(8,128)(2,1)} async-done(((bf16[1,1,32,32,1024]{4,2,1,0,3:T(8,128)(2,1)}), bf16[1,1,32,32,1024]{4,2,1,0,3:T(8,128)(2,1)}, u32[]{:S(2)}, u32[]{:S(2)}) %all-to-all-start.2) | async-done | bytes 2097184 | tf_op jit(solution)/shard_map/all_to_all | solution.py:67
  184.1 9.7 %all-to-all-start.1 = ((bf16[1,1,32,32,1024]{4,2,1,0,3:T(8,128)(2,1)}), bf16[1,1,32,32,1024]{4,2,1,0,3:T(8,128)(2,1)}, u32[]{:S(2)}, u32[]{:S(2)}) async-start(bf16[1,1,32,32,1024]{4,2,1,0,3:T(8,128)(2,1)} %copy.23), calls=%async_computation.1 | async-start | bytes 4194304 | tf_op jit(solution)/shard_map/all_to_all | solution.py:67
  193.7 4.0 %fusion.14 = bf16[1024,1024]{1,0:T(8,128)(2,1)S(1)} fusion(bf16[1024,1024]{1,0:T(8,128)(2,1)} %bitcast.32, bf16[1,1024,1024]{2,1,0:T(8,128)(2,1)S(1)} %copy-done.3), kind=kOutput, calls=%fused_computation.21 | convolution fusion | flops 2148532224 | bytes 6291456 | tf_op jit(solution)/shard_map/skc,sjc->kj/dot_general | solution.py:101
  197.7 0.0 copy-start.8
  197.7 0.1 dynamic-slice_bitcast_fusion.2
  197.9 1.3 collective-permute-start.4
  199.1 2.3 collective-permute-start.6
  201.4 0.6 collective-permute-start.5
  202.0 6.0 %convolution_bitcast_fusion = f32[1,1024,1024]{2,1,0:T(8,128)} fusion(bf16[1024,1024]{1,0:T(8,128)(2,1)} %bitcast.32, bf16[1,1024,1024]{2,1,0:T(8,128)(2,1)S(1)} %copy-done.8), kind=kOutput, calls=%fused_computation.9 | convolution fusion | flops 2147483648 | bytes 8388608 | tf_op jit(solution)/shard_map/kj,skc->sjc/dot_general | solution.py:105
  208.0 6.0 %collective-permute-done.4 = bf16[2,128,1024]{2,1,0:T(8,128)(2,1)S(1)} collective-permute-done((bf16[2,128,1024]{2,1,0:T(8,128)(2,1)S(1)}, bf16[2,128,1024]{2,1,0:T(8,128)(2,1)S(1)}, u32[]{:S(2)}, u32[]{:S(2)}) %collective-permute-start.4) | collective-permute-done | bytes 524320 | tf_op jit(solution)/shard_map/ppermute | solution.py:41
  214.0 9.9 %collective-permute-done.6 = bf16[2,128,1024]{2,1,0:T(8,128)(2,1)S(1)} collective-permute-done((bf16[2,128,1024]{2,1,0:T(8,128)(2,1)S(1)}, bf16[2,128,1024]{2,1,0:T(8,128)(2,1)S(1)}, u32[]{:S(2)}, u32[]{:S(2)}) %collective-permute-start.6) | collective-permute-done | bytes 524320 | tf_op jit(solution)/shard_map/ppermute | solution.py:41
  223.8 0.9 collective-permute-done.5
  224.7 0.3 fusion.28
  225.1 16.6 %all-to-all-done.1 = bf16[1,1,32,32,1024]{4,2,1,0,3:T(8,128)(2,1)} async-done(((bf16[1,1,32,32,1024]{4,2,1,0,3:T(8,128)(2,1)}), bf16[1,1,32,32,1024]{4,2,1,0,3:T(8,128)(2,1)}, u32[]{:S(2)}, u32[]{:S(2)}) %all-to-all-start.1) | async-done | bytes 2097184 | tf_op jit(solution)/shard_map/all_to_all | solution.py:67
  241.7 3.2 %collective-permute-start.7 = (bf16[128,1024]{1,0:T(8,128)(2,1)S(1)}, bf16[128,1024]{1,0:T(8,128)(2,1)S(1)}, u32[]{:S(2)}, u32[]{:S(2)}) collective-permute-start(bf16[128,1024]{1,0:T(8,128)(2,1)S(1)} %fusion.33), channel_id=1, source_target_pairs={{0,128},{32,160},{64,192},{96,224},{128,0},{160,32},{192,64},{224,... | collective-permute-start | bytes 786440 | tf_op jit(solution)/shard_map/ppermute | solution.py:53
  245.0 8.0 %fusion.3 = (bf16[1,1024,1024]{2,1,0:T(8,128)(2,1)}, bf16[1,1024,1024]{2,1,0:T(8,128)(2,1)}) fusion(f32[1,1024,1024]{2,1,0:T(8,128)} %convolution_bitcast_fusion, bf16[1,1024,1024]{2,1,0:T(8,128)(2,1)} %bitcast.26, bf16[1,1024,1024]{2,1,0:T(8,128)(2,1)} %param.5, bf16[1,1024,1024]{2,1,0:T(8,128)(2,1)} %param.4), kind=kLoop, calls=%fused_computation.6 | loop fusion | flops 8388608 | bytes 14680064 | tf_op jit(solution)/shard_map/convert_element_type | solution.py:109
  252.9 7.3 %collective-permute-done.7 = bf16[128,1024]{1,0:T(8,128)(2,1)S(1)} collective-permute-done((bf16[128,1024]{1,0:T(8,128)(2,1)S(1)}, bf16[128,1024]{1,0:T(8,128)(2,1)S(1)}, u32[]{:S(2)}, u32[]{:S(2)}) %collective-permute-start.7) | collective-permute-done | bytes 262176 | tf_op jit(solution)/shard_map/ppermute | solution.py:53
  260.2 0.9 fusion.31
  (13 shorter events, 0.1 us)
Async XLA Ops:
  0.6 112.1 %copy-start = (bf16[1,1024,1024]{2,1,0:T(8,128)(2,1)S(1)}, bf16[1,1024,1024]{2,1,0:T(8,128)(2,1)}, u32[]{:S(2)}) copy-start(bf16[1,1024,1024]{2,1,0:T(8,128)(2,1)} %param.7) | copy-start | bytes 6291460
  0.6 3.4 %copy-start.2 = (bf16[1,1024,1024]{2,1,0:T(8,128)(2,1)S(1)}, bf16[1,1024,1024]{2,1,0:T(8,128)(2,1)}, u32[]{:S(2)}) copy-start(bf16[1,1024,1024]{2,1,0:T(8,128)(2,1)} %param.4) | copy-start | bytes 6291460
  0.7 3.6 %copy-start.7 = (bf16[1,1024,1024]{2,1,0:T(8,128)(2,1)S(1)}, bf16[1,1024,1024]{2,1,0:T(8,128)(2,1)}, u32[]{:S(2)}) copy-start(bf16[1,1024,1024]{2,1,0:T(8,128)(2,1)} %param.6) | copy-start | bytes 6291460
  112.8 2.5 copy-start.6
  117.7 66.3 %all-to-all-start.2 = ((bf16[1,1,32,32,1024]{4,2,1,0,3:T(8,128)(2,1)}), bf16[1,1,32,32,1024]{4,2,1,0,3:T(8,128)(2,1)}, u32[]{:S(2)}, u32[]{:S(2)}) async-start(bf16[1,1,32,32,1024]{4,2,1,0,3:T(8,128)(2,1)} %copy.24), calls=%async_computation.2 | async-start | bytes 4194304 | tf_op jit(solution)/shard_map/all_to_all | solution.py:67
  129.6 1.3 copy-start.4
  131.8 15.5 %collective-permute-start = (bf16[2,128,1024]{2,1,0:T(8,128)(2,1)}, bf16[2,128,1024]{2,1,0:T(8,128)(2,1)}, u32[]{:S(2)}, u32[]{:S(2)}) collective-permute-start(bf16[2,128,1024]{2,1,0:T(8,128)(2,1)} %get-tuple-element.19), channel_id=1, source_target_pairs={{0,32},{32,64},{64,96},{96,0},{128,160},{160,192},{192,224},{224,1... | collective-permute-start | bytes 1572872 | tf_op jit(solution)/shard_map/ppermute | solution.py:41
  133.3 24.2 %collective-permute-start.2 = (bf16[2,128,1024]{2,1,0:T(8,128)(2,1)S(1)}, bf16[2,128,1024]{2,1,0:T(8,128)(2,1)}, u32[]{:S(2)}, u32[]{:S(2)}) collective-permute-start(bf16[2,128,1024]{2,1,0:T(8,128)(2,1)S(1)} %get-tuple-element.20), channel_id=1, source_target_pairs={{0,96},{32,0},{64,32},{96,64},{128,224},{160,128},{192,160},{224,1... | collective-permute-start | bytes 1572872 | tf_op jit(solution)/shard_map/ppermute | solution.py:41
  135.1 24.5 %collective-permute-start.1 = (bf16[2,128,1024]{2,1,0:T(8,128)(2,1)S(1)}, bf16[2,128,1024]{2,1,0:T(8,128)(2,1)}, u32[]{:S(2)}, u32[]{:S(2)}) collective-permute-start(bf16[2,128,1024]{2,1,0:T(8,128)(2,1)S(1)} %get-tuple-element.21), channel_id=1, source_target_pairs={{0,64},{32,96},{64,0},{96,32},{128,192},{160,224},{192,128},{224,1... | collective-permute-start | bytes 1572872 | tf_op jit(solution)/shard_map/ppermute | solution.py:41
  136.9 29.1 %copy-start.5 = (bf16[1,1,32,32,1,1024]{5,3,2,4,1,0:T(8,128)(2,1)S(1)}, bf16[1,1,32,32,1,1024]{5,3,2,4,1,0:T(8,128)(2,1)}, u32[]{:S(2)}) copy-start(bf16[1,1,32,32,1,1024]{5,3,2,4,1,0:T(8,128)(2,1)} %get-tuple-element.13) | copy-start | bytes 6291460
  161.4 11.8 %collective-permute-start.3 = (bf16[128,1024]{1,0:T(8,128)(2,1)S(1)}, bf16[128,1024]{1,0:T(8,128)(2,1)S(1)}, u32[]{:S(2)}, u32[]{:S(2)}) collective-permute-start(bf16[128,1024]{1,0:T(8,128)(2,1)S(1)} %fusion.32), channel_id=1, source_target_pairs={{0,128},{32,160},{64,192},{96,224},{128,0},{160,32},{192,64},{224,... | collective-permute-start | bytes 786440 | tf_op jit(solution)/shard_map/ppermute | solution.py:53
  179.4 14.3 %copy-start.3 = (bf16[1,1024,1024]{2,1,0:T(8,128)(2,1)S(1)}, bf16[1,1024,1024]{2,1,0:T(8,128)(2,1)}, u32[]{:S(2)}) copy-start(bf16[1,1024,1024]{2,1,0:T(8,128)(2,1)} %param.4) | copy-start | bytes 6291460
  184.1 57.6 %all-to-all-start.1 = ((bf16[1,1,32,32,1024]{4,2,1,0,3:T(8,128)(2,1)}), bf16[1,1,32,32,1024]{4,2,1,0,3:T(8,128)(2,1)}, u32[]{:S(2)}, u32[]{:S(2)}) async-start(bf16[1,1,32,32,1024]{4,2,1,0,3:T(8,128)(2,1)} %copy.23), calls=%async_computation.1 | async-start | bytes 4194304 | tf_op jit(solution)/shard_map/all_to_all | solution.py:67
  197.7 4.3 %copy-start.8 = (bf16[1,1024,1024]{2,1,0:T(8,128)(2,1)S(1)}, bf16[1,1024,1024]{2,1,0:T(8,128)(2,1)}, u32[]{:S(2)}) copy-start(bf16[1,1024,1024]{2,1,0:T(8,128)(2,1)} %param.6) | copy-start | bytes 6291460
  197.9 16.1 %collective-permute-start.4 = (bf16[2,128,1024]{2,1,0:T(8,128)(2,1)S(1)}, bf16[2,128,1024]{2,1,0:T(8,128)(2,1)S(1)}, u32[]{:S(2)}, u32[]{:S(2)}) collective-permute-start(bf16[2,128,1024]{2,1,0:T(8,128)(2,1)S(1)} %get-tuple-element.16), channel_id=1, source_target_pairs={{0,32},{32,64},{64,96},{96,0},{128,160},{160,192},{192,224},{224,1... | collective-permute-start | bytes 1572872 | tf_op jit(solution)/shard_map/ppermute | solution.py:41
  199.1 24.7 %collective-permute-start.6 = (bf16[2,128,1024]{2,1,0:T(8,128)(2,1)S(1)}, bf16[2,128,1024]{2,1,0:T(8,128)(2,1)S(1)}, u32[]{:S(2)}, u32[]{:S(2)}) collective-permute-start(bf16[2,128,1024]{2,1,0:T(8,128)(2,1)S(1)} %get-tuple-element.17), channel_id=1, source_target_pairs={{0,96},{32,0},{64,32},{96,64},{128,224},{160,128},{192,160},{224,1... | collective-permute-start | bytes 1572872 | tf_op jit(solution)/shard_map/ppermute | solution.py:41
  201.4 23.3 %collective-permute-start.5 = (bf16[2,128,1024]{2,1,0:T(8,128)(2,1)S(1)}, bf16[2,128,1024]{2,1,0:T(8,128)(2,1)S(1)}, u32[]{:S(2)}, u32[]{:S(2)}) collective-permute-start(bf16[2,128,1024]{2,1,0:T(8,128)(2,1)S(1)} %get-tuple-element.18), channel_id=1, source_target_pairs={{0,64},{32,96},{64,0},{96,32},{128,192},{160,224},{192,128},{224,1... | collective-permute-start | bytes 1572872 | tf_op jit(solution)/shard_map/ppermute | solution.py:41
  241.7 18.5 %collective-permute-start.7 = (bf16[128,1024]{1,0:T(8,128)(2,1)S(1)}, bf16[128,1024]{1,0:T(8,128)(2,1)S(1)}, u32[]{:S(2)}, u32[]{:S(2)}) collective-permute-start(bf16[128,1024]{1,0:T(8,128)(2,1)S(1)} %fusion.33), channel_id=1, source_target_pairs={{0,128},{32,160},{64,192},{96,224},{128,0},{160,32},{192,64},{224,... | collective-permute-start | bytes 786440 | tf_op jit(solution)/shard_map/ppermute | solution.py:53
  245.0 16.1 %copy-start.1 = (bf16[1,1024,1024]{2,1,0:T(8,128)(2,1)S(1)}, bf16[1,1024,1024]{2,1,0:T(8,128)(2,1)}, u32[]{:S(2)}) copy-start(bf16[1,1024,1024]{2,1,0:T(8,128)(2,1)} %param.7) | copy-start | bytes 6291460
